TPU v7x, 512 devices: a whole 4x4x16 slice. The times are simulated.
512 devices in a mesh: seq: 128 (over x, z, core), head: 4 (over y).
Axes of the slice: x: 4, y: 4, z: 16, core: 2. Of those that a mesh axis runs over, the one named last changes fastest.
Arguments:
- hidden: bfloat16 [32768, 2560], P(('seq', 'head')), may hold values from -6 to 6
- w_values: bfloat16 [2560, 2560], P('seq', 'head'), may hold values from -0.125 to 0.125
- w_gates: bfloat16 [2560, 2560], P('seq', 'head'), may hold values from -0.125 to 0.125
- w_steps: bfloat16 [2560, 40], P('seq', 'head'), may hold values from -0.0625 to 0.0625
- w_states: bfloat16 [2560, 256], P('seq'), may hold values from -0.125 to 0.125
- conv_weight: float32 [4, 2816], replicated, may hold values from -3 to 3
- conv_bias: float32 [2816], replicated, may hold values from -3 to 3
- step_bias: float32 [40], P('head'), may hold values from -1 to 0.5
- decay_rate: float32 [40], P('head'), may hold values from 0 to 1, as said below
- skip_gain: float32 [40], P('head'), may hold values from 1 to 8
- norm_gain: float32 [2560], replicated, may hold values from 0.5 to 1.5
- lengths: int32 [64], replicated, may hold values from 256 to 768, as said below
Outputs:
- gated_out: bfloat16 [32768, 2560], P(('seq', 'head'))
- final_states: float32 [128, 40, 64, 128], P('seq', 'head')
Inputs may be any that keep to these rules, and one draw needn't show every extreme that they name: Prompts are packed in order, each holding 256 to 768 tokens; the lengths sum to 32768. `decay_rate`: positive rates.
All inputs are finite; a program needn't handle non-finite values.
Results may differ from a plain program's by a relative error of at most 0.01.
Values may be sent and summed in bfloat16 or wider, within the bound.
No kernel may reach another device: no remote copies, remote signals or barrier semaphores. Data moves between devices by JAX's collectives and lax.ppermute only.
A program may use at most 128 MiB of HBM per device.

v0:
```python
import jax
import jax.numpy as jnp
from jax import lax
from jax.sharding import PartitionSpec as P

STRETCH = 256


epsilon = 1e-05


def from_behind(block, axis, distance):
    devices = range(lax.axis_size(axis))
    route = [(i - distance, i) for i in devices if i - distance in devices]
    return lax.ppermute(block, axis, route)


def prefix(value, axis, join, neutral):
    place = lax.axis_index(axis)
    gathered = jax.tree.map(
        lambda a, kind: lax.all_gather(a.astype(kind), axis), value, (jnp.bfloat16, jnp.bfloat16)
    )
    state = jax.tree.map(lambda a, e: jnp.zeros_like(a) + jnp.asarray(e, a.dtype), value, neutral)

    def one(turn, state):
        return join(
            state,
            jax.tree.map(
                lambda a, own: lax.dynamic_index_in_dim(a, turn, 0, False).astype(own.dtype),
                gathered,
                value,
            ),
        )

    return lax.fori_loop(0, place, one, state)


def segments_at(positions, prompt_ends):
    counted = jnp.sum((prompt_ends[None, :] <= positions[:, None]).astype(jnp.int32), axis=1)
    return jnp.where(positions < 0, -1, counted)


def on_device(
    hidden,
    w_values,
    w_gates,
    w_steps,
    w_states,
    conv_weight,
    conv_bias,
    step_bias,
    decay_rate,
    skip_gain,
    norm_gain,
    lengths,
):
    groups = lax.axis_size("head")
    group_index = lax.axis_index("head")
    block_index = lax.axis_index("seq")
    local_width = w_values.shape[1]
    inner_width = local_width * groups
    local_heads = decay_rate.shape[0]
    head_width = local_width // local_heads
    state_width = w_states.shape[1] // 2
    conv_taps = conv_weight.shape[0]
    prompt_ends = jnp.cumsum(lengths)
    block_hidden = lax.all_gather(hidden, "head", axis=0, tiled=True)
    block_rows = block_hidden.shape[0]
    sub_rows = block_rows // groups

    def contract(piece):
        return jnp.dot(block_hidden, piece, preferred_element_type=jnp.float32)

    pieces = (
        lax.all_gather(w_values, "seq", axis=0, tiled=True),
        lax.all_gather(w_states, "seq", axis=0, tiled=True),
        lax.all_gather(w_steps, "seq", axis=0, tiled=True),
        lax.all_gather(w_gates, "seq", axis=0, tiled=True),
    )
    values_sum, states_sum, steps_sum, gates_sum = tuple((contract(piece) for piece in pieces))
    pre_rows = jnp.concatenate(
        [values_sum.astype(jnp.bfloat16), states_sum.astype(jnp.bfloat16)], axis=1
    )
    local_taps = jnp.concatenate(
        [
            lax.dynamic_slice_in_dim(conv_weight, group_index * local_width, local_width, 1),
            conv_weight[:, inner_width:],
        ],
        axis=1,
    )
    local_bias = jnp.concatenate(
        [
            lax.dynamic_slice_in_dim(conv_bias, group_index * local_width, local_width, 0),
            conv_bias[inner_width:],
        ],
        axis=0,
    )
    block_start = block_index * block_rows
    rim_rows = pre_rows[block_rows - (conv_taps - 1) :]
    prior_rim = from_behind(rim_rows, "seq", 1)
    extended = jnp.concatenate([prior_rim, pre_rows], axis=0)
    ext_positions = (
        block_start - (conv_taps - 1) + jnp.arange(block_rows + conv_taps - 1, dtype=jnp.int32)
    )
    ext_ids = segments_at(ext_positions, prompt_ends)
    own_ids = ext_ids[conv_taps - 1 :]
    filtered = jnp.zeros(pre_rows.shape, jnp.float32) + local_bias[None, :]
    for offset in range(conv_taps):
        matches = (ext_ids[offset : offset + block_rows] == own_ids).astype(jnp.float32)
        filtered = (
            filtered
            + local_taps[offset][None, :]
            * extended[offset : offset + block_rows].astype(jnp.float32)
            * matches[:, None]
        )
    conv_out = jax.nn.silu(filtered).astype(jnp.bfloat16)
    head_values = conv_out[:, :local_width]
    both_states = conv_out[:, local_width:]
    stretch_rows = STRETCH
    stretches = block_rows // stretch_rows
    positions = block_start + jnp.arange(block_rows, dtype=jnp.int32)
    segment_ids = segments_at(positions, prompt_ends)
    next_ids = segments_at(positions + 1, prompt_ends)
    before_ids = segments_at(positions - 1, prompt_ends)
    stretch_ids = segment_ids.reshape(stretches, stretch_rows)
    prior_ids = before_ids.reshape(stretches, stretch_rows)[:, 0]
    ends_mask = (segment_ids != next_ids).reshape(stretches, stretch_rows)
    step_sizes = jax.nn.softplus(steps_sum + step_bias[None, :])
    decay_steps = step_sizes * decay_rate[None, :]
    log_decay = -jnp.cumsum(decay_steps.reshape(stretches, stretch_rows, local_heads), axis=1)
    decay_heads = jnp.swapaxes(log_decay, 1, 2)
    step_heads = jnp.swapaxes(step_sizes.reshape(stretches, stretch_rows, local_heads), 1, 2)
    values = head_values.reshape(stretches, stretch_rows, local_heads, head_width)
    write_state = both_states[:, :state_width].reshape(stretches, stretch_rows, state_width)
    read_state = both_states[:, state_width:].reshape(stretches, stretch_rows, state_width)
    intersection = jnp.einsum(
        "ctn,csn->cts", read_state, write_state, preferred_element_type=jnp.float32
    )
    token_order = jnp.arange(stretch_rows, dtype=jnp.int32)
    causal = token_order[:, None] >= token_order[None, :]
    allowed = causal[None] & (stretch_ids[:, :, None] == stretch_ids[:, None, :])
    spread = decay_heads[:, :, :, None] - decay_heads[:, :, None, :]
    weights = (
        jnp.where(allowed[:, None], jnp.exp(jnp.minimum(spread, 0.0)), 0.0)
        * step_heads[:, :, None, :]
    )
    scores = (intersection[:, None] * weights).astype(jnp.bfloat16)
    within_stretch = jnp.einsum(
        "chts,cshp->cthp", scores, values, preferred_element_type=jnp.float32
    )
    last_ids = stretch_ids[:, -1]
    tail_decay = decay_heads[:, :, -1:]
    keep_tail = (stretch_ids == last_ids[:, None])[:, None, :]
    tail_coef = (
        jnp.where(keep_tail, jnp.exp(jnp.minimum(tail_decay - decay_heads, 0.0)), 0.0) * step_heads
    )
    tail_rows = (values.astype(jnp.float32) * jnp.swapaxes(tail_coef, 1, 2)[:, :, :, None]).astype(
        jnp.bfloat16
    )
    stretch_states = jnp.einsum(
        "clhp,cln->chpn", tail_rows, write_state, preferred_element_type=jnp.float32
    )
    stretch_gates = (
        jnp.exp(decay_heads[:, :, -1]) * (last_ids == prior_ids).astype(jnp.float32)[:, None]
    )
    block_gate = jnp.ones((local_heads,), jnp.float32)
    block_state = jnp.zeros((local_heads, head_width, state_width), jnp.float32)
    block_state = stretch_gates[0][:, None, None] * block_state + stretch_states[0]
    block_gate = block_gate * stretch_gates[0]

    def compose(earlier, later):
        return (earlier[0] * later[0], later[0][:, None, None] * earlier[1] + later[1])

    identity_pair = (jnp.ones_like(block_gate), jnp.zeros_like(block_state))
    carried = prefix((block_gate, block_state), "seq", compose, identity_pair)
    incoming = carried[1]
    arriving = []
    arriving.append(incoming)
    arriving = jnp.stack(arriving)
    carry_mask = (stretch_ids == prior_ids[:, None]).astype(jnp.float32)
    carry_decay = jnp.exp(log_decay) * carry_mask[:, :, None]
    from_before = (
        jnp.einsum(
            "cln,chpn->clhp",
            read_state,
            arriving.astype(jnp.bfloat16),
            preferred_element_type=jnp.float32,
        )
        * carry_decay[:, :, :, None]
    )
    result = (
        within_stretch + from_before + skip_gain[None, None, :, None] * values.astype(jnp.float32)
    )
    ssm_rows = result.reshape(block_rows, local_width).astype(jnp.bfloat16)
    end_weight = ends_mask.astype(jnp.float32)
    has_end = jnp.sum(end_weight, axis=1)
    end_decay = jnp.sum(decay_heads * end_weight[:, None, :], axis=2)
    end_ids = jnp.sum(jnp.where(ends_mask, stretch_ids, 0), axis=1)
    keep_end = ((stretch_ids == end_ids[:, None]) & (has_end[:, None] > 0))[:, None, :]
    end_coef = (
        jnp.where(keep_end, jnp.exp(jnp.minimum(end_decay[:, :, None] - decay_heads, 0.0)), 0.0)
        * step_heads
    )
    end_rows = (values.astype(jnp.float32) * jnp.swapaxes(end_coef, 1, 2)[:, :, :, None]).astype(
        jnp.bfloat16
    )
    end_states = jnp.einsum(
        "clhp,cln->chpn", end_rows, write_state, preferred_element_type=jnp.float32
    )
    end_carry = (
        jnp.exp(end_decay) * ((end_ids == prior_ids) & (has_end > 0)).astype(jnp.float32)[:, None]
    )
    end_states = end_states + end_carry[:, :, None, None] * arriving
    final_block = jnp.sum(end_states, axis=0)[None]
    head_gates = gates_sum.astype(jnp.bfloat16)
    norm_slice = lax.dynamic_slice_in_dim(norm_gain, group_index * local_width, local_width)
    gated = ssm_rows.astype(jnp.float32) * jax.nn.silu(head_gates.astype(jnp.float32))
    squares = lax.psum(jnp.sum(gated * gated, axis=1), "head")
    scaled = gated * lax.rsqrt(squares / inner_width + epsilon)[:, None] * norm_slice[None, :]
    outgoing = scaled.astype(jnp.bfloat16)
    returned = lax.all_to_all(
        outgoing.reshape(groups, sub_rows, local_width),
        "head",
        split_axis=0,
        concat_axis=2,
        tiled=True,
    )
    gated_out = returned.reshape(sub_rows, inner_width)
    return (gated_out, final_block)


def solution(mesh):
    in_specs = (
        P(("seq", "head"), None),
        P("seq", "head"),
        P("seq", "head"),
        P("seq", "head"),
        P("seq", None),
        P(),
        P(),
        P("head"),
        P("head"),
        P("head"),
        P(),
        P(),
    )
    out_specs = (P(("seq", "head"), None), P("seq", "head", None, None))
    return jax.shard_map(
        on_device, mesh=mesh, in_specs=in_specs, out_specs=out_specs, check_vma=False
    )
```

profile of v0, /device:TPU:486, one launch (start us, length us, event | category | flops | bytes accessed | tf_op | source)
XLA Modules:
  0.0 797.8 jit_solution(4028374135680535163)
XLA Ops:
  10.0 80.7 %all-gather.4 = bf16[128,20,10]{1,2,0:T(8,128)(2,1)S(1)} all-gather(bf16[1,20,10]{1,2,0:T(8,128)(2,1)} %bitcast.160), channel_id=1, replica_groups=mesh['seq'=128,'head'=4] {'seq'}, dimensions={0}, use_global_device_ids=true | all-gather | bytes 51600 | tf_op jit(solution)/shard_map/all_gather | solution.py:77
  102.6 1.2 broadcast_compare_fusion
  104.5 1.9 broadcast_multiply_fusion
  109.7 72.2 %all-gather.18.cloned.1.call-done = bf16[128,20,256]{2,1,0:T(8,128)(2,1)} async-done(((bf16[1,20,256]{2,1,0:T(8,128)(2,1)}), bf16[128,20,256]{2,1,0:T(8,128)(2,1)}) %all-gather.18.cloned.1.call-update) | async-done | bytes 1310736 | tf_op jit(solution)/shard_map/all_gather | solution.py:76
  181.9 2.3 reshape.524
  184.7 138.0 %all-gather.16.cloned.1.call-done = bf16[128,20,640]{2,1,0:T(8,128)(2,1)} async-done(((bf16[1,20,640]{2,1,0:T(8,128)(2,1)}), bf16[128,20,640]{2,1,0:T(8,128)(2,1)}) %all-gather.16.cloned.1.call-update) | async-done | bytes 3276816 | tf_op jit(solution)/shard_map/all_gather | solution.py:75
  322.7 4.6 reshape.522
  327.3 2.5 convolution_convert_fusion.1
  330.7 2.3 collective-permute-start
  334.7 1.1 collective-permute-done
  339.8 72.9 %all-gather = bf16[128,10,1]{1,2,0:T(2,128)(2,1)S(1)} all-gather(bf16[1,10,1]{1,2,0:T(2,128)(2,1)S(1)} %copy-done.18), channel_id=2, replica_groups=mesh['seq'=128,'head'=4] {'seq'}, dimensions={0}, use_global_device_ids=true | all-gather | bytes 2580 | tf_op jit(solution)/shard_map/all_gather | solution.py:21
  413.0 50.4 %all-gather.20.cloned.1.call-done = bf16[128,20,640]{2,1,0:T(8,128)(2,1)} async-done(((bf16[1,20,640]{2,1,0:T(8,128)(2,1)}), bf16[128,20,640]{2,1,0:T(8,128)(2,1)}) %all-gather.20.cloned.1.call-update) | async-done | bytes 3276816 | tf_op jit(solution)/shard_map/all_gather | solution.py:78
  463.4 6.1 reshape.528
  470.2 156.1 %all-gather.14.cloned.1.call-done = bf16[1280,64,128]{2,1,0:T(8,128)(2,1)} async-done(((bf16[10,64,128]{2,1,0:T(8,128)(2,1)}), bf16[1280,64,128]{2,1,0:T(8,128)(2,1)}) %all-gather.14.cloned.1.call-update) | async-done | bytes 20971536 | tf_op jit(solution)/shard_map/all_gather | solution.py:21
  626.3 136.8 %while.12 = (s32[]{:T(128)}, f32[10,64,128]{2,1,0:T(8,128)S(1)}, s32[]{:T(128)}, bf16[128,10]{1,0:T(8,128)(2,1)S(1)}, bf16[128,10,64,128]{3,2,1,0:T(8,128)(2,1)}, /*index=5*/s32[]{:T(128)}, s32[]{:T(128)}, s32[]{:T(128)}) while((s32[]{:T(128)}, f32[10,64,128]{2,1,0:T(8,128)S(1)}, s32[]{:T(128)}, bf16[128,10]{1,0:T(8,128)(2,1)S(1)}, ...), condition=%wide.region_7.8_spmd, body=%wide.region_6.7_spmd.sunk | while | flops 245775 | bytes 819435 | solution.py:35
  626.3 1.0 convert_add_fusion.2
  628.5 1.0 convert_add_fusion.2
  630.6 1.0 convert_add_fusion.2
  631.7 1.0 convert_add_fusion.2
  632.8 1.0 convert_add_fusion.2
  633.9 1.0 convert_add_fusion.2
  636.1 1.0 convert_add_fusion.2
  638.2 1.0 convert_add_fusion.2
  640.4 1.0 convert_add_fusion.2
  642.6 1.0 convert_add_fusion.2
  644.7 1.0 convert_add_fusion.2
  646.9 1.0 convert_add_fusion.2
  649.1 1.0 convert_add_fusion.2
  651.2 1.0 convert_add_fusion.2
  652.3 1.0 convert_add_fusion.2
  653.4 1.0 convert_add_fusion.2
  654.5 1.0 convert_add_fusion.2
  656.7 1.0 convert_add_fusion.2
  658.8 1.0 convert_add_fusion.2
  661.0 1.0 convert_add_fusion.2
  663.2 1.0 convert_add_fusion.2
  665.3 1.0 convert_add_fusion.2
  667.5 1.0 convert_add_fusion.2
  669.7 1.0 convert_add_fusion.2
  671.8 1.0 convert_add_fusion.2
  672.9 1.0 convert_add_fusion.2
  674.0 1.0 convert_add_fusion.2
  675.1 1.0 convert_add_fusion.2
  677.3 1.0 convert_add_fusion.2
  764.6 3.6 multiply_reduce_fusion
  768.3 10.5 %psum.7 = f32[256]{0:T(256)S(1)} all-reduce(f32[256]{0:T(256)S(1)} %get-tuple-element.105), channel_id=1, replica_groups=mesh['seq'=128,'head'=4] {'head'}, use_global_device_ids=true, to_apply=%region_9.10 | all-reduce | flops 256 | bytes 2048 | tf_op jit(solution)/shard_map/psum | solution.py:218
  779.6 3.5 all-to-all-start
  784.3 5.9 all-to-all-done
  (360 shorter events, 129.6 us)
Async XLA Ops:
  7.2 97.3 %all-gather.12.cloned.1.call-start = ((), (), s32[]{:S(2)}) async-start(), calls=%async_computation.1 | async-start | bytes 1638400 | tf_op jit(solution)/shard_map/all_gather | solution.py:67
  7.9 174.0 %all-gather.18.cloned.1.call-start = ((), (), s32[]{:S(2)}) async-start(), calls=%async_computation.4 | async-start | bytes 1585152 | tf_op jit(solution)/shard_map/all_gather | solution.py:76
  8.6 314.0 %all-gather.16.cloned.1.call-start = ((), (), s32[]{:S(2)}) async-start(), calls=%async_computation.3 | async-start | bytes 3962880 | tf_op jit(solution)/shard_map/all_gather | solution.py:75
  9.4 454.0 %all-gather.20.cloned.1.call-start = ((), (), s32[]{:S(2)}) async-start(), calls=%async_computation.5 | async-start | bytes 3962880 | tf_op jit(solution)/shard_map/all_gather | solution.py:78
  10.0 616.3 %all-gather.14.cloned.1.call-start = ((), (), s32[]{:S(2)}) async-start(), calls=%async_computation.2 | async-start | bytes 21135360 | tf_op jit(solution)/shard_map/all_gather | solution.py:21
  99.3 5.2 copy-start.12
  104.5 79.7 %copy-start.21 = (bf16[256,2560]{1,0:T(8,128)(2,1)S(1)}, bf16[256,2560]{1,0:T(8,128)(2,1)}, u32[]{:S(2)}) copy-start(bf16[256,2560]{1,0:T(8,128)(2,1)} %all-gather.12.cloned.1.call-done) | copy-start | bytes 3932164
  106.4 3.2 copy-start.2
  107.4 74.5 %copy-start.10 = (f32[10,2]{0,1:T(2,128)}, f32[10,2]{0,1:T(2,128)S(1)}, u32[]{:S(2)}) copy-start(f32[10,2]{0,1:T(2,128)S(1)} %slice_bitcast_fusion) | copy-start | bytes 244
  107.6 2.1 copy-start.19
  329.8 0.7 copy-start
  330.6 3.7 copy-start.4
  330.6 5.2 copy-start.1
  330.6 5.3 copy-start.5
  330.6 5.3 copy-start.6
  330.6 5.3 copy-start.7
  330.6 5.3 copy-start.8
  330.6 5.3 copy-start.9
  330.6 5.3 copy-start.14
  330.7 5.3 copy-start.15
  330.7 5.3 copy-start.16
  330.7 5.1 collective-permute-start
  336.0 3.4 copy-start.13
  336.0 3.6 copy-start.11
  336.0 3.7 copy-start.17
  336.8 3.0 copy-start.18
  336.8 76.0 %copy-start.3 = (f32[256,10]{1,0:T(8,128)S(1)}, f32[256,10]{1,0:T(8,128)}, u32[]{:S(2)}) copy-start(f32[256,10]{1,0:T(8,128)} %copy-done.2) | copy-start | bytes 30724
  626.3 137.1 %copy-start.22 = (f32[10]{0:T(128)S(1)}, f32[10]{0:T(128)}, u32[]{:S(2)}) copy-start(f32[10]{0:T(128)} %param.23) | copy-start | bytes 124
  764.6 18.5 %copy-start.20 = (f32[10]{0:T(128)S(1)}, f32[10]{0:T(128)}, u32[]{:S(2)}) copy-start(f32[10]{0:T(128)} %copy-done.19) | copy-start | bytes 124
  779.6 10.6 %all-to-all-start = ((bf16[4,64,640]{2,1,0:T(8,128)(2,1)}), bf16[4,64,640]{2,1,0:T(8,128)(2,1)S(1)}, u32[]{:S(2)}, u32[]{:S(2)}) async-start(bf16[4,64,640]{2,1,0:T(8,128)(2,1)} %bitcast.41), calls=%async_computation | async-start | bytes 655360 | tf_op jit(solution)/shard_map/all_to_all | solution.py:221
Sparse Core Ops, SparseCore 0:
  10.1 31.5 all-gather.11
  44.7 137.1 all-gather.17
  185.0 137.6 all-gather.15
  325.6 137.7 all-gather.19
  466.9 159.2 all-gather.13
where the time goes:
time: 801 us; the launch traced here: 798 us
  waiting for transfers between devices  426 us (53%)
  blocking collectives  164 us (20%)
  other arithmetic  143 us (18%)
  local copies, waits for them, and re-layouts  24.9 us (3%)
  between operations  18.1 us (2%)
  matrix products  11.9 us (1%)
    all_gather x1, waiting for transfers between devices, prefix(): lax.all_gather(a.astype(kind), axis)  156 us
    all_gather x1, waiting for transfers between devices, on_device(): lax.all_gather(w_values, 'seq', axis=0, tiled=True)  138 us
    add x126, other arithmetic, compose(): later[0][:, None, None] * earlier[1] + later[1]  131 us
    all_gather x1, blocking collectives, on_device(): lax.all_gather(w_steps, 'seq', axis=0, tiled=True)  80.7 us
    all_gather x1, blocking collectives, prefix(): lax.all_gather(a.astype(kind), axis)  72.9 us
    all_gather x1, waiting for transfers between devices, on_device(): lax.all_gather(w_states, 'seq', axis=0, tiled=True)  72.2 us
    all_gather x1, waiting for transfers between devices, on_device(): lax.all_gather(w_gates, 'seq', axis=0, tiled=True)  50.4 us
  transfers between devices with their start and end apart: 7, of which 6 were waited for; matrix products, arithmetic and copies ran while one was open for 5% of the time, Pallas kernels for 0%

commit v1 on v0

--- a/solution.py
+++ b/solution.py
@@ -13,26 +13,6 @@
     devices = range(lax.axis_size(axis))
     route = [(i - distance, i) for i in devices if i - distance in devices]
     return lax.ppermute(block, axis, route)
-
-
-def prefix(value, axis, join, neutral):
-    place = lax.axis_index(axis)
-    gathered = jax.tree.map(
-        lambda a, kind: lax.all_gather(a.astype(kind), axis), value, (jnp.bfloat16, jnp.bfloat16)
-    )
-    state = jax.tree.map(lambda a, e: jnp.zeros_like(a) + jnp.asarray(e, a.dtype), value, neutral)
-
-    def one(turn, state):
-        return join(
-            state,
-            jax.tree.map(
-                lambda a, own: lax.dynamic_index_in_dim(a, turn, 0, False).astype(own.dtype),
-                gathered,
-                value,
-            ),
-        )
-
-    return lax.fori_loop(0, place, one, state)
 
 
 def segments_at(positions, prompt_ends):
@@ -64,23 +44,19 @@
     state_width = w_states.shape[1] // 2
     conv_taps = conv_weight.shape[0]
     prompt_ends = jnp.cumsum(lengths)
-    block_hidden = lax.all_gather(hidden, "head", axis=0, tiled=True)
+    block_hidden = lax.all_to_all(
+        jnp.broadcast_to(hidden[None], (groups,) + hidden.shape), "head", 0, 0, tiled=True
+    ).reshape(groups * hidden.shape[0], hidden.shape[1])
     block_rows = block_hidden.shape[0]
     sub_rows = block_rows // groups
-
-    def contract(piece):
-        return jnp.dot(block_hidden, piece, preferred_element_type=jnp.float32)
-
-    pieces = (
-        lax.all_gather(w_values, "seq", axis=0, tiled=True),
-        lax.all_gather(w_states, "seq", axis=0, tiled=True),
-        lax.all_gather(w_steps, "seq", axis=0, tiled=True),
-        lax.all_gather(w_gates, "seq", axis=0, tiled=True),
-    )
-    values_sum, states_sum, steps_sum, gates_sum = tuple((contract(piece) for piece in pieces))
-    pre_rows = jnp.concatenate(
-        [values_sum.astype(jnp.bfloat16), states_sum.astype(jnp.bfloat16)], axis=1
-    )
+    step_width = w_steps.shape[1]
+    merged = jnp.concatenate([w_values, w_states, w_gates, w_steps], axis=1)
+    full = lax.all_gather(merged, "seq", axis=0, tiled=True)
+    projected = jnp.dot(block_hidden, full, preferred_element_type=jnp.float32)
+    conv_end = local_width + 2 * state_width
+    pre_rows = projected[:, :conv_end].astype(jnp.bfloat16)
+    gates_sum = projected[:, conv_end : conv_end + local_width]
+    steps_sum = projected[:, conv_end + local_width : conv_end + local_width + step_width]
     local_taps = jnp.concatenate(
         [
             lax.dynamic_slice_in_dim(conv_weight, group_index * local_width, local_width, 1),
@@ -163,20 +139,12 @@
     stretch_gates = (
         jnp.exp(decay_heads[:, :, -1]) * (last_ids == prior_ids).astype(jnp.float32)[:, None]
     )
-    block_gate = jnp.ones((local_heads,), jnp.float32)
-    block_state = jnp.zeros((local_heads, head_width, state_width), jnp.float32)
-    block_state = stretch_gates[0][:, None, None] * block_state + stretch_states[0]
-    block_gate = block_gate * stretch_gates[0]
-
-    def compose(earlier, later):
-        return (earlier[0] * later[0], later[0][:, None, None] * earlier[1] + later[1])
-
-    identity_pair = (jnp.ones_like(block_gate), jnp.zeros_like(block_state))
-    carried = prefix((block_gate, block_state), "seq", compose, identity_pair)
-    incoming = carried[1]
-    arriving = []
-    arriving.append(incoming)
-    arriving = jnp.stack(arriving)
+    own_pair = (stretch_gates[0], stretch_states[0])
+    g1, s1 = from_behind(own_pair, "seq", 1)
+    g2, s2 = from_behind(own_pair, "seq", 2)
+    g3, s3 = from_behind(own_pair, "seq", 3)
+    incoming = s1 + g1[:, None, None] * (s2 + g2[:, None, None] * s3)
+    arriving = incoming[None]
     carry_mask = (stretch_ids == prior_ids[:, None]).astype(jnp.float32)
     carry_decay = jnp.exp(log_decay) * carry_mask[:, :, None]
     from_before = (
@@ -213,19 +181,13 @@
     end_states = end_states + end_carry[:, :, None, None] * arriving
     final_block = jnp.sum(end_states, axis=0)[None]
     head_gates = gates_sum.astype(jnp.bfloat16)
-    norm_slice = lax.dynamic_slice_in_dim(norm_gain, group_index * local_width, local_width)
-    gated = ssm_rows.astype(jnp.float32) * jax.nn.silu(head_gates.astype(jnp.float32))
-    squares = lax.psum(jnp.sum(gated * gated, axis=1), "head")
-    scaled = gated * lax.rsqrt(squares / inner_width + epsilon)[:, None] * norm_slice[None, :]
-    outgoing = scaled.astype(jnp.bfloat16)
-    returned = lax.all_to_all(
-        outgoing.reshape(groups, sub_rows, local_width),
-        "head",
-        split_axis=0,
-        concat_axis=2,
-        tiled=True,
-    )
-    gated_out = returned.reshape(sub_rows, inner_width)
+    both = jnp.stack([ssm_rows, head_gates]).reshape(2, groups, sub_rows, local_width)
+    returned = lax.all_to_all(both, "head", split_axis=1, concat_axis=3, tiled=True)
+    token_rows = returned.reshape(2, sub_rows, inner_width).astype(jnp.float32)
+    gated = token_rows[0] * jax.nn.silu(token_rows[1])
+    mean_square = jnp.mean(gated * gated, axis=1)
+    scaled = gated * lax.rsqrt(mean_square + epsilon)[:, None] * norm_gain[None, :]
+    gated_out = scaled.astype(jnp.bfloat16)
     return (gated_out, final_block)
 
 

time: 801 us -> 261 us (0.33)
  the two profiles are of different devices: /device:TPU:486 before, /device:TPU:6 now
where the time goes in v1:
time: 261 us; the launch traced here: 258 us
  waiting for transfers between devices  170 us (65%)
  local copies, waits for them, and re-layouts  26.9 us (10%)
  starting transfers between devices  23.2 us (9%)
  between operations  18.4 us (7%)
  other arithmetic  11.4 us (4%)
  matrix products  8.43 us (3%)
    all_gather x1, waiting for transfers between devices, on_device(): full = lax.all_gather(merged, 'seq', axis=0, tiled=True)  138 us
    ppermute x6, waiting for transfers between devices, from_behind(): return lax.ppermute(block, axis, route)  21.9 us
    unnamed x24, local copies, waits for them, and re-layouts  16 us
    ppermute x6, starting transfers between devices, from_behind(): return lax.ppermute(block, axis, route)  14.3 us
    all_to_all x1, waiting for transfers between devices, on_device(): lax.all_to_all(both, 'head', split_axis=1, concat_axis=3, tiled=True)  9.34 us
    dot_general x1, matrix products, on_device(): projected = jnp.dot(block_hidden, full, preferred_element_type=jnp.float32)  5.85 us
  transfers between devices with their start and end apart: 9, of which 6 were waited for; matrix products, arithmetic and copies ran while one was open for 11% of the time, Pallas kernels for 0%

profile of v1, /device:TPU:6, one launch (start us, length us, event | category | flops | bytes accessed | tf_op | source)
XLA Modules:
  0.0 257.9 jit_solution(16076834221550302030)
XLA Ops:
  7.2 0.8 copy.65
  8.0 1.4 maximum_bitcast_fusion
  9.5 2.1 broadcast_in_dim.39
  11.6 4.6 %all-to-all-start = ((bf16[4,64,2560]{2,1,0:T(8,128)(2,1)}), bf16[4,64,2560]{2,1,0:T(8,128)(2,1)S(1)}, u32[]{:S(2)}, u32[]{:S(2)}) async-start(bf16[4,64,2560]{2,1,0:T(8,128)(2,1)} %broadcast_in_dim.39), calls=%async_computation | async-start | bytes 2621440 | tf_op jit(solution)/shard_map/all_to_all | solution.py:47
  16.5 0.7 slice.91
  17.2 0.8 dynamic_slice.6
  18.1 0.7 slice.136
  18.8 0.6 fusion.49
  20.6 0.5 slice.139
  22.4 0.6 convert_reduce_fusion.4
  23.8 0.6 select_reduce_fusion
  24.6 0.7 broadcast_compare_fusion
  25.4 138.3 %all-gather.3.cloned.1.call-done = bf16[128,20,1546]{2,1,0:T(8,128)(2,1)} async-done(((bf16[1,20,1546]{2,1,0:T(8,128)(2,1)}), bf16[128,20,1546]{2,1,0:T(8,128)(2,1)}) %all-gather.3.cloned.1.call-update) | async-done | bytes 7915536 | tf_op jit(solution)/shard_map/all_gather | solution.py:54
  163.7 13.7 %reshape.504 = bf16[2560,1546]{1,0:T(8,128)(2,1)} reshape(bf16[128,20,1546]{2,1,0:T(8,128)(2,1)} %all-gather.3.cloned.1.call-done) | data formatting | bytes 15831040
  177.5 5.8 %fusion.50 = (bf16[256,1546]{0,1:T(8,128)(2,1)S(1)}, f32[256,1546]{0,1:T(8,128)S(1)}) fusion(bf16[2560,1546]{1,0:T(8,128)(2,1)} %reshape.504, bf16[256,2560]{1,0:T(8,128)(2,1)S(1)} %bitcast.126), kind=kOutput, calls=%fused_computation.113 | convolution fusion | flops 2026768896 | bytes 11600896 | tf_op jit(solution)/shard_map/dot_general | solution.py:55
  183.4 1.0 copy-done.4
  184.5 0.6 reduce-window.19
  185.7 0.8 fusion.31
  186.7 3.6 %collective-permute-start.4 = (f32[10]{0:T(128)S(1)}, f32[10]{0:T(128)S(1)}, u32[]{:S(2)}, u32[]{:S(2)}) collective-permute-start(f32[10]{0:T(128)S(1)} %exponential_multiply_fusion.1), channel_id=1, source_target_pairs={{0,8},{4,12},{8,16},{12,20},{16,24},{20,28},{24,32},{28,36},{32,40... | collective-permute-start | bytes 128 | tf_op jit(solution)/shard_map/ppermute | solution.py:15
  190.3 1.9 collective-permute-start.2
  192.4 2.8 %collective-permute-start = (bf16[3,896]{0,1:T(8,128)(2,1)S(1)}, bf16[3,896]{0,1:T(8,128)(2,1)S(1)}, u32[]{:S(2)}, u32[]{:S(2)}) collective-permute-start(bf16[3,896]{0,1:T(8,128)(2,1)S(1)} %slice.120), channel_id=1, source_target_pairs={{0,4},{4,8},{8,12},{12,16},{16,20},{20,24},{24,28},{28,32},{32,36}... | collective-permute-start | bytes 16136 | tf_op jit(solution)/shard_map/ppermute | solution.py:15
  195.2 0.8 fusion.32
  196.1 0.2 copy.74
  196.3 0.8 copy.75
  197.2 4.7 %collective-permute-done = bf16[3,896]{0,1:T(8,128)(2,1)S(1)} collective-permute-done((bf16[3,896]{0,1:T(8,128)(2,1)S(1)}, bf16[3,896]{0,1:T(8,128)(2,1)S(1)}, u32[]{:S(2)}, u32[]{:S(2)}) %collective-permute-start) | collective-permute-done | bytes 5408 | tf_op jit(solution)/shard_map/ppermute | solution.py:15
  201.8 1.5 multiply_convert_fusion.4
  203.4 0.8 fusion.12
  204.3 0.2 fusion.20
  204.5 1.9 collective-permute-start.1
  206.4 1.9 collective-permute-start.3
  208.3 2.2 collective-permute-start.5
  210.5 0.2 fusion.26
  210.8 0.9 fusion.7
  211.7 4.2 %collective-permute-done.1 = f32[10,64,128]{2,1,0:T(8,128)S(1)} collective-permute-done((f32[10,64,128]{2,1,0:T(8,128)S(1)}, f32[10,64,128]{2,1,0:T(8,128)S(1)}, u32[]{:S(2)}, u32[]{:S(2)}) %collective-permute-start.1) | collective-permute-done | bytes 327712 | tf_op jit(solution)/shard_map/ppermute | solution.py:15
  215.9 5.1 %collective-permute-done.3 = f32[10,64,128]{2,1,0:T(8,128)S(1)} collective-permute-done((f32[10,64,128]{2,1,0:T(8,128)S(1)}, f32[10,64,128]{2,1,0:T(8,128)S(1)}, u32[]{:S(2)}, u32[]{:S(2)}) %collective-permute-start.3) | collective-permute-done | bytes 327712 | tf_op jit(solution)/shard_map/ppermute | solution.py:15
  221.1 7.8 %collective-permute-done.5 = f32[10,64,128]{2,1,0:T(8,128)S(1)} collective-permute-done((f32[10,64,128]{2,1,0:T(8,128)S(1)}, f32[10,64,128]{2,1,0:T(8,128)S(1)}, u32[]{:S(2)}, u32[]{:S(2)}) %collective-permute-start.5) | collective-permute-done | bytes 327712 | tf_op jit(solution)/shard_map/ppermute | solution.py:15
  229.0 0.2 fusion.11
  229.3 0.3 convert_element_type.165
  229.6 1.1 pad_maximum_fusion
  230.7 2.4 copy.76
  233.1 4.3 %all-to-all-start.1 = ((bf16[2,4,64,640]{3,2,0,1:T(8,128)(2,1)}), bf16[2,4,64,640]{3,2,0,1:T(8,128)(2,1)S(1)}, u32[]{:S(2)}, u32[]{:S(2)}) async-start(bf16[2,4,64,640]{3,2,0,1:T(8,128)(2,1)} %copy.76), calls=%async_computation.1 | async-start | bytes 1310720 | tf_op jit(solution)/shard_map/all_to_all | solution.py:185
  238.1 1.0 add_bitcast_fusion
  239.0 9.3 %all-to-all-done.1 = bf16[2,4,64,640]{3,2,0,1:T(8,128)(2,1)S(1)} async-done(((bf16[2,4,64,640]{3,2,0,1:T(8,128)(2,1)}), bf16[2,4,64,640]{3,2,0,1:T(8,128)(2,1)S(1)}, u32[]{:S(2)}, u32[]{:S(2)}) %all-to-all-start.1) | async-done | bytes 655392 | tf_op jit(solution)/shard_map/all_to_all | solution.py:185
  248.6 0.4 copy.77
  249.1 0.4 copy.78
  249.6 0.3 multiply_reduce_fusion
  249.9 0.3 copy-done.2
  250.2 0.8 multiply_convert_fusion.5
  (68 shorter events, 2.5 us)
Async XLA Ops:
  7.2 156.6 %all-gather.3.cloned.1.call-start = ((), (), s32[]{:S(2)}) async-start(), calls=%async_computation.2 | async-start | bytes 10303488 | tf_op jit(solution)/shard_map/all_gather | solution.py:54
  11.6 4.6 %copy-start.5 = (s32[64]{0:T(128)S(1)}, s32[64]{0:T(128)}, u32[]{:S(2)}) copy-start(s32[64]{0:T(128)} %param.23) | copy-start | bytes 772
  11.6 12.1 %copy-start.1 = (f32[4,2816]{1,0:T(4,128)S(1)}, f32[4,2816]{1,0:T(4,128)}, u32[]{:S(2)}) copy-start(f32[4,2816]{1,0:T(4,128)} %param.17) | copy-start | bytes 135172
  11.6 12.1 %slice-start = ((f32[4,2816]{1,0:T(4,128)}), f32[4,256]{1,0:T(4,128)S(1)}, s32[]{:S(2)}) async-start(f32[4,2816]{1,0:T(4,128)} %param.17), calls=%async_computation.3 | async-start | bytes 8192 | tf_op jit(solution)/shard_map/slice | solution.py:63
  11.6 165.8 %all-to-all-start = ((bf16[4,64,2560]{2,1,0:T(8,128)(2,1)}), bf16[4,64,2560]{2,1,0:T(8,128)(2,1)S(1)}, u32[]{:S(2)}, u32[]{:S(2)}) async-start(bf16[4,64,2560]{2,1,0:T(8,128)(2,1)} %broadcast_in_dim.39), calls=%async_computation | async-start | bytes 2621440 | tf_op jit(solution)/shard_map/all_to_all | solution.py:47
  177.5 5.9 %copy-start.3 = (f32[10]{0:T(128)S(1)}, f32[10]{0:T(128)}, u32[]{:S(2)}) copy-start(f32[10]{0:T(128)} %param.19) | copy-start | bytes 124
  177.5 5.9 %copy-start.6 = (f32[10]{0:T(128)S(1)}, f32[10]{0:T(128)}, u32[]{:S(2)}) copy-start(f32[10]{0:T(128)} %param.20) | copy-start | bytes 124
  183.3 1.2 copy-start.4
  186.7 25.0 %collective-permute-start.4 = (f32[10]{0:T(128)S(1)}, f32[10]{0:T(128)S(1)}, u32[]{:S(2)}, u32[]{:S(2)}) collective-permute-start(f32[10]{0:T(128)S(1)} %exponential_multiply_fusion.1), channel_id=1, source_target_pairs={{0,8},{4,12},{8,16},{12,20},{16,24},{20,28},{24,32},{28,36},{32,40... | collective-permute-start | bytes 128 | tf_op jit(solution)/shard_map/ppermute | solution.py:15
  190.3 21.4 %collective-permute-start.2 = (f32[10]{0:T(128)S(1)}, f32[10]{0:T(128)S(1)}, u32[]{:S(2)}, u32[]{:S(2)}) collective-permute-start(f32[10]{0:T(128)S(1)} %exponential_multiply_fusion.1), channel_id=1, source_target_pairs={{0,4},{4,8},{8,12},{12,16},{16,20},{20,24},{24,28},{28,32},{32,36}... | collective-permute-start | bytes 128 | tf_op jit(solution)/shard_map/ppermute | solution.py:15
  192.4 9.4 %collective-permute-start = (bf16[3,896]{0,1:T(8,128)(2,1)S(1)}, bf16[3,896]{0,1:T(8,128)(2,1)S(1)}, u32[]{:S(2)}, u32[]{:S(2)}) collective-permute-start(bf16[3,896]{0,1:T(8,128)(2,1)S(1)} %slice.120), channel_id=1, source_target_pairs={{0,4},{4,8},{8,12},{12,16},{16,20},{20,24},{24,28},{28,32},{32,36}... | collective-permute-start | bytes 16136 | tf_op jit(solution)/shard_map/ppermute | solution.py:15
  204.5 11.4 %collective-permute-start.1 = (f32[10,64,128]{2,1,0:T(8,128)S(1)}, f32[10,64,128]{2,1,0:T(8,128)S(1)}, u32[]{:S(2)}, u32[]{:S(2)}) collective-permute-start(f32[10,64,128]{2,1,0:T(8,128)S(1)} %fusion.20), channel_id=1, source_target_pairs={{0,4},{4,8},{8,12},{12,16},{16,20},{20,24},{24,28},{28,32},{32,36}... | collective-permute-start | bytes 983048 | tf_op jit(solution)/shard_map/ppermute | solution.py:15
  206.4 14.7 %collective-permute-start.3 = (f32[10,64,128]{2,1,0:T(8,128)S(1)}, f32[10,64,128]{2,1,0:T(8,128)S(1)}, u32[]{:S(2)}, u32[]{:S(2)}) collective-permute-start(f32[10,64,128]{2,1,0:T(8,128)S(1)} %fusion.20), channel_id=1, source_target_pairs={{0,8},{4,12},{8,16},{12,20},{16,24},{20,28},{24,32},{28,36},{32,40... | collective-permute-start | bytes 983048 | tf_op jit(solution)/shard_map/ppermute | solution.py:15
  208.3 20.6 %collective-permute-start.5 = (f32[10,64,128]{2,1,0:T(8,128)S(1)}, f32[10,64,128]{2,1,0:T(8,128)S(1)}, u32[]{:S(2)}, u32[]{:S(2)}) collective-permute-start(f32[10,64,128]{2,1,0:T(8,128)S(1)} %fusion.20), channel_id=1, source_target_pairs={{0,12},{4,16},{8,20},{12,24},{16,28},{20,32},{24,36},{28,40},{32,4... | collective-permute-start | bytes 983048 | tf_op jit(solution)/shard_map/ppermute | solution.py:15
  210.8 18.3 %copy-start.7 = (f32[10]{0:T(128)S(1)}, f32[10]{0:T(128)}, u32[]{:S(2)}) copy-start(f32[10]{0:T(128)} %param.21) | copy-start | bytes 124
  230.7 7.4 %copy-start = (bf16[256,640]{0,1:T(8,128)(2,1)S(1)}, bf16[256,640]{0,1:T(8,128)(2,1)}, u32[]{:S(2)}) copy-start(bf16[256,640]{0,1:T(8,128)(2,1)} %get-tuple-element.20) | copy-start | bytes 983044
  233.1 15.3 %all-to-all-start.1 = ((bf16[2,4,64,640]{3,2,0,1:T(8,128)(2,1)}), bf16[2,4,64,640]{3,2,0,1:T(8,128)(2,1)S(1)}, u32[]{:S(2)}, u32[]{:S(2)}) async-start(bf16[2,4,64,640]{3,2,0,1:T(8,128)(2,1)} %copy.76), calls=%async_computation.1 | async-start | bytes 1310720 | tf_op jit(solution)/shard_map/all_to_all | solution.py:185
  249.5 0.7 copy-start.2
Sparse Core Ops, SparseCore 0:
  11.7 151.9 all-gather.2

commit v2 on v1

--- a/solution.py
+++ b/solution.py
@@ -51,12 +51,30 @@
     sub_rows = block_rows // groups
     step_width = w_steps.shape[1]
     merged = jnp.concatenate([w_values, w_states, w_gates, w_steps], axis=1)
+    shard_rows = merged.shape[0]
+    padded_rows = -(-shard_rows // 16) * 16
+    merged = jnp.pad(merged, ((0, padded_rows - shard_rows), (0, 0)))
     full = lax.all_gather(merged, "seq", axis=0, tiled=True)
-    projected = jnp.dot(block_hidden, full, preferred_element_type=jnp.float32)
+    shards = full.shape[0] // padded_rows
+
+    def spread_rows(rows):
+        count = rows.shape[0]
+        split = rows.reshape(count, shards, shard_rows)
+        split = jnp.pad(split, ((0, 0), (0, 0), (0, padded_rows - shard_rows)))
+        return split.reshape(count, shards * padded_rows)
+
+    rim_hidden = from_behind(block_hidden[block_rows - (conv_taps - 1) :], "seq", 1)
+    projected = jnp.dot(spread_rows(block_hidden), full, preferred_element_type=jnp.float32)
+    rim_projected = jnp.dot(spread_rows(rim_hidden), full, preferred_element_type=jnp.float32)
     conv_end = local_width + 2 * state_width
     pre_rows = projected[:, :conv_end].astype(jnp.bfloat16)
+    prior_rim = rim_projected[:, :conv_end].astype(jnp.bfloat16)
     gates_sum = projected[:, conv_end : conv_end + local_width]
     steps_sum = projected[:, conv_end + local_width : conv_end + local_width + step_width]
+    head_gates = gates_sum.astype(jnp.bfloat16)
+    gates_tokens = lax.all_to_all(
+        head_gates.reshape(groups, sub_rows, local_width), "head", 0, 2, tiled=True
+    ).reshape(sub_rows, inner_width)
     local_taps = jnp.concatenate(
         [
             lax.dynamic_slice_in_dim(conv_weight, group_index * local_width, local_width, 1),
@@ -72,8 +90,6 @@
         axis=0,
     )
     block_start = block_index * block_rows
-    rim_rows = pre_rows[block_rows - (conv_taps - 1) :]
-    prior_rim = from_behind(rim_rows, "seq", 1)
     extended = jnp.concatenate([prior_rim, pre_rows], axis=0)
     ext_positions = (
         block_start - (conv_taps - 1) + jnp.arange(block_rows + conv_taps - 1, dtype=jnp.int32)
@@ -139,11 +155,14 @@
     stretch_gates = (
         jnp.exp(decay_heads[:, :, -1]) * (last_ids == prior_ids).astype(jnp.float32)[:, None]
     )
-    own_pair = (stretch_gates[0], stretch_states[0])
-    g1, s1 = from_behind(own_pair, "seq", 1)
-    g2, s2 = from_behind(own_pair, "seq", 2)
-    g3, s3 = from_behind(own_pair, "seq", 3)
-    incoming = s1 + g1[:, None, None] * (s2 + g2[:, None, None] * s3)
+    own_gate = jnp.broadcast_to(stretch_gates[0][:, None, None], (local_heads, 8, state_width))
+    packed = jnp.concatenate([stretch_states[0], own_gate], axis=1)
+    p1 = from_behind(packed, "seq", 1)
+    p2 = from_behind(packed, "seq", 2)
+    p3 = from_behind(packed, "seq", 3)
+    g1 = p1[:, head_width : head_width + 1, :1]
+    g2 = p2[:, head_width : head_width + 1, :1]
+    incoming = p1[:, :head_width] + g1 * (p2[:, :head_width] + g2 * p3[:, :head_width])
     arriving = incoming[None]
     carry_mask = (stretch_ids == prior_ids[:, None]).astype(jnp.float32)
     carry_decay = jnp.exp(log_decay) * carry_mask[:, :, None]
@@ -180,10 +199,10 @@
     )
     end_states = end_states + end_carry[:, :, None, None] * arriving
     final_block = jnp.sum(end_states, axis=0)[None]
-    head_gates = gates_sum.astype(jnp.bfloat16)
-    both = jnp.stack([ssm_rows, head_gates]).reshape(2, groups, sub_rows, local_width)
-    returned = lax.all_to_all(both, "head", split_axis=1, concat_axis=3, tiled=True)
-    token_rows = returned.reshape(2, sub_rows, inner_width).astype(jnp.float32)
+    y_tokens = lax.all_to_all(
+        ssm_rows.reshape(groups, sub_rows, local_width), "head", 0, 2, tiled=True
+    ).reshape(sub_rows, inner_width)
+    token_rows = (y_tokens.astype(jnp.float32), gates_tokens.astype(jnp.float32))
     gated = token_rows[0] * jax.nn.silu(token_rows[1])
     mean_square = jnp.mean(gated * gated, axis=1)
     scaled = gated * lax.rsqrt(mean_square + epsilon)[:, None] * norm_gain[None, :]

time: 261 us -> 248 us (0.950)
  waiting for transfers between devices: 170 us -> 149 us
  matrix products: 8.43 us -> 19.7 us
  local copies, waits for them, and re-layouts: 26.9 us -> 22 us
    all_gather x1, waiting for transfers between devices: 138 us -> 123 us  [on_device(): full = lax.all_gather(merged, 'seq', axis=0, tiled=True)]
    unnamed x24 -> x27, local copies, waits for them, and re-layouts: 16 us -> 3.09 us
    dot_general x1 -> x2, matrix products: 5.85 us -> 15.4 us  [the longest x1 8.69 us: on_device(): jnp.dot(spread_rows(block_hidden), full, preferred_element_type=jnp.float32)]
    ppermute x6 -> x4, waiting for transfers between devices: 21.9 us -> 12.6 us  [from_behind(): return lax.ppermute(block, axis, route)]
    all_to_all x1, waiting for transfers between devices: 0.01 us -> 8.16 us  [on_device(): lax.all_to_all(jnp.broadcast_to(hidden[None], (groups,) + hidden.shape),...]
    all_to_all x1 -> x2, starting transfers between devices: 4.28 us -> 8.55 us  [the longest x1 4.28 us: on_device(): lax.all_to_all(head_gates.reshape(groups, sub_rows, local_width), 'head',...]
    all_to_all x1 -> x2, waiting for transfers between devices: 9.34 us -> 5.5 us  [the longest x1 5.5 us: on_device(): lax.all_to_all(ssm_rows.reshape(groups, sub_rows, local_width), 'head', 0...]
    all_to_all x0 -> x1, local copies, waits for them, and re-layouts: none -> 3.82 us  [on_device(): lax.all_to_all(jnp.broadcast_to(hidden[None], (groups,) + hidden.shape),...]
  transfers between devices with their start and end apart: 9 -> 8, of which waited for: 6 -> 6; matrix products, arithmetic and copies ran while one was open for 11% -> 11% of each run, Pallas kernels for 0% -> 0%
where the time goes in v2:
time: 248 us; the launch traced here: 246 us
  waiting for transfers between devices  149 us (60%)
  starting transfers between devices  23.8 us (10%)
  local copies, waits for them, and re-layouts  22 us (9%)
  matrix products  19.7 us (8%)
  between operations  18.4 us (7%)
  other arithmetic  13.4 us (5%)
    all_gather x1, waiting for transfers between devices, on_device(): full = lax.all_gather(merged, 'seq', axis=0, tiled=True)  123 us
    ppermute x4, waiting for transfers between devices, from_behind(): return lax.ppermute(block, axis, route)  12.6 us
    ppermute x4, starting transfers between devices, from_behind(): return lax.ppermute(block, axis, route)  10.8 us
    dot_general x1, matrix products, on_device(): jnp.dot(spread_rows(block_hidden), full, preferred_element_type=jnp.float32)  8.69 us
    all_to_all x1, waiting for transfers between devices, on_device(): lax.all_to_all(jnp.broadcast_to(hidden[None], (groups,) + hidden.shape),...  8.16 us
    dot_general x1, matrix products, on_device(): jnp.dot(spread_rows(rim_hidden), full, preferred_element_type=jnp.float32)  6.73 us
    all_to_all x1, waiting for transfers between devices, on_device(): lax.all_to_all(ssm_rows.reshape(groups, sub_rows, local_width), 'head', 0...  5.5 us
  transfers between devices with their start and end apart: 8, of which 6 were waited for; matrix products, arithmetic and copies ran while one was open for 11% of the time, Pallas kernels for 0%

profile of v2, /device:TPU:6, one launch (start us, length us, event | category | flops | bytes accessed | tf_op | source)
XLA Modules:
  0.0 246.4 jit_solution(13518906915074317925)
XLA Ops:
  7.2 0.8 copy.72
  8.0 1.4 fusion.27
  9.5 2.1 broadcast_in_dim.41
  11.6 4.5 %all-to-all-start = ((bf16[4,64,2560]{2,1,0:T(8,128)(2,1)}), bf16[4,64,2560]{2,1,0:T(8,128)(2,1)S(1)}, u32[]{:S(2)}, u32[]{:S(2)}) async-start(bf16[4,64,2560]{2,1,0:T(8,128)(2,1)} %broadcast_in_dim.41), calls=%async_computation | async-start | bytes 2621440 | tf_op jit(solution)/shard_map/all_to_all | solution.py:47
  16.1 0.7 slice.101
  16.8 0.6 fusion.58
  18.7 0.8 dynamic_slice.6
  19.9 0.5 slice.154
  20.5 0.6 slice.151
  22.3 0.6 convert_reduce_fusion.4
  23.7 0.6 select_reduce_fusion
  24.4 0.7 broadcast_compare_fusion
  25.1 0.7 fusion.19
  25.8 8.2 %all-to-all-done = bf16[4,64,2560]{2,1,0:T(8,128)(2,1)S(1)} async-done(((bf16[4,64,2560]{2,1,0:T(8,128)(2,1)}), bf16[4,64,2560]{2,1,0:T(8,128)(2,1)S(1)}, u32[]{:S(2)}, u32[]{:S(2)}) %all-to-all-start) | async-done | bytes 1310752 | tf_op jit(solution)/shard_map/all_to_all | solution.py:47
  34.0 1.9 collective-permute-start
  36.7 3.8 %copy.73 = bf16[4,64,2560]{1,0,2:T(4,128)(2,1)S(1)} copy(bf16[4,64,2560]{2,1,0:T(8,128)(2,1)} %copy-done) | data formatting | bytes 2621440 | tf_op jit(solution)/shard_map/all_to_all | solution.py:47
  40.5 3.0 %reshape_reshape.3 = bf16[256,128,20]{0,2,1:T(8,128)(2,1)} reshape(bf16[4,64,2560]{1,0,2:T(4,128)(2,1)S(1)} %copy.73) | data formatting | bytes 2621440 | tf_op jit(solution)/shard_map/reshape;reshape | solution.py:62
  43.5 1.7 pad.14
  45.8 122.8 %all-gather.2.cloned.1.call-done = bf16[4096,1546]{1,0:T(8,128)(2,1)} async-done(((bf16[32,1546]{1,0:T(8,128)(2,1)}), bf16[4096,1546]{1,0:T(8,128)(2,1)}) %all-gather.2.cloned.1.call-update) | async-done | bytes 12664848 | tf_op jit(solution)/shard_map/all_gather | solution.py:57
  168.6 8.7 %fusion.59 = (bf16[256,1546]{0,1:T(8,128)(2,1)S(1)}, f32[256,1546]{0,1:T(8,128)S(1)}) fusion(bf16[256,4096]{0,1:T(8,128)(2,1)S(1)} %bitcast.141, bf16[4096,1546]{1,0:T(8,128)(2,1)} %all-gather.2.cloned.1.call-done), kind=kOutput, calls=%fused_computation.124 | convolution fusion | flops 3242592768 | bytes 17136640 | tf_op jit(solution)/shard_map/dot_general | solution.py:67
  177.3 0.8 multiply_bitcast_fusion.1
  178.5 0.6 reduce-window.19
  179.5 0.6 pad.36
  180.1 6.7 %fusion.60 = bf16[3,1546]{1,0:T(4,128)(2,1)S(1)} fusion(bf16[3,4096]{1,0:T(4,128)(2,1)S(1)} %reshape.497, bf16[4096,1546]{1,0:T(8,128)(2,1)} %all-gather.2.cloned.1.call-done), kind=kOutput, calls=%fused_computation.125 | convolution fusion | flops 37994496 | bytes 12698684 | tf_op jit(solution)/shard_map/dot_general | solution.py:68
  187.3 0.8 fusion.41
  188.3 0.8 fusion.42
  189.1 1.5 multiply_convert_fusion.4
  190.6 0.9 fusion.36
  192.0 3.6 %collective-permute-start.3 = (f32[10,72,128]{2,1,0:T(8,128)S(1)}, f32[10,72,128]{2,1,0:T(8,128)}, u32[]{:S(2)}, u32[]{:S(2)}) collective-permute-start(f32[10,72,128]{2,1,0:T(8,128)S(1)} %pad_maximum_fusion.1), channel_id=1, source_target_pairs={{0,12},{4,16},{8,20},{12,24},{16,28},{20,32},{24,36},{28,40},{32,4... | collective-permute-start | bytes 1105928 | tf_op jit(solution)/shard_map/ppermute | solution.py:15
  195.6 2.2 collective-permute-start.2
  197.8 3.1 %collective-permute-start.1 = (f32[10,72,128]{2,1,0:T(8,128)S(1)}, f32[10,72,128]{2,1,0:T(8,128)S(1)}, u32[]{:S(2)}, u32[]{:S(2)}) collective-permute-start(f32[10,72,128]{2,1,0:T(8,128)S(1)} %pad_maximum_fusion.1), channel_id=1, source_target_pairs={{0,4},{4,8},{8,12},{12,16},{16,20},{20,24},{24,28},{28,32},{32,36}... | collective-permute-start | bytes 1105928 | tf_op jit(solution)/shard_map/ppermute | solution.py:15
  201.0 0.6 copy.94
  201.6 0.6 copy.95
  202.2 0.9 copy.85
  203.1 4.3 %all-to-all-start.2 = ((bf16[4,64,640]{2,1,0:T(8,128)(2,1)}), bf16[4,64,640]{2,1,0:T(8,128)(2,1)S(1)}, u32[]{:S(2)}, u32[]{:S(2)}) async-start(bf16[4,64,640]{2,1,0:T(8,128)(2,1)} %bitcast.32), calls=%async_computation.2 | async-start | bytes 655360 | tf_op jit(solution)/shard_map/all_to_all | solution.py:75
  207.4 0.7 add_negate_fusion
  208.1 1.9 fusion.7
  210.0 0.6 exponential_multiply_fusion
  210.6 8.0 %collective-permute-done.2 = f32[10,72,128]{2,1,0:T(8,128)S(1)} collective-permute-done((f32[10,72,128]{2,1,0:T(8,128)S(1)}, f32[10,72,128]{2,1,0:T(8,128)S(1)}, u32[]{:S(2)}, u32[]{:S(2)}) %collective-permute-start.2) | collective-permute-done | bytes 368672 | tf_op jit(solution)/shard_map/ppermute | solution.py:15
  218.8 4.4 %collective-permute-done.1 = f32[10,72,128]{2,1,0:T(8,128)S(1)} collective-permute-done((f32[10,72,128]{2,1,0:T(8,128)S(1)}, f32[10,72,128]{2,1,0:T(8,128)S(1)}, u32[]{:S(2)}, u32[]{:S(2)}) %collective-permute-start.1) | collective-permute-done | bytes 368672 | tf_op jit(solution)/shard_map/ppermute | solution.py:15
  223.3 1.1 fusion.18
  225.0 1.4 copy.83
  226.4 4.3 %all-to-all-start.1 = ((bf16[4,64,640]{2,1,0:T(8,128)(2,1)}), bf16[4,64,640]{2,1,0:T(8,128)(2,1)S(1)}, u32[]{:S(2)}, u32[]{:S(2)}) async-start(bf16[4,64,640]{2,1,0:T(8,128)(2,1)} %copy.83), calls=%async_computation.1 | async-start | bytes 655360 | tf_op jit(solution)/shard_map/all_to_all | solution.py:202
  230.7 0.4 copy.86
  231.2 1.0 add_bitcast_fusion
  232.2 5.5 %all-to-all-done.1 = bf16[4,64,640]{2,1,0:T(8,128)(2,1)S(1)} async-done(((bf16[4,64,640]{2,1,0:T(8,128)(2,1)}), bf16[4,64,640]{2,1,0:T(8,128)(2,1)S(1)}, u32[]{:S(2)}, u32[]{:S(2)}) %all-to-all-start.1) | async-done | bytes 327712 | tf_op jit(solution)/shard_map/all_to_all | solution.py:202
  238.1 0.4 copy.84
  238.6 1.0 multiply_convert_fusion.5
  (80 shorter events, 4.7 us)
Async XLA Ops:
  7.2 12.3 %copy-start.6 = (s32[64]{0:T(128)S(1)}, s32[64]{0:T(128)}, u32[]{:S(2)}) copy-start(s32[64]{0:T(128)} %param.23) | copy-start | bytes 772
  7.2 16.4 %copy-start.2 = (f32[4,2816]{1,0:T(4,128)S(1)}, f32[4,2816]{1,0:T(4,128)}, u32[]{:S(2)}) copy-start(f32[4,2816]{1,0:T(4,128)} %param.17) | copy-start | bytes 135172
  7.2 29.4 %slice-start = ((f32[4,2816]{1,0:T(4,128)}), f32[4,256]{1,0:T(4,128)S(1)}, s32[]{:S(2)}) async-start(f32[4,2816]{1,0:T(4,128)} %param.17), calls=%async_computation.4 | async-start | bytes 8192 | tf_op jit(solution)/shard_map/slice | solution.py:81
  7.2 161.4 %all-gather.2.cloned.1.call-start = ((), (), s32[]{:S(2)}) async-start(), calls=%async_computation.3 | async-start | bytes 13737984 | tf_op jit(solution)/shard_map/all_gather | solution.py:57
  11.6 22.4 %all-to-all-start = ((bf16[4,64,2560]{2,1,0:T(8,128)(2,1)}), bf16[4,64,2560]{2,1,0:T(8,128)(2,1)S(1)}, u32[]{:S(2)}, u32[]{:S(2)}) async-start(bf16[4,64,2560]{2,1,0:T(8,128)(2,1)} %broadcast_in_dim.41), calls=%async_computation | async-start | bytes 2621440 | tf_op jit(solution)/shard_map/all_to_all | solution.py:47
  34.0 2.6 %copy-start = (bf16[4,64,2560]{2,1,0:T(8,128)(2,1)}, bf16[4,64,2560]{2,1,0:T(8,128)(2,1)S(1)}, u32[]{:S(2)}) copy-start(bf16[4,64,2560]{2,1,0:T(8,128)(2,1)S(1)} %all-to-all-done) | copy-start | bytes 3932164
  34.0 11.4 %collective-permute-start = (bf16[3,2560]{1,0:T(4,128)(2,1)S(1)}, bf16[3,2560]{1,0:T(4,128)(2,1)S(1)}, u32[]{:S(2)}, u32[]{:S(2)}) collective-permute-start(bf16[3,2560]{1,0:T(4,128)(2,1)S(1)} %slice.134), channel_id=1, source_target_pairs={{0,4},{4,8},{8,12},{12,16},{16,20},{20,24},{24,28},{28,32},{32,36}... | collective-permute-start | bytes 46088 | tf_op jit(solution)/shard_map/ppermute | solution.py:15
  168.6 8.7 %copy-start.4 = (f32[10]{0:T(128)S(1)}, f32[10]{0:T(128)}, u32[]{:S(2)}) copy-start(f32[10]{0:T(128)} %param.19) | copy-start | bytes 124
  168.6 8.7 %copy-start.7 = (f32[10]{0:T(128)S(1)}, f32[10]{0:T(128)}, u32[]{:S(2)}) copy-start(f32[10]{0:T(128)} %param.20) | copy-start | bytes 124
  177.3 1.2 copy-start.5
  189.1 12.5 %copy-start.1 = (f32[16,2,128]{2,1,0:T(2,128)S(1)}, f32[16,2,128]{2,1,0:T(2,128)}, u32[]{:S(2)}) copy-start(f32[16,2,128]{2,1,0:T(2,128)} %pad.36) | copy-start | bytes 49156
  192.0 31.3 %collective-permute-start.3 = (f32[10,72,128]{2,1,0:T(8,128)S(1)}, f32[10,72,128]{2,1,0:T(8,128)}, u32[]{:S(2)}, u32[]{:S(2)}) collective-permute-start(f32[10,72,128]{2,1,0:T(8,128)S(1)} %pad_maximum_fusion.1), channel_id=1, source_target_pairs={{0,12},{4,16},{8,20},{12,24},{16,28},{20,32},{24,36},{28,40},{32,4... | collective-permute-start | bytes 1105928 | tf_op jit(solution)/shard_map/ppermute | solution.py:15
  195.6 23.0 %collective-permute-start.2 = (f32[10,72,128]{2,1,0:T(8,128)S(1)}, f32[10,72,128]{2,1,0:T(8,128)S(1)}, u32[]{:S(2)}, u32[]{:S(2)}) collective-permute-start(f32[10,72,128]{2,1,0:T(8,128)S(1)} %pad_maximum_fusion.1), channel_id=1, source_target_pairs={{0,8},{4,12},{8,16},{12,20},{16,24},{20,28},{24,32},{28,36},{32,40... | collective-permute-start | bytes 1105928 | tf_op jit(solution)/shard_map/ppermute | solution.py:15
  197.8 25.3 %collective-permute-start.1 = (f32[10,72,128]{2,1,0:T(8,128)S(1)}, f32[10,72,128]{2,1,0:T(8,128)S(1)}, u32[]{:S(2)}, u32[]{:S(2)}) collective-permute-start(f32[10,72,128]{2,1,0:T(8,128)S(1)} %pad_maximum_fusion.1), channel_id=1, source_target_pairs={{0,4},{4,8},{8,12},{12,16},{16,20},{20,24},{24,28},{28,32},{32,36}... | collective-permute-start | bytes 1105928 | tf_op jit(solution)/shard_map/ppermute | solution.py:15
  203.1 23.3 %all-to-all-start.2 = ((bf16[4,64,640]{2,1,0:T(8,128)(2,1)}), bf16[4,64,640]{2,1,0:T(8,128)(2,1)S(1)}, u32[]{:S(2)}, u32[]{:S(2)}) async-start(bf16[4,64,640]{2,1,0:T(8,128)(2,1)} %bitcast.32), calls=%async_computation.2 | async-start | bytes 655360 | tf_op jit(solution)/shard_map/all_to_all | solution.py:75
  208.1 16.3 %copy-start.8 = (f32[10]{0:T(128)S(1)}, f32[10]{0:T(128)}, u32[]{:S(2)}) copy-start(f32[10]{0:T(128)} %param.21) | copy-start | bytes 124
  225.0 6.2 %copy-start.9 = (f32[10]{0:T(128)S(1)}, f32[10]{0:T(128)}, u32[]{:S(2)}) copy-start(f32[10]{0:T(128)} %exponential_multiply_fusion) | copy-start | bytes 124
  226.4 11.3 %all-to-all-start.1 = ((bf16[4,64,640]{2,1,0:T(8,128)(2,1)}), bf16[4,64,640]{2,1,0:T(8,128)(2,1)S(1)}, u32[]{:S(2)}, u32[]{:S(2)}) async-start(bf16[4,64,640]{2,1,0:T(8,128)(2,1)} %copy.83), calls=%async_computation.1 | async-start | bytes 655360 | tf_op jit(solution)/shard_map/all_to_all | solution.py:202
  231.2 7.4 %copy-start.3 = (f32[2560]{0:T(1024)S(1)}, f32[2560]{0:T(1024)}, u32[]{:S(2)}) copy-start(f32[2560]{0:T(1024)} %param.22) | copy-start | bytes 30724
Sparse Core Ops, SparseCore 0:
  11.7 156.8 all-gather.1

commit v3 on v2

--- a/solution.py
+++ b/solution.py
@@ -64,11 +64,15 @@
         return split.reshape(count, shards * padded_rows)
 
     rim_hidden = from_behind(block_hidden[block_rows - (conv_taps - 1) :], "seq", 1)
-    projected = jnp.dot(spread_rows(block_hidden), full, preferred_element_type=jnp.float32)
-    rim_projected = jnp.dot(spread_rows(rim_hidden), full, preferred_element_type=jnp.float32)
+    rim_count = rim_hidden.shape[0]
+    both_rows = jnp.concatenate(
+        [block_hidden, rim_hidden, jnp.zeros((8 - rim_count, block_hidden.shape[1]), jnp.bfloat16)]
+    )
+    projected = jnp.dot(spread_rows(both_rows), full, preferred_element_type=jnp.float32)
     conv_end = local_width + 2 * state_width
+    prior_rim = projected[block_rows : block_rows + rim_count, :conv_end].astype(jnp.bfloat16)
+    projected = projected[:block_rows]
     pre_rows = projected[:, :conv_end].astype(jnp.bfloat16)
-    prior_rim = rim_projected[:, :conv_end].astype(jnp.bfloat16)
     gates_sum = projected[:, conv_end : conv_end + local_width]
     steps_sum = projected[:, conv_end + local_width : conv_end + local_width + step_width]
     head_gates = gates_sum.astype(jnp.bfloat16)
@@ -156,12 +160,13 @@
         jnp.exp(decay_heads[:, :, -1]) * (last_ids == prior_ids).astype(jnp.float32)[:, None]
     )
     own_gate = jnp.broadcast_to(stretch_gates[0][:, None, None], (local_heads, 8, state_width))
-    packed = jnp.concatenate([stretch_states[0], own_gate], axis=1)
+    packed = jnp.concatenate([stretch_states[0], own_gate], axis=1).astype(jnp.bfloat16)
     p1 = from_behind(packed, "seq", 1)
     p2 = from_behind(packed, "seq", 2)
     p3 = from_behind(packed, "seq", 3)
     g1 = p1[:, head_width : head_width + 1, :1]
     g2 = p2[:, head_width : head_width + 1, :1]
+    p1, p2, p3, g1, g2 = (part.astype(jnp.float32) for part in (p1, p2, p3, g1, g2))
     incoming = p1[:, :head_width] + g1 * (p2[:, :head_width] + g2 * p3[:, :head_width])
     arriving = incoming[None]
     carry_mask = (stretch_ids == prior_ids[:, None]).astype(jnp.float32)

time: 248 us -> 230 us (0.927)
  waiting for transfers between devices: 149 us -> 137 us
  matrix products: 19.7 us -> 13 us
    ppermute x4, waiting for transfers between devices: 12.6 us -> 2.03 us  [from_behind(): return lax.ppermute(block, axis, route)]
    dot_general x2 -> x1, matrix products: 15.4 us -> 7.46 us  [on_device(): jnp.dot(spread_rows(both_rows), full, preferred_element_type=jnp.float32)]
    concatenate x0 -> x4, local copies, waits for them, and re-layouts: none -> 4.17 us  [on_device(): jnp.concatenate([block_hidden, rim_hidden, jnp.zeros((8 - rim_count, bloc...]
    all_gather x1, waiting for transfers between devices: 123 us -> 120 us  [on_device(): full = lax.all_gather(merged, 'seq', axis=0, tiled=True)]
    another operation x10 -> x9, local copies, waits for them, and re-layouts: 3.28 us -> 0.31 us  [the longest x1 2.96 us: spread_rows(): split = rows.reshape(count, shards, shard_rows)]
    concatenate x1 -> x2, other arithmetic: 0.03 us -> 2.66 us  [the longest x1 1.97 us: on_device(): jnp.concatenate([block_hidden, rim_hidden, jnp.zeros((8 - rim_count, bloc...]
  transfers between devices with their start and end apart: 8 -> 8, of which waited for: 6 -> 5; matrix products, arithmetic and copies ran while one was open for 11% -> 13% of each run, Pallas kernels for 0% -> 0%
where the time goes in v3:
time: 230 us; the launch traced here: 228 us
  waiting for transfers between devices  137 us (60%)
  starting transfers between devices  24.6 us (11%)
  local copies, waits for them, and re-layouts  22 us (10%)
  between operations  18.5 us (8%)
  matrix products  13 us (6%)
  other arithmetic  12.6 us (5%)
    all_gather x1, waiting for transfers between devices, on_device(): full = lax.all_gather(merged, 'seq', axis=0, tiled=True)  120 us
    ppermute x4, starting transfers between devices, from_behind(): return lax.ppermute(block, axis, route)  11.2 us
    all_to_all x1, waiting for transfers between devices, on_device(): lax.all_to_all(jnp.broadcast_to(hidden[None], (groups,) + hidden.shape),...  8.74 us
    dot_general x1, matrix products, on_device(): jnp.dot(spread_rows(both_rows), full, preferred_element_type=jnp.float32)  7.46 us
    all_to_all x1, waiting for transfers between devices, on_device(): lax.all_to_all(ssm_rows.reshape(groups, sub_rows, local_width), 'head', 0...  6.54 us
    all_to_all x1, starting transfers between devices, on_device(): lax.all_to_all(ssm_rows.reshape(groups, sub_rows, local_width), 'head', 0...  4.63 us
  transfers between devices with their start and end apart: 8, of which 5 were waited for; matrix products, arithmetic and copies ran while one was open for 13% of the time, Pallas kernels for 0%

profile of v3, /device:TPU:6, one launch (start us, length us, event | category | flops | bytes accessed | tf_op | source)
XLA Modules:
  0.0 227.7 jit_solution(11827139594763536378)
XLA Ops:
  7.2 0.8 copy.132
  8.0 1.4 fusion.28
  9.5 2.1 broadcast_in_dim.43
  11.6 4.5 %all-to-all-start = ((bf16[4,64,2560]{2,1,0:T(8,128)(2,1)}), bf16[4,64,2560]{2,1,0:T(8,128)(2,1)S(1)}, u32[]{:S(2)}, u32[]{:S(2)}) async-start(bf16[4,64,2560]{2,1,0:T(8,128)(2,1)} %broadcast_in_dim.43), calls=%async_computation | async-start | bytes 2621440 | tf_op jit(solution)/shard_map/all_to_all | solution.py:47
  16.4 0.7 slice.114
  17.1 0.8 dynamic_slice.6
  18.0 0.6 slice.167
  18.6 0.6 fusion.60
  20.6 0.5 slice.170
  22.3 0.6 convert_reduce_fusion.4
  23.8 0.6 select_reduce_fusion
  24.4 0.7 broadcast_compare_fusion
  25.3 8.7 %all-to-all-done = bf16[4,64,2560]{2,1,0:T(8,128)(2,1)S(1)} async-done(((bf16[4,64,2560]{2,1,0:T(8,128)(2,1)}), bf16[4,64,2560]{2,1,0:T(8,128)(2,1)S(1)}, u32[]{:S(2)}, u32[]{:S(2)}) %all-to-all-start) | async-done | bytes 1310752 | tf_op jit(solution)/shard_map/all_to_all | solution.py:47
  34.0 1.9 collective-permute-start
  36.8 3.8 %copy.130 = bf16[4,64,2560]{1,0,2:T(4,128)(2,1)S(1)} copy(bf16[4,64,2560]{2,1,0:T(8,128)(2,1)} %copy-done) | data formatting | bytes 2621440 | tf_op jit(solution)/shard_map/all_to_all | solution.py:47
  40.6 3.0 %concatenate.26 = bf16[256,128,20]{0,2,1:T(8,128)(2,1)} reshape(bf16[4,64,2560]{1,0,2:T(4,128)(2,1)S(1)} %copy.130) | data formatting | bytes 2621440 | tf_op jit(solution)/shard_map/concatenate | solution.py:68
  43.6 1.8 collective-permute-done
  45.4 0.2 concatenate.27
  45.6 0.9 copy.131
  46.5 2.0 maximum_maximum_fusion
  48.5 0.4 pad.8
  48.9 119.7 %all-gather.2.cloned.1.call-done = bf16[4096,1546]{1,0:T(8,128)(2,1)} async-done(((bf16[32,1546]{1,0:T(8,128)(2,1)}), bf16[4096,1546]{1,0:T(8,128)(2,1)}) %all-gather.2.cloned.1.call-update) | async-done | bytes 12664848 | tf_op jit(solution)/shard_map/all_gather | solution.py:57
  168.6 7.5 %fusion.61 = (bf16[264,1546]{1,0:T(8,128)(2,1)S(1)}, f32[264,1546]{1,0:T(8,128)S(1)}) fusion(bf16[264,4096]{0,1:T(8,128)(2,1)S(1)} %bitcast.127, bf16[4096,1546]{1,0:T(8,128)(2,1)} %all-gather.2.cloned.1.call-done), kind=kOutput, calls=%fused_computation.123 | convolution fusion | flops 3343923712 | bytes 17276384 | tf_op jit(solution)/shard_map/dot_general | solution.py:71
  176.2 0.9 copy-done.2
  177.3 0.6 reduce-window.19
  178.0 0.8 multiply_convert_fusion.4
  178.9 0.9 fusion.36
  181.2 0.8 multiply_convert_fusion.5
  182.2 0.2 convolution_convert_fusion
  182.6 0.7 pad_maximum_fusion.1
  183.3 3.7 %collective-permute-start.2 = (bf16[10,72,128]{2,1,0:T(8,128)(2,1)}, bf16[10,72,128]{2,1,0:T(8,128)(2,1)}, u32[]{:S(2)}, u32[]{:S(2)}) collective-permute-start(bf16[10,72,128]{2,1,0:T(8,128)(2,1)} %pad_maximum_fusion.1), channel_id=1, source_target_pairs={{0,8},{4,12},{8,16},{12,20},{16,24},{20,28},{24,32},{28,36},{32,40... | collective-permute-start | bytes 552968 | tf_op jit(solution)/shard_map/ppermute | solution.py:15
  187.0 1.9 collective-permute-start.1
  188.9 3.7 %collective-permute-start.3 = (bf16[10,72,128]{2,1,0:T(8,128)(2,1)}, bf16[10,72,128]{2,1,0:T(8,128)(2,1)}, u32[]{:S(2)}, u32[]{:S(2)}) collective-permute-start(bf16[10,72,128]{2,1,0:T(8,128)(2,1)} %pad_maximum_fusion.1), channel_id=1, source_target_pairs={{0,12},{4,16},{8,20},{12,24},{16,28},{20,32},{24,36},{28,40},{32,4... | collective-permute-start | bytes 552968 | tf_op jit(solution)/shard_map/ppermute | solution.py:15
  192.6 1.7 slice.176
  194.5 4.3 %all-to-all-start.2 = ((bf16[4,64,640]{2,1,0:T(8,128)(2,1)}), bf16[4,64,640]{2,1,0:T(8,128)(2,1)S(1)}, u32[]{:S(2)}, u32[]{:S(2)}) async-start(bf16[4,64,640]{2,1,0:T(8,128)(2,1)} %bitcast.32), calls=%async_computation.2 | async-start | bytes 655360 | tf_op jit(solution)/shard_map/all_to_all | solution.py:79
  198.9 0.9 fusion.7
  200.2 0.9 fusion.44
  201.1 0.9 fusion.45
  202.2 1.4 fusion.11
  203.6 0.3 convert_element_type.193
  203.9 1.4 copy.144
  205.3 2.0 add_bitcast_fusion
  207.3 4.6 %all-to-all-start.1 = ((bf16[4,64,640]{2,1,0:T(8,128)(2,1)}), bf16[4,64,640]{2,1,0:T(8,128)(2,1)S(1)}, u32[]{:S(2)}, u32[]{:S(2)}) async-start(bf16[4,64,640]{2,1,0:T(8,128)(2,1)} %copy.144), calls=%async_computation.1 | async-start | bytes 655360 | tf_op jit(solution)/shard_map/all_to_all | solution.py:207
  212.0 0.4 copy.146
  212.5 6.5 %all-to-all-done.1 = bf16[4,64,640]{2,1,0:T(8,128)(2,1)S(1)} async-done(((bf16[4,64,640]{2,1,0:T(8,128)(2,1)}), bf16[4,64,640]{2,1,0:T(8,128)(2,1)S(1)}, u32[]{:S(2)}, u32[]{:S(2)}) %all-to-all-start.1) | async-done | bytes 327712 | tf_op jit(solution)/shard_map/all_to_all | solution.py:207
  219.1 0.4 copy.145
  219.6 0.3 multiply_reduce_fusion
  219.9 1.0 multiply_convert_fusion.6
  (88 shorter events, 4.0 us)
Async XLA Ops:
  7.2 8.9 %copy-start.7 = (s32[64]{0:T(128)S(1)}, s32[64]{0:T(128)}, u32[]{:S(2)}) copy-start(s32[64]{0:T(128)} %param.23) | copy-start | bytes 772
  7.2 16.4 %copy-start.4 = (f32[4,2816]{1,0:T(4,128)S(1)}, f32[4,2816]{1,0:T(4,128)}, u32[]{:S(2)}) copy-start(f32[4,2816]{1,0:T(4,128)} %param.17) | copy-start | bytes 135172
  7.2 29.5 %slice-start = ((f32[4,2816]{1,0:T(4,128)}), f32[4,256]{1,0:T(4,128)S(1)}, s32[]{:S(2)}) async-start(f32[4,2816]{1,0:T(4,128)} %param.17), calls=%async_computation.4 | async-start | bytes 8192 | tf_op jit(solution)/shard_map/slice | solution.py:85
  7.2 161.4 %all-gather.2.cloned.1.call-start = ((), (), s32[]{:S(2)}) async-start(), calls=%async_computation.3 | async-start | bytes 13737984 | tf_op jit(solution)/shard_map/all_gather | solution.py:57
  11.6 22.4 %all-to-all-start = ((bf16[4,64,2560]{2,1,0:T(8,128)(2,1)}), bf16[4,64,2560]{2,1,0:T(8,128)(2,1)S(1)}, u32[]{:S(2)}, u32[]{:S(2)}) async-start(bf16[4,64,2560]{2,1,0:T(8,128)(2,1)} %broadcast_in_dim.43), calls=%async_computation | async-start | bytes 2621440 | tf_op jit(solution)/shard_map/all_to_all | solution.py:47
  34.0 2.7 %copy-start = (bf16[4,64,2560]{2,1,0:T(8,128)(2,1)}, bf16[4,64,2560]{2,1,0:T(8,128)(2,1)S(1)}, u32[]{:S(2)}) copy-start(bf16[4,64,2560]{2,1,0:T(8,128)(2,1)S(1)} %all-to-all-done) | copy-start | bytes 3932164
  34.0 11.4 %collective-permute-start = (bf16[3,2560]{1,0:T(4,128)(2,1)S(1)}, bf16[3,2560]{1,0:T(4,128)(2,1)S(1)}, u32[]{:S(2)}, u32[]{:S(2)}) collective-permute-start(bf16[3,2560]{1,0:T(4,128)(2,1)S(1)} %slice.150), channel_id=1, source_target_pairs={{0,4},{4,8},{8,12},{12,16},{16,20},{20,24},{24,28},{28,32},{32,36}... | collective-permute-start | bytes 46088 | tf_op jit(solution)/shard_map/ppermute | solution.py:15
  168.6 8.5 %copy-start.6 = (f32[10]{0:T(128)S(1)}, f32[10]{0:T(128)}, u32[]{:S(2)}) copy-start(f32[10]{0:T(128)} %param.19) | copy-start | bytes 124
  168.6 8.5 %copy-start.8 = (f32[10]{0:T(128)S(1)}, f32[10]{0:T(128)}, u32[]{:S(2)}) copy-start(f32[10]{0:T(128)} %param.20) | copy-start | bytes 124
  176.1 0.9 copy-start.2
  182.1 16.8 %copy-start.3 = (f32[256,256]{1,0:T(8,128)S(1)}, f32[256,256]{1,0:T(8,128)}, u32[]{:S(2)}) copy-start(f32[256,256]{1,0:T(8,128)} %fusion.36) | copy-start | bytes 786436
  183.3 17.0 %collective-permute-start.2 = (bf16[10,72,128]{2,1,0:T(8,128)(2,1)}, bf16[10,72,128]{2,1,0:T(8,128)(2,1)}, u32[]{:S(2)}, u32[]{:S(2)}) collective-permute-start(bf16[10,72,128]{2,1,0:T(8,128)(2,1)} %pad_maximum_fusion.1), channel_id=1, source_target_pairs={{0,8},{4,12},{8,16},{12,20},{16,24},{20,28},{24,32},{28,36},{32,40... | collective-permute-start | bytes 552968 | tf_op jit(solution)/shard_map/ppermute | solution.py:15
  187.0 14.2 %collective-permute-start.1 = (bf16[10,72,128]{2,1,0:T(8,128)(2,1)}, bf16[10,72,128]{2,1,0:T(8,128)(2,1)}, u32[]{:S(2)}, u32[]{:S(2)}) collective-permute-start(bf16[10,72,128]{2,1,0:T(8,128)(2,1)} %pad_maximum_fusion.1), channel_id=1, source_target_pairs={{0,4},{4,8},{8,12},{12,16},{16,20},{20,24},{24,28},{28,32},{32,36}... | collective-permute-start | bytes 552968 | tf_op jit(solution)/shard_map/ppermute | solution.py:15
  188.9 13.3 %collective-permute-start.3 = (bf16[10,72,128]{2,1,0:T(8,128)(2,1)}, bf16[10,72,128]{2,1,0:T(8,128)(2,1)}, u32[]{:S(2)}, u32[]{:S(2)}) collective-permute-start(bf16[10,72,128]{2,1,0:T(8,128)(2,1)} %pad_maximum_fusion.1), channel_id=1, source_target_pairs={{0,12},{4,16},{8,20},{12,24},{16,28},{20,32},{24,36},{28,40},{32,4... | collective-permute-start | bytes 552968 | tf_op jit(solution)/shard_map/ppermute | solution.py:15
  194.5 12.8 %all-to-all-start.2 = ((bf16[4,64,640]{2,1,0:T(8,128)(2,1)}), bf16[4,64,640]{2,1,0:T(8,128)(2,1)S(1)}, u32[]{:S(2)}, u32[]{:S(2)}) async-start(bf16[4,64,640]{2,1,0:T(8,128)(2,1)} %bitcast.32), calls=%async_computation.2 | async-start | bytes 655360 | tf_op jit(solution)/shard_map/all_to_all | solution.py:79
  198.8 1.2 copy-start.1
  198.8 3.4 %copy-start.9 = (f32[10]{0:T(128)S(1)}, f32[10]{0:T(128)}, u32[]{:S(2)}) copy-start(f32[10]{0:T(128)} %param.21) | copy-start | bytes 124
  207.3 11.7 %all-to-all-start.1 = ((bf16[4,64,640]{2,1,0:T(8,128)(2,1)}), bf16[4,64,640]{2,1,0:T(8,128)(2,1)S(1)}, u32[]{:S(2)}, u32[]{:S(2)}) async-start(bf16[4,64,640]{2,1,0:T(8,128)(2,1)} %copy.144), calls=%async_computation.1 | async-start | bytes 655360 | tf_op jit(solution)/shard_map/all_to_all | solution.py:207
  212.4 7.5 %copy-start.5 = (f32[2560]{0:T(1024)S(1)}, f32[2560]{0:T(1024)}, u32[]{:S(2)}) copy-start(f32[2560]{0:T(1024)} %param.22) | copy-start | bytes 30724
Sparse Core Ops, SparseCore 0:
  11.7 156.8 all-gather.1

commit v4 on v3

--- a/solution.py
+++ b/solution.py
@@ -1,16 +1,17 @@
 import jax
 import jax.numpy as jnp
 from jax import lax
-from jax.sharding import PartitionSpec as P
+from jax.sharding import Mesh, PartitionSpec as P
 
 STRETCH = 256
+SEQ = ("x", "z", "c")
 
 
 epsilon = 1e-05
 
 
 def from_behind(block, axis, distance):
-    devices = range(lax.axis_size(axis))
+    devices = range(lax.psum(1, axis))
     route = [(i - distance, i) for i in devices if i - distance in devices]
     return lax.ppermute(block, axis, route)
 
@@ -36,7 +37,7 @@
 ):
     groups = lax.axis_size("head")
     group_index = lax.axis_index("head")
-    block_index = lax.axis_index("seq")
+    block_index = lax.axis_index(SEQ)
     local_width = w_values.shape[1]
     inner_width = local_width * groups
     local_heads = decay_rate.shape[0]
@@ -53,22 +54,36 @@
     merged = jnp.concatenate([w_values, w_states, w_gates, w_steps], axis=1)
     shard_rows = merged.shape[0]
     padded_rows = -(-shard_rows // 16) * 16
-    merged = jnp.pad(merged, ((0, padded_rows - shard_rows), (0, 0)))
-    full = lax.all_gather(merged, "seq", axis=0, tiled=True)
-    shards = full.shape[0] // padded_rows
+    half = local_width + 2 * state_width
+    merged = jnp.pad(merged, ((0, padded_rows - shard_rows), (0, 2 * half - merged.shape[1])))
+    halves = jnp.stack([merged[:, :half], merged[:, half:]])
+    own_half = lax.all_to_all(halves, "c", 0, 0, tiled=True).reshape(2 * padded_rows, half)
+    own_half = lax.all_gather(own_half, "x", axis=0, tiled=True)
+    own_half = lax.all_gather(own_half, "z", axis=0, tiled=True)
+    other_half = lax.ppermute(own_half, "c", [(0, 1), (1, 0)])
+    x_size = lax.psum(1, "x")
+    z_size = lax.psum(1, "z")
+    c_size = lax.psum(1, "c")
+    core_index = lax.axis_index("c")
 
     def spread_rows(rows):
         count = rows.shape[0]
-        split = rows.reshape(count, shards, shard_rows)
-        split = jnp.pad(split, ((0, 0), (0, 0), (0, padded_rows - shard_rows)))
-        return split.reshape(count, shards * padded_rows)
-
-    rim_hidden = from_behind(block_hidden[block_rows - (conv_taps - 1) :], "seq", 1)
+        split = rows.reshape(count, x_size, z_size, c_size, shard_rows)
+        split = jnp.pad(split, ((0, 0), (0, 0), (0, 0), (0, 0), (0, padded_rows - shard_rows)))
+        split = jnp.transpose(split, (0, 2, 1, 3, 4))
+        return split.reshape(count, x_size * z_size * c_size * padded_rows)
+
+    rim_hidden = from_behind(block_hidden[block_rows - (conv_taps - 1) :], SEQ, 1)
     rim_count = rim_hidden.shape[0]
     both_rows = jnp.concatenate(
         [block_hidden, rim_hidden, jnp.zeros((8 - rim_count, block_hidden.shape[1]), jnp.bfloat16)]
     )
-    projected = jnp.dot(spread_rows(both_rows), full, preferred_element_type=jnp.float32)
+    spread = spread_rows(both_rows)
+    with_own = jnp.dot(spread, own_half, preferred_element_type=jnp.float32)
+    with_other = jnp.dot(spread, other_half, preferred_element_type=jnp.float32)
+    first_cols = jnp.where(core_index == 0, with_own, with_other)
+    second_cols = jnp.where(core_index == 0, with_other, with_own)
+    projected = jnp.concatenate([first_cols, second_cols], axis=1)
     conv_end = local_width + 2 * state_width
     prior_rim = projected[block_rows : block_rows + rim_count, :conv_end].astype(jnp.bfloat16)
     projected = projected[:block_rows]
@@ -161,9 +176,9 @@
     )
     own_gate = jnp.broadcast_to(stretch_gates[0][:, None, None], (local_heads, 8, state_width))
     packed = jnp.concatenate([stretch_states[0], own_gate], axis=1).astype(jnp.bfloat16)
-    p1 = from_behind(packed, "seq", 1)
-    p2 = from_behind(packed, "seq", 2)
-    p3 = from_behind(packed, "seq", 3)
+    p1 = from_behind(packed, SEQ, 1)
+    p2 = from_behind(packed, SEQ, 2)
+    p3 = from_behind(packed, SEQ, 3)
     g1 = p1[:, head_width : head_width + 1, :1]
     g2 = p2[:, head_width : head_width + 1, :1]
     p1, p2, p3, g1, g2 = (part.astype(jnp.float32) for part in (p1, p2, p3, g1, g2))
@@ -216,12 +231,14 @@
 
 
 def solution(mesh):
+    seq_size, head_size = mesh.devices.shape
+    fine = Mesh(mesh.devices.reshape(4, seq_size // 8, 2, head_size), SEQ + ("head",))
     in_specs = (
-        P(("seq", "head"), None),
-        P("seq", "head"),
-        P("seq", "head"),
-        P("seq", "head"),
-        P("seq", None),
+        P(SEQ + ("head",), None),
+        P(SEQ, "head"),
+        P(SEQ, "head"),
+        P(SEQ, "head"),
+        P(SEQ, None),
         P(),
         P(),
         P("head"),
@@ -230,7 +247,7 @@
         P(),
         P(),
     )
-    out_specs = (P(("seq", "head"), None), P("seq", "head", None, None))
+    out_specs = (P(SEQ + ("head",), None), P(SEQ, "head", None, None))
     return jax.shard_map(
-        on_device, mesh=mesh, in_specs=in_specs, out_specs=out_specs, check_vma=False
-    )
+        on_device, mesh=fine, in_specs=in_specs, out_specs=out_specs, check_vma=False
+    )

time: 230 us -> 233 us (1.013)
  waiting for transfers between devices: 137 us -> 115 us
  blocking collectives: 0 us -> 20.1 us
  matrix products: 13 us -> 17 us
    all_gather x1, waiting for transfers between devices: 120 us -> 97.3 us  [on_device(): own_half = lax.all_gather(own_half, 'z', axis=0, tiled=True)]
    all_gather x0 -> x1, blocking collectives: none -> 16.3 us  [on_device(): own_half = lax.all_gather(own_half, 'x', axis=0, tiled=True)]
    all_to_all x0 -> x1, blocking collectives: none -> 3.82 us  [on_device(): lax.all_to_all(halves, 'c', 0, 0, tiled=True).reshape(2 * padded_rows, half)]
    dot_general x1 -> x2, matrix products: 7.46 us -> 10.5 us  [the longest x1 6.52 us: on_device(): with_other = jnp.dot(spread, other_half, preferred_element_type=jnp.float32)]
  transfers between devices with their start and end apart: 8 -> 9, of which waited for: 5 -> 4; matrix products, arithmetic and copies ran while one was open for 13% -> 13% of each run, Pallas kernels for 0% -> 0%
where the time goes in v4:
time: 233 us; the launch traced here: 230 us
  waiting for transfers between devices  115 us (49%)
  starting transfers between devices  24.6 us (11%)
  local copies, waits for them, and re-layouts  21.4 us (9%)
  blocking collectives  20.1 us (9%)
  between operations  18.4 us (8%)
  matrix products  17 us (7%)
  other arithmetic  13.9 us (6%)
    all_gather x1, waiting for transfers between devices, on_device(): own_half = lax.all_gather(own_half, 'z', axis=0, tiled=True)  97.3 us
    all_gather x1, blocking collectives, on_device(): own_half = lax.all_gather(own_half, 'x', axis=0, tiled=True)  16.3 us
    ppermute x4, starting transfers between devices, from_behind(): return lax.ppermute(block, axis, route)  10.7 us
    all_to_all x1, waiting for transfers between devices, on_device(): lax.all_to_all(jnp.broadcast_to(hidden[None], (groups,) + hidden.shape),...  8.98 us
    all_to_all x1, waiting for transfers between devices, on_device(): lax.all_to_all(ssm_rows.reshape(groups, sub_rows, local_width), 'head', 0...  7.91 us
    dot_general x1, matrix products, on_device(): with_other = jnp.dot(spread, other_half, preferred_element_type=jnp.float32)  6.52 us
  transfers between devices with their start and end apart: 9, of which 4 were waited for; matrix products, arithmetic and copies ran while one was open for 13% of the time, Pallas kernels for 0%

profile of v4, /device:TPU:6, one launch (start us, length us, event | category | flops | bytes accessed | tf_op | source)
XLA Modules:
  0.0 230.1 jit_solution(7230176724680147984)
XLA Ops:
  7.2 0.8 copy.136
  8.0 0.8 fusion.32
  8.9 3.8 %all_to_all.28 = bf16[2,32,896]{2,1,0:T(8,128)(2,1)S(1)} all-to-all(bf16[2,32,896]{2,1,0:T(8,128)(2,1)S(1)} %pad_maximum_fusion.2), channel_id=1, replica_groups=mesh['x'=4,'z'=16,'c'=2,'head'=4] {'c'}, dimensions={0} | all-to-all | bytes 229376 | tf_op jit(solution)/shard_map/all_to_all | solution.py:60
  12.7 16.3 %all_gather.6 = bf16[256,896]{1,0:T(8,128)(2,1)} all-gather(bf16[64,896]{1,0:T(8,128)(2,1)S(1)} %bitcast.151), channel_id=1, replica_groups=mesh['x'=4,'z'=16,'c'=2,'head'=4] {'x'}, dimensions={0}, use_global_device_ids=true | all-gather | bytes 573440 | tf_op jit(solution)/shard_map/all_gather | solution.py:61
  29.0 97.3 %all-gather.2.cloned.1.call-done = bf16[4096,896]{1,0:T(8,128)(2,1)} async-done(((bf16[256,896]{1,0:T(8,128)(2,1)}), bf16[4096,896]{1,0:T(8,128)(2,1)}) %all-gather.2.cloned.1.call-update) | async-done | bytes 7340048 | tf_op jit(solution)/shard_map/all_gather | solution.py:62
  126.2 1.9 collective-permute-start.1
  128.2 2.1 broadcast_in_dim.43
  130.3 4.3 %all-to-all-start = ((bf16[4,64,2560]{2,1,0:T(8,128)(2,1)}), bf16[4,64,2560]{2,1,0:T(8,128)(2,1)S(1)}, u32[]{:S(2)}, u32[]{:S(2)}) async-start(bf16[4,64,2560]{2,1,0:T(8,128)(2,1)} %broadcast_in_dim.43), calls=%async_computation | async-start | bytes 2621440 | tf_op jit(solution)/shard_map/all_to_all | solution.py:48
  134.9 0.7 slice.123
  135.6 0.8 dynamic_slice.6
  136.5 0.6 slice.180
  137.1 0.6 fusion.67
  139.0 0.5 slice.183
  140.8 0.6 convert_reduce_fusion.4
  142.2 0.6 select_reduce_fusion
  142.8 1.2 broadcast_compare_fusion
  144.2 9.0 %all-to-all-done = bf16[4,64,2560]{2,1,0:T(8,128)(2,1)S(1)} async-done(((bf16[4,64,2560]{2,1,0:T(8,128)(2,1)}), bf16[4,64,2560]{2,1,0:T(8,128)(2,1)S(1)}, u32[]{:S(2)}, u32[]{:S(2)}) %all-to-all-start) | async-done | bytes 1310752 | tf_op jit(solution)/shard_map/all_to_all | solution.py:48
  153.2 1.9 collective-permute-start
  155.9 3.8 %copy.133 = bf16[4,64,2560]{1,0,2:T(4,128)(2,1)S(1)} copy(bf16[4,64,2560]{2,1,0:T(8,128)(2,1)} %copy-done) | data formatting | bytes 2621440 | tf_op jit(solution)/shard_map/all_to_all | solution.py:48
  159.7 3.0 %concatenate.27 = bf16[256,4,16,2,20]{0,4,3,2,1:T(8,128)(2,1)} reshape(bf16[4,64,2560]{1,0,2:T(4,128)(2,1)S(1)} %copy.133) | data formatting | bytes 2621440 | tf_op jit(solution)/shard_map/concatenate | solution.py:78
  163.0 0.9 copy.134
  163.8 2.0 maximum_maximum_fusion
  165.8 0.6 pad_bitcast_fusion
  166.9 6.5 %fusion.68 = f32[264,896]{0,1:T(8,128)S(1)} fusion(bf16[264,4096]{0,1:T(8,128)(2,1)S(1)} %bitcast.143, bf16[4096,896]{1,0:T(8,128)(2,1)} %collective-permute-done.1), kind=kOutput, calls=%fused_computation.141 | convolution fusion | flops 1937768448 | bytes 10448896 | tf_op jit(solution)/shard_map/dot_general | solution.py:83
  173.5 4.0 %select_convert_fusion = (bf16[264,896]{0,1:T(8,128)(2,1)S(1)}, f32[264,896]{0,1:T(8,128)S(1)}) fusion(f32[264,896]{0,1:T(8,128)S(1)} %fusion.68, pred[]{:T(512)S(6)} %eq.85, bf16[264,4096]{0,1:T(8,128)(2,1)S(1)} %bitcast.144, bf16[4096,896]{1,0:T(8,128)(2,1)S(1)} %bitcast.165), kind=kOutput, calls=%fused_computation.3 | convolution fusion | flops 1938004992 | bytes 11868161 | tf_op jit(solution)/shard_map/dot_general | solution.py:82
  178.1 0.7 multiply_bitcast_fusion.1
  178.8 0.6 reduce-window.19
  179.4 0.6 copy.171
  180.2 1.5 multiply_convert_fusion.4
  181.8 0.9 fusion.43
  184.1 0.7 pad_maximum_fusion.1
  184.8 1.9 collective-permute-start.3
  186.7 3.1 %collective-permute-start.2 = (bf16[10,72,128]{2,1,0:T(8,128)(2,1)}, bf16[10,72,128]{2,1,0:T(8,128)(2,1)}, u32[]{:S(2)}, u32[]{:S(2)}) collective-permute-start(bf16[10,72,128]{2,1,0:T(8,128)(2,1)} %pad_maximum_fusion.1), channel_id=1, source_target_pairs={{0,4},{4,8},{8,12},{12,16},{16,20},{20,24},{24,28},{28,32},{32,36}... | collective-permute-start | bytes 552968 | tf_op jit(solution)/shard_map/ppermute | solution.py:16
  189.9 3.8 %collective-permute-start.4 = (bf16[10,72,128]{2,1,0:T(8,128)(2,1)}, bf16[10,72,128]{2,1,0:T(8,128)(2,1)}, u32[]{:S(2)}, u32[]{:S(2)}) collective-permute-start(bf16[10,72,128]{2,1,0:T(8,128)(2,1)} %pad_maximum_fusion.1), channel_id=1, source_target_pairs={{0,12},{4,16},{8,20},{12,24},{16,28},{20,32},{24,36},{28,40},{32,4... | collective-permute-start | bytes 552968 | tf_op jit(solution)/shard_map/ppermute | solution.py:16
  193.7 0.7 pad.35
  194.4 0.6 multiply_bitcast_fusion
  195.0 0.9 copy.151
  195.9 3.6 %all-to-all-start.3 = ((bf16[4,64,640]{2,1,0:T(8,128)(2,1)}), bf16[4,64,640]{2,1,0:T(8,128)(2,1)S(1)}, u32[]{:S(2)}, u32[]{:S(2)}) async-start(bf16[4,64,640]{2,1,0:T(8,128)(2,1)} %bitcast.36), calls=%async_computation.3 | async-start | bytes 655360 | tf_op jit(solution)/shard_map/all_to_all | solution.py:94
  199.6 1.9 fusion.7
  201.5 0.9 fusion.51
  202.4 0.9 fusion.52
  203.3 0.6 collective-permute-done.4
  203.9 1.4 fusion.11
  205.5 1.4 copy.149
  206.9 2.0 add_bitcast_fusion
  209.0 4.0 %all-to-all-start.2 = ((bf16[4,64,640]{2,1,0:T(8,128)(2,1)}), bf16[4,64,640]{2,1,0:T(8,128)(2,1)S(1)}, u32[]{:S(2)}, u32[]{:S(2)}) async-start(bf16[4,64,640]{2,1,0:T(8,128)(2,1)} %copy.149), calls=%async_computation.2 | async-start | bytes 655360 | tf_op jit(solution)/shard_map/all_to_all | solution.py:222
  213.5 7.9 %all-to-all-done.2 = bf16[4,64,640]{2,1,0:T(8,128)(2,1)S(1)} async-done(((bf16[4,64,640]{2,1,0:T(8,128)(2,1)}), bf16[4,64,640]{2,1,0:T(8,128)(2,1)S(1)}, u32[]{:S(2)}, u32[]{:S(2)}) %all-to-all-start.2) | async-done | bytes 327712 | tf_op jit(solution)/shard_map/all_to_all | solution.py:222
  222.3 1.0 multiply_convert_fusion.5
  (91 shorter events, 5.7 us)
Async XLA Ops:
  7.2 119.1 %all-gather.2.cloned.1.call-start = ((), (), s32[]{:S(2)}) async-start(), calls=%async_computation.4 | async-start | bytes 7798784 | tf_op jit(solution)/shard_map/all_gather | solution.py:62
  12.7 121.9 %copy-start.6 = (s32[64]{0:T(128)S(1)}, s32[64]{0:T(128)}, u32[]{:S(2)}) copy-start(s32[64]{0:T(128)} %param.23) | copy-start | bytes 772
  28.9 113.1 %copy-start.1 = (f32[4,2816]{1,0:T(4,128)S(1)}, f32[4,2816]{1,0:T(4,128)}, u32[]{:S(2)}) copy-start(f32[4,2816]{1,0:T(4,128)} %param.17) | copy-start | bytes 135172
  28.9 126.9 %slice-start = ((f32[4,2816]{1,0:T(4,128)}), f32[4,256]{1,0:T(4,128)S(1)}, s32[]{:S(2)}) async-start(f32[4,2816]{1,0:T(4,128)} %param.17), calls=%async_computation.5 | async-start | bytes 8192 | tf_op jit(solution)/shard_map/slice | solution.py:100
  126.2 40.6 %collective-permute-start.1 = (bf16[4096,896]{1,0:T(8,128)(2,1)}, bf16[4096,896]{1,0:T(8,128)(2,1)}, u32[]{:S(2)}, u32[]{:S(2)}) collective-permute-start(bf16[4096,896]{1,0:T(8,128)(2,1)} %all-gather.2.cloned.1.call-done), channel_id=1, source_target_pairs={{0,4},{4,0},{1,5},{5,1},{2,6},{6,2},{3,7},{7,3},{8,12},{12,8},{9,1... | collective-permute-start | bytes 22020104 | tf_op jit(solution)/shard_map/ppermute | solution.py:63
  130.3 22.8 %all-to-all-start = ((bf16[4,64,2560]{2,1,0:T(8,128)(2,1)}), bf16[4,64,2560]{2,1,0:T(8,128)(2,1)S(1)}, u32[]{:S(2)}, u32[]{:S(2)}) async-start(bf16[4,64,2560]{2,1,0:T(8,128)(2,1)} %broadcast_in_dim.43), calls=%async_computation | async-start | bytes 2621440 | tf_op jit(solution)/shard_map/all_to_all | solution.py:48
  153.1 2.7 %copy-start = (bf16[4,64,2560]{2,1,0:T(8,128)(2,1)}, bf16[4,64,2560]{2,1,0:T(8,128)(2,1)S(1)}, u32[]{:S(2)}) copy-start(bf16[4,64,2560]{2,1,0:T(8,128)(2,1)S(1)} %all-to-all-done) | copy-start | bytes 3932164
  153.2 9.5 %collective-permute-start = (bf16[3,2560]{1,0:T(4,128)(2,1)S(1)}, bf16[3,2560]{1,0:T(4,128)(2,1)S(1)}, u32[]{:S(2)}, u32[]{:S(2)}) collective-permute-start(bf16[3,2560]{1,0:T(4,128)(2,1)S(1)} %slice.161), channel_id=1, source_target_pairs={{0,4},{4,8},{8,12},{12,16},{16,20},{20,24},{24,28},{28,32},{32,36}... | collective-permute-start | bytes 46088 | tf_op jit(solution)/shard_map/ppermute | solution.py:16
  166.4 7.0 %slice-start.1 = ((s8[7340032]{0:T(1024)(128)(4,1)}), s8[4194304]{0:T(1024)(128)(4,1)S(1)}, s32[]{:S(2)}) async-start(s8[7340032]{0:T(1024)(128)(4,1)} %bitcast.164), calls=%async_computation.6 | async-start | bytes 8388608
  166.9 6.5 %slice-start.2 = ((s8[7340032]{0:T(1024)(128)(4,1)}), s8[3145728]{0:T(1024)(128)(4,1)S(1)}, s32[]{:S(2)}) async-start(s8[7340032]{0:T(1024)(128)(4,1)} %bitcast.164), calls=%async_computation.7 | async-start | bytes 6291456
  177.5 0.7 copy-start.3
  177.5 0.7 copy-start.7
  183.1 0.6 copy-start.4
  184.8 16.7 %collective-permute-start.3 = (bf16[10,72,128]{2,1,0:T(8,128)(2,1)}, bf16[10,72,128]{2,1,0:T(8,128)(2,1)}, u32[]{:S(2)}, u32[]{:S(2)}) collective-permute-start(bf16[10,72,128]{2,1,0:T(8,128)(2,1)} %pad_maximum_fusion.1), channel_id=1, source_target_pairs={{0,8},{4,12},{8,16},{12,20},{16,24},{20,28},{24,32},{28,36},{32,40... | collective-permute-start | bytes 552968 | tf_op jit(solution)/shard_map/ppermute | solution.py:16
  186.7 15.7 %collective-permute-start.2 = (bf16[10,72,128]{2,1,0:T(8,128)(2,1)}, bf16[10,72,128]{2,1,0:T(8,128)(2,1)}, u32[]{:S(2)}, u32[]{:S(2)}) collective-permute-start(bf16[10,72,128]{2,1,0:T(8,128)(2,1)} %pad_maximum_fusion.1), channel_id=1, source_target_pairs={{0,4},{4,8},{8,12},{12,16},{16,20},{20,24},{24,28},{28,32},{32,36}... | collective-permute-start | bytes 552968 | tf_op jit(solution)/shard_map/ppermute | solution.py:16
  189.9 14.0 %collective-permute-start.4 = (bf16[10,72,128]{2,1,0:T(8,128)(2,1)}, bf16[10,72,128]{2,1,0:T(8,128)(2,1)}, u32[]{:S(2)}, u32[]{:S(2)}) collective-permute-start(bf16[10,72,128]{2,1,0:T(8,128)(2,1)} %pad_maximum_fusion.1), channel_id=1, source_target_pairs={{0,12},{4,16},{8,20},{12,24},{16,28},{20,32},{24,36},{28,40},{32,4... | collective-permute-start | bytes 552968 | tf_op jit(solution)/shard_map/ppermute | solution.py:16
  195.9 13.1 %all-to-all-start.3 = ((bf16[4,64,640]{2,1,0:T(8,128)(2,1)}), bf16[4,64,640]{2,1,0:T(8,128)(2,1)S(1)}, u32[]{:S(2)}, u32[]{:S(2)}) async-start(bf16[4,64,640]{2,1,0:T(8,128)(2,1)} %bitcast.36), calls=%async_computation.3 | async-start | bytes 655360 | tf_op jit(solution)/shard_map/all_to_all | solution.py:94
  199.6 1.9 copy-start.5
  199.6 4.3 %copy-start.8 = (f32[10]{0:T(128)S(1)}, f32[10]{0:T(128)}, u32[]{:S(2)}) copy-start(f32[10]{0:T(128)} %param.21) | copy-start | bytes 124
  209.0 12.5 %all-to-all-start.2 = ((bf16[4,64,640]{2,1,0:T(8,128)(2,1)}), bf16[4,64,640]{2,1,0:T(8,128)(2,1)S(1)}, u32[]{:S(2)}, u32[]{:S(2)}) async-start(bf16[4,64,640]{2,1,0:T(8,128)(2,1)} %copy.149), calls=%async_computation.2 | async-start | bytes 655360 | tf_op jit(solution)/shard_map/all_to_all | solution.py:222
  213.5 8.8 %copy-start.2 = (f32[2560]{0:T(1024)S(1)}, f32[2560]{0:T(1024)}, u32[]{:S(2)}) copy-start(f32[2560]{0:T(1024)} %param.22) | copy-start | bytes 30724
Sparse Core Ops, SparseCore 0:
  29.1 97.1 all-gather.1

commit v5 on v4

--- a/solution.py
+++ b/solution.py
@@ -59,6 +59,7 @@
     halves = jnp.stack([merged[:, :half], merged[:, half:]])
     own_half = lax.all_to_all(halves, "c", 0, 0, tiled=True).reshape(2 * padded_rows, half)
     own_half = lax.all_gather(own_half, "x", axis=0, tiled=True)
+    block_hidden, own_half = lax.optimization_barrier((block_hidden, own_half))
     own_half = lax.all_gather(own_half, "z", axis=0, tiled=True)
     other_half = lax.ppermute(own_half, "c", [(0, 1), (1, 0)])
     x_size = lax.psum(1, "x")

time: 233 us -> 224 us (0.961)
  local copies, waits for them, and re-layouts: 21.4 us -> 18.5 us
    all_to_all x1, waiting for transfers between devices: 8.98 us -> 2.98 us  [on_device(): lax.all_to_all(jnp.broadcast_to(hidden[None], (groups,) + hidden.shape),...]
    ppermute x4, waiting for transfers between devices: 0.57 us -> 5.1 us  [from_behind(): return lax.ppermute(block, axis, route)]
    all_to_all x1 -> x0, local copies, waits for them, and re-layouts: 3.82 us -> none  [on_device(): lax.all_to_all(jnp.broadcast_to(hidden[None], (groups,) + hidden.shape),...]
    reshape x0 -> x1, local copies, waits for them, and re-layouts: none -> 2.51 us  [spread_rows(): split = rows.reshape(count, x_size, z_size, c_size, shard_rows)]
  transfers between devices with their start and end apart: 9 -> 9, of which waited for: 4 -> 5; matrix products, arithmetic and copies ran while one was open for 13% -> 11% of each run, Pallas kernels for 0% -> 0%
where the time goes in v5:
time: 224 us; the launch traced here: 222 us
  waiting for transfers between devices  113 us (50%)
  starting transfers between devices  24 us (11%)
  blocking collectives  19.1 us (9%)
  local copies, waits for them, and re-layouts  18.5 us (8%)
  between operations  18.4 us (8%)
  matrix products  17 us (8%)
  other arithmetic  12.3 us (5%)
    all_gather x1, waiting for transfers between devices, on_device(): own_half = lax.all_gather(own_half, 'z', axis=0, tiled=True)  97.9 us
    all_gather x1, blocking collectives, on_device(): own_half = lax.all_gather(own_half, 'x', axis=0, tiled=True)  15.2 us
    ppermute x4, starting transfers between devices, from_behind(): return lax.ppermute(block, axis, route)  9.09 us
    dot_general x1, matrix products, on_device(): with_other = jnp.dot(spread, other_half, preferred_element_type=jnp.float32)  6.52 us
    all_to_all x1, waiting for transfers between devices, on_device(): lax.all_to_all(ssm_rows.reshape(groups, sub_rows, local_width), 'head', 0...  6.5 us
    ppermute x4, waiting for transfers between devices, from_behind(): return lax.ppermute(block, axis, route)  5.1 us
  transfers between devices with their start and end apart: 9, of which 5 were waited for; matrix products, arithmetic and copies ran while one was open for 11% of the time, Pallas kernels for 0%

profile of v5, /device:TPU:6, one launch (start us, length us, event | category | flops | bytes accessed | tf_op | source)
XLA Modules:
  0.0 221.8 jit_solution(2296827116824187327)
XLA Ops:
  7.2 0.8 copy.129
  8.0 0.8 fusion.32
  8.8 3.8 %all_to_all.28 = bf16[2,32,896]{2,1,0:T(8,128)(2,1)S(1)} all-to-all(bf16[2,32,896]{2,1,0:T(8,128)(2,1)S(1)} %pad_maximum_fusion.2), channel_id=1, replica_groups=mesh['x'=4,'z'=16,'c'=2,'head'=4] {'c'}, dimensions={0} | all-to-all | bytes 229376 | tf_op jit(solution)/shard_map/all_to_all | solution.py:60
  12.6 2.2 broadcast_in_dim.43
  14.8 4.5 %all-to-all-start = ((bf16[4,64,2560]{2,1,0:T(8,128)(2,1)}), bf16[4,64,2560]{2,1,0:T(8,128)(2,1)S(1)}, u32[]{:S(2)}, u32[]{:S(2)}) async-start(bf16[4,64,2560]{2,1,0:T(8,128)(2,1)} %broadcast_in_dim.43), calls=%async_computation | async-start | bytes 2621440 | tf_op jit(solution)/shard_map/all_to_all | solution.py:48
  19.2 15.2 %all_gather.6 = bf16[256,896]{1,0:T(8,128)(2,1)} all-gather(bf16[64,896]{1,0:T(8,128)(2,1)S(1)} %bitcast.152), channel_id=1, replica_groups=mesh['x'=4,'z'=16,'c'=2,'head'=4] {'x'}, dimensions={0}, use_global_device_ids=true | all-gather | bytes 573440 | tf_op jit(solution)/shard_map/all_gather | solution.py:61
  34.5 3.0 %all-to-all-done = bf16[4,64,2560]{2,1,0:T(8,128)(2,1)S(1)} async-done(((bf16[4,64,2560]{2,1,0:T(8,128)(2,1)}), bf16[4,64,2560]{2,1,0:T(8,128)(2,1)S(1)}, u32[]{:S(2)}, u32[]{:S(2)}) %all-to-all-start) | async-done | bytes 1310752 | tf_op jit(solution)/shard_map/all_to_all | solution.py:48
  37.5 97.9 %all-gather.2.cloned.1.call-done = bf16[4096,896]{1,0:T(8,128)(2,1)} async-done(((bf16[256,896]{1,0:T(8,128)(2,1)}), bf16[4096,896]{1,0:T(8,128)(2,1)}) %all-gather.2.cloned.1.call-update) | async-done | bytes 7340048 | tf_op jit(solution)/shard_map/all_gather | solution.py:63
  135.4 1.9 collective-permute-start.1
  137.7 0.7 slice.123
  138.4 0.8 dynamic_slice.6
  139.3 0.6 slice.179
  139.9 0.6 fusion.67
  141.8 0.5 slice.182
  143.6 0.6 convert_reduce_fusion.4
  144.9 0.6 select_reduce_fusion
  145.6 1.2 broadcast_compare_fusion
  147.1 2.4 %collective-permute-start = (bf16[3,2560]{1,0:T(4,128)(2,1)S(1)}, bf16[3,2560]{1,0:T(4,128)(2,1)S(1)}, u32[]{:S(2)}, u32[]{:S(2)}) collective-permute-start(bf16[3,2560]{1,0:T(4,128)(2,1)S(1)} %slice.128), channel_id=1, source_target_pairs={{0,4},{4,8},{8,12},{12,16},{16,20},{20,24},{24,28},{28,32},{32,36}... | collective-permute-start | bytes 46088 | tf_op jit(solution)/shard_map/ppermute | solution.py:16
  150.3 4.0 %collective-permute-done = bf16[3,2560]{1,0:T(4,128)(2,1)S(1)} collective-permute-done((bf16[3,2560]{1,0:T(4,128)(2,1)S(1)}, bf16[3,2560]{1,0:T(4,128)(2,1)S(1)}, u32[]{:S(2)}, u32[]{:S(2)}) %collective-permute-start) | collective-permute-done | bytes 15392 | tf_op jit(solution)/shard_map/ppermute | solution.py:16
  154.6 2.4 %copy.130 = bf16[264,2560]{0,1:T(8,128)(2,1)} copy(bf16[264,2560]{1,0:T(8,128)(2,1)S(1)} %maximum_maximum_fusion) | data formatting | bytes 2703360 | tf_op jit(solution)/shard_map/concatenate | solution.py:79
  157.0 2.5 %reshape.497 = bf16[264,4,16,2,20]{0,4,3,2,1:T(8,128)(2,1)S(1)} reshape(bf16[264,2560]{0,1:T(8,128)(2,1)} %copy.130) | data formatting | bytes 2703360 | tf_op jit(solution)/shard_map/reshape | solution.py:72
  159.5 0.6 pad_bitcast_fusion
  160.1 0.4 copy.131
  160.6 6.5 %fusion.68 = f32[264,896]{0,1:T(8,128)S(1)} fusion(bf16[264,4096]{0,1:T(8,128)(2,1)S(1)} %bitcast.144, bf16[4096,896]{1,0:T(8,128)(2,1)} %collective-permute-done.1), kind=kOutput, calls=%fused_computation.141 | convolution fusion | flops 1937768448 | bytes 10448896 | tf_op jit(solution)/shard_map/dot_general | solution.py:84
  167.2 4.0 %select_convert_fusion = (bf16[264,896]{0,1:T(8,128)(2,1)S(1)}, f32[264,896]{0,1:T(8,128)S(1)}) fusion(f32[264,896]{0,1:T(8,128)S(1)} %fusion.68, pred[]{:T(512)S(6)} %eq.85, bf16[264,4096]{0,1:T(8,128)(2,1)S(1)} %bitcast.145, bf16[4096,896]{1,0:T(8,128)(2,1)S(1)} %bitcast.166), kind=kOutput, calls=%fused_computation.2 | convolution fusion | flops 1938004992 | bytes 11868161 | tf_op jit(solution)/shard_map/dot_general | solution.py:83
  171.8 0.7 multiply_bitcast_fusion.1
  172.5 0.6 reduce-window.19
  173.1 0.6 copy.166
  173.9 1.5 multiply_convert_fusion.4
  175.5 0.9 fusion.43
  177.8 0.7 pad_maximum_fusion.1
  178.5 1.9 collective-permute-start.3
  180.4 1.9 collective-permute-start.2
  182.4 2.9 %collective-permute-start.4 = (bf16[10,72,128]{2,1,0:T(8,128)(2,1)}, bf16[10,72,128]{2,1,0:T(8,128)(2,1)}, u32[]{:S(2)}, u32[]{:S(2)}) collective-permute-start(bf16[10,72,128]{2,1,0:T(8,128)(2,1)} %pad_maximum_fusion.1), channel_id=1, source_target_pairs={{0,12},{4,16},{8,20},{12,24},{16,28},{20,32},{24,36},{28,40},{32,4... | collective-permute-start | bytes 552968 | tf_op jit(solution)/shard_map/ppermute | solution.py:16
  185.3 0.7 pad.35
  186.0 0.7 multiply_bitcast_fusion
  186.7 0.9 copy.146
  187.6 4.3 %all-to-all-start.3 = ((bf16[4,64,640]{2,1,0:T(8,128)(2,1)}), bf16[4,64,640]{2,1,0:T(8,128)(2,1)S(1)}, u32[]{:S(2)}, u32[]{:S(2)}) async-start(bf16[4,64,640]{2,1,0:T(8,128)(2,1)} %bitcast.36), calls=%async_computation.3 | async-start | bytes 655360 | tf_op jit(solution)/shard_map/all_to_all | solution.py:95
  191.9 1.9 fusion.7
  193.8 0.9 fusion.51
  194.7 0.9 fusion.52
  195.6 1.1 collective-permute-done.4
  196.7 1.4 fusion.11
  198.4 1.4 copy.144
  199.8 2.0 add_bitcast_fusion
  201.8 4.3 %all-to-all-start.2 = ((bf16[4,64,640]{2,1,0:T(8,128)(2,1)}), bf16[4,64,640]{2,1,0:T(8,128)(2,1)S(1)}, u32[]{:S(2)}, u32[]{:S(2)}) async-start(bf16[4,64,640]{2,1,0:T(8,128)(2,1)} %copy.144), calls=%async_computation.2 | async-start | bytes 655360 | tf_op jit(solution)/shard_map/all_to_all | solution.py:223
  206.7 6.5 %all-to-all-done.2 = bf16[4,64,640]{2,1,0:T(8,128)(2,1)S(1)} async-done(((bf16[4,64,640]{2,1,0:T(8,128)(2,1)}), bf16[4,64,640]{2,1,0:T(8,128)(2,1)S(1)}, u32[]{:S(2)}, u32[]{:S(2)}) %all-to-all-start.2) | async-done | bytes 327712 | tf_op jit(solution)/shard_map/all_to_all | solution.py:223
  214.0 1.0 multiply_convert_fusion.5
  (87 shorter events, 5.2 us)
Async XLA Ops:
  12.6 124.7 %copy-start.5 = (s32[64]{0:T(128)S(1)}, s32[64]{0:T(128)}, u32[]{:S(2)}) copy-start(s32[64]{0:T(128)} %param.23) | copy-start | bytes 772
  12.6 132.9 %copy-start = (f32[4,2816]{1,0:T(4,128)S(1)}, f32[4,2816]{1,0:T(4,128)}, u32[]{:S(2)}) copy-start(f32[4,2816]{1,0:T(4,128)} %param.17) | copy-start | bytes 135172
  12.6 137.6 %slice-start = ((f32[4,2816]{1,0:T(4,128)}), f32[4,256]{1,0:T(4,128)S(1)}, s32[]{:S(2)}) async-start(f32[4,2816]{1,0:T(4,128)} %param.17), calls=%async_computation.5 | async-start | bytes 8192 | tf_op jit(solution)/shard_map/slice | solution.py:101
  14.8 22.7 %all-to-all-start = ((bf16[4,64,2560]{2,1,0:T(8,128)(2,1)}), bf16[4,64,2560]{2,1,0:T(8,128)(2,1)S(1)}, u32[]{:S(2)}, u32[]{:S(2)}) async-start(bf16[4,64,2560]{2,1,0:T(8,128)(2,1)} %broadcast_in_dim.43), calls=%async_computation | async-start | bytes 2621440 | tf_op jit(solution)/shard_map/all_to_all | solution.py:48
  19.2 116.2 %all-gather.2.cloned.1.call-start = ((), (), s32[]{:S(2)}) async-start(), calls=%async_computation.4 | async-start | bytes 7798784 | tf_op jit(solution)/shard_map/all_gather | solution.py:63
  135.4 25.1 %collective-permute-start.1 = (bf16[4096,896]{1,0:T(8,128)(2,1)}, bf16[4096,896]{1,0:T(8,128)(2,1)}, u32[]{:S(2)}, u32[]{:S(2)}) collective-permute-start(bf16[4096,896]{1,0:T(8,128)(2,1)} %all-gather.2.cloned.1.call-done), channel_id=1, source_target_pairs={{0,4},{4,0},{1,5},{5,1},{2,6},{6,2},{3,7},{7,3},{8,12},{12,8},{9,1... | collective-permute-start | bytes 22020104 | tf_op jit(solution)/shard_map/ppermute | solution.py:64
  147.1 7.2 %collective-permute-start = (bf16[3,2560]{1,0:T(4,128)(2,1)S(1)}, bf16[3,2560]{1,0:T(4,128)(2,1)S(1)}, u32[]{:S(2)}, u32[]{:S(2)}) collective-permute-start(bf16[3,2560]{1,0:T(4,128)(2,1)S(1)} %slice.128), channel_id=1, source_target_pairs={{0,4},{4,8},{8,12},{12,16},{16,20},{20,24},{24,28},{28,32},{32,36}... | collective-permute-start | bytes 46088 | tf_op jit(solution)/shard_map/ppermute | solution.py:16
  160.1 7.0 %slice-start.1 = ((s8[7340032]{0:T(1024)(128)(4,1)}), s8[4194304]{0:T(1024)(128)(4,1)S(1)}, s32[]{:S(2)}) async-start(s8[7340032]{0:T(1024)(128)(4,1)} %bitcast.165), calls=%async_computation.6 | async-start | bytes 8388608
  160.6 6.6 %slice-start.2 = ((s8[7340032]{0:T(1024)(128)(4,1)}), s8[3145728]{0:T(1024)(128)(4,1)S(1)}, s32[]{:S(2)}) async-start(s8[7340032]{0:T(1024)(128)(4,1)} %bitcast.165), calls=%async_computation.7 | async-start | bytes 6291456
  171.2 0.7 copy-start.2
  171.2 0.7 copy-start.6
  176.8 0.6 copy-start.3
  178.5 15.3 %collective-permute-start.3 = (bf16[10,72,128]{2,1,0:T(8,128)(2,1)}, bf16[10,72,128]{2,1,0:T(8,128)(2,1)}, u32[]{:S(2)}, u32[]{:S(2)}) collective-permute-start(bf16[10,72,128]{2,1,0:T(8,128)(2,1)} %pad_maximum_fusion.1), channel_id=1, source_target_pairs={{0,8},{4,12},{8,16},{12,20},{16,24},{20,28},{24,32},{28,36},{32,40... | collective-permute-start | bytes 552968 | tf_op jit(solution)/shard_map/ppermute | solution.py:16
  180.4 14.2 %collective-permute-start.2 = (bf16[10,72,128]{2,1,0:T(8,128)(2,1)}, bf16[10,72,128]{2,1,0:T(8,128)(2,1)}, u32[]{:S(2)}, u32[]{:S(2)}) collective-permute-start(bf16[10,72,128]{2,1,0:T(8,128)(2,1)} %pad_maximum_fusion.1), channel_id=1, source_target_pairs={{0,4},{4,8},{8,12},{12,16},{16,20},{20,24},{24,28},{28,32},{32,36}... | collective-permute-start | bytes 552968 | tf_op jit(solution)/shard_map/ppermute | solution.py:16
  182.4 14.3 %collective-permute-start.4 = (bf16[10,72,128]{2,1,0:T(8,128)(2,1)}, bf16[10,72,128]{2,1,0:T(8,128)(2,1)}, u32[]{:S(2)}, u32[]{:S(2)}) collective-permute-start(bf16[10,72,128]{2,1,0:T(8,128)(2,1)} %pad_maximum_fusion.1), channel_id=1, source_target_pairs={{0,12},{4,16},{8,20},{12,24},{16,28},{20,32},{24,36},{28,40},{32,4... | collective-permute-start | bytes 552968 | tf_op jit(solution)/shard_map/ppermute | solution.py:16
  187.6 14.3 %all-to-all-start.3 = ((bf16[4,64,640]{2,1,0:T(8,128)(2,1)}), bf16[4,64,640]{2,1,0:T(8,128)(2,1)S(1)}, u32[]{:S(2)}, u32[]{:S(2)}) async-start(bf16[4,64,640]{2,1,0:T(8,128)(2,1)} %bitcast.36), calls=%async_computation.3 | async-start | bytes 655360 | tf_op jit(solution)/shard_map/all_to_all | solution.py:95
  191.9 1.9 copy-start.4
  191.9 4.8 %copy-start.7 = (f32[10]{0:T(128)S(1)}, f32[10]{0:T(128)}, u32[]{:S(2)}) copy-start(f32[10]{0:T(128)} %param.21) | copy-start | bytes 124
  201.8 11.3 %all-to-all-start.2 = ((bf16[4,64,640]{2,1,0:T(8,128)(2,1)}), bf16[4,64,640]{2,1,0:T(8,128)(2,1)S(1)}, u32[]{:S(2)}, u32[]{:S(2)}) async-start(bf16[4,64,640]{2,1,0:T(8,128)(2,1)} %copy.144), calls=%async_computation.2 | async-start | bytes 655360 | tf_op jit(solution)/shard_map/all_to_all | solution.py:223
  206.6 7.4 %copy-start.1 = (f32[2560]{0:T(1024)S(1)}, f32[2560]{0:T(1024)}, u32[]{:S(2)}) copy-start(f32[2560]{0:T(1024)} %param.22) | copy-start | bytes 30724
Sparse Core Ops, SparseCore 0:
  37.6 97.7 all-gather.1

commit v6 on v4

--- a/solution.py
+++ b/solution.py
@@ -59,12 +59,12 @@
     halves = jnp.stack([merged[:, :half], merged[:, half:]])
     own_half = lax.all_to_all(halves, "c", 0, 0, tiled=True).reshape(2 * padded_rows, half)
     own_half = lax.all_gather(own_half, "x", axis=0, tiled=True)
-    own_half = lax.all_gather(own_half, "z", axis=0, tiled=True)
-    other_half = lax.ppermute(own_half, "c", [(0, 1), (1, 0)])
     x_size = lax.psum(1, "x")
     z_size = lax.psum(1, "z")
     c_size = lax.psum(1, "c")
     core_index = lax.axis_index("c")
+    is_first = core_index == 0
+    swap = [(0, 1), (1, 0)]
 
     def spread_rows(rows):
         count = rows.shape[0]
@@ -73,23 +73,45 @@
         split = jnp.transpose(split, (0, 2, 1, 3, 4))
         return split.reshape(count, x_size * z_size * c_size * padded_rows)
 
-    rim_hidden = from_behind(block_hidden[block_rows - (conv_taps - 1) :], SEQ, 1)
-    rim_count = rim_hidden.shape[0]
-    both_rows = jnp.concatenate(
-        [block_hidden, rim_hidden, jnp.zeros((8 - rim_count, block_hidden.shape[1]), jnp.bfloat16)]
-    )
-    spread = spread_rows(both_rows)
-    with_own = jnp.dot(spread, own_half, preferred_element_type=jnp.float32)
-    with_other = jnp.dot(spread, other_half, preferred_element_type=jnp.float32)
-    first_cols = jnp.where(core_index == 0, with_own, with_other)
-    second_cols = jnp.where(core_index == 0, with_other, with_own)
-    projected = jnp.concatenate([first_cols, second_cols], axis=1)
+    last_rows = block_hidden[block_rows - (conv_taps - 1) :]
+    rim_count = last_rows.shape[0]
+    rim_near = from_behind(last_rows, SEQ, 1)
+    rim_far = from_behind(last_rows, SEQ, 2)
+    partner_block = lax.ppermute(block_hidden, "c", swap)
+    filler = jnp.zeros((8 - rim_count, block_hidden.shape[1]), jnp.bfloat16)
+    chip_rows = jnp.concatenate(
+        [
+            jnp.where(is_first, block_hidden, partner_block),
+            jnp.where(is_first, rim_near, rim_far),
+            filler,
+            jnp.where(is_first, partner_block, block_hidden),
+            jnp.where(is_first, last_rows, rim_near),
+            filler,
+        ]
+    )
+    spread, own_half = lax.optimization_barrier((spread_rows(chip_rows), own_half))
+    own_half = lax.all_gather(own_half, "z", axis=0, tiled=True)
+    core_rows = block_rows + 8
+    results = jnp.dot(spread, own_half, preferred_element_type=jnp.float32)
+    own_rows = lax.dynamic_slice_in_dim(results, core_index * core_rows, core_rows, 0)
+    partner_rows = lax.dynamic_slice_in_dim(results, (1 - core_index) * core_rows, core_rows, 0)
+    sent_narrow, sent_wide = lax.ppermute(
+        (partner_rows.astype(jnp.bfloat16), partner_rows[:, local_width : local_width + 128]),
+        "c",
+        swap,
+    )
+    conv_part = jnp.where(is_first, own_rows.astype(jnp.bfloat16), sent_narrow)
+    gate_part = jnp.where(
+        is_first, sent_narrow[:, :local_width], own_rows[:, :local_width].astype(jnp.bfloat16)
+    )
+    step_part = jnp.where(
+        is_first, sent_wide[:, :step_width], own_rows[:, local_width : local_width + step_width]
+    )
     conv_end = local_width + 2 * state_width
-    prior_rim = projected[block_rows : block_rows + rim_count, :conv_end].astype(jnp.bfloat16)
-    projected = projected[:block_rows]
-    pre_rows = projected[:, :conv_end].astype(jnp.bfloat16)
-    gates_sum = projected[:, conv_end : conv_end + local_width]
-    steps_sum = projected[:, conv_end + local_width : conv_end + local_width + step_width]
+    prior_rim = conv_part[block_rows : block_rows + rim_count]
+    pre_rows = conv_part[:block_rows]
+    gates_sum = gate_part[:block_rows]
+    steps_sum = step_part[:block_rows]
     head_gates = gates_sum.astype(jnp.bfloat16)
     gates_tokens = lax.all_to_all(
         head_gates.reshape(groups, sub_rows, local_width), "head", 0, 2, tiled=True

time: 233 us -> 247 us (1.060)
  local copies, waits for them, and re-layouts: 21.4 us -> 37.3 us
  starting transfers between devices: 24.6 us -> 36.8 us
  blocking collectives: 20.1 us -> 13.9 us
  matrix products: 17 us -> 11.6 us
    all_gather x1, waiting for transfers between devices: 97.3 us -> 86.3 us  [on_device(): own_half = lax.all_gather(own_half, 'z', axis=0, tiled=True)]
    concatenate x4 -> x2, local copies, waits for them, and re-layouts: 4.17 us -> 14.6 us  [on_device(): jnp.concatenate([jnp.where(is_first, block_hidden, partner_block), jnp.wh...]
    all_to_all x1, waiting for transfers between devices: 8.98 us -> 17.8 us  [on_device(): lax.all_to_all(jnp.broadcast_to(hidden[None], (groups,) + hidden.shape),...]
    transpose x2, local copies, waits for them, and re-layouts: 1.03 us -> 5.96 us  [spread_rows(): split = jnp.transpose(split, (0, 2, 1, 3, 4))]
    ppermute x4 -> x5, starting transfers between devices: 10.7 us -> 15 us  [from_behind(): return lax.ppermute(block, axis, route)]
    ppermute x1 -> x3, starting transfers between devices: 1.91 us -> 6.21 us  [the longest x2 4.3 us: on_device(): lax.ppermute((partner_rows.astype(jnp.bfloat16), partner_rows[:, local_wi...]
    all_to_all x1 -> x0, local copies, waits for them, and re-layouts: 3.82 us -> none  [on_device(): lax.all_to_all(jnp.broadcast_to(hidden[None], (groups,) + hidden.shape),...]
    all_to_all x1 -> x0, blocking collectives: 3.82 us -> none  [on_device(): lax.all_to_all(halves, 'c', 0, 0, tiled=True).reshape(2 * padded_rows, half)]
  transfers between devices with their start and end apart: 9 -> 13, of which waited for: 4 -> 5; matrix products, arithmetic and copies ran while one was open for 13% -> 8% of each run, Pallas kernels for 0% -> 0%
where the time goes in v6:
time: 247 us; the launch traced here: 246 us
  waiting for transfers between devices  114 us (46%)
  local copies, waits for them, and re-layouts  37.3 us (15%)
  starting transfers between devices  36.8 us (15%)
  between operations  18.5 us (7%)
  other arithmetic  14.1 us (6%)
  blocking collectives  13.9 us (6%)
  matrix products  11.6 us (5%)
    all_gather x1, waiting for transfers between devices, on_device(): own_half = lax.all_gather(own_half, 'z', axis=0, tiled=True)  86.3 us
    all_to_all x1, waiting for transfers between devices, on_device(): lax.all_to_all(jnp.broadcast_to(hidden[None], (groups,) + hidden.shape),...  17.8 us
    ppermute x5, starting transfers between devices, from_behind(): return lax.ppermute(block, axis, route)  15 us
    concatenate x2, local copies, waits for them, and re-layouts, on_device(): jnp.concatenate([jnp.where(is_first, block_hidden, partner_block), jnp.wh...  14.6 us
    all_gather x1, blocking collectives, on_device(): own_half = lax.all_gather(own_half, 'x', axis=0, tiled=True)  13.9 us
    dot_general x1, matrix products, on_device(): results = jnp.dot(spread, own_half, preferred_element_type=jnp.float32)  8.98 us
    all_to_all x1, waiting for transfers between devices, on_device(): lax.all_to_all(ssm_rows.reshape(groups, sub_rows, local_width), 'head', 0...  6.6 us
    transpose x2, local copies, waits for them, and re-layouts, spread_rows(): split = jnp.transpose(split, (0, 2, 1, 3, 4))  5.96 us
  transfers between devices with their start and end apart: 13, of which 5 were waited for; matrix products, arithmetic and copies ran while one was open for 8% of the time, Pallas kernels for 0%

profile of v6, /device:TPU:6, one launch (start us, length us, event | category | flops | bytes accessed | tf_op | source)
XLA Modules:
  0.0 246.1 jit_solution(14929917803831824667)
XLA Ops:
  7.2 2.2 broadcast_in_dim.43
  9.4 4.5 %all-to-all-start = ((bf16[4,64,2560]{2,1,0:T(8,128)(2,1)}), bf16[4,64,2560]{2,1,0:T(8,128)(2,1)S(1)}, u32[]{:S(2)}, u32[]{:S(2)}) async-start(bf16[4,64,2560]{2,1,0:T(8,128)(2,1)} %broadcast_in_dim.43), calls=%async_computation | async-start | bytes 2621440 | tf_op jit(solution)/shard_map/all_to_all | solution.py:48
  13.9 17.8 %all-to-all-done = bf16[4,64,2560]{2,1,0:T(8,128)(2,1)S(1)} async-done(((bf16[4,64,2560]{2,1,0:T(8,128)(2,1)}), bf16[4,64,2560]{2,1,0:T(8,128)(2,1)S(1)}, u32[]{:S(2)}, u32[]{:S(2)}) %all-to-all-start) | async-done | bytes 1310752 | tf_op jit(solution)/shard_map/all_to_all | solution.py:48
  31.7 1.9 collective-permute-start
  33.7 0.7 pad_maximum_fusion.2
  34.4 3.4 %all-to-all-start.1 = ((bf16[2,32,896]{2,1,0:T(8,128)(2,1)}), bf16[2,32,896]{2,1,0:T(8,128)(2,1)S(1)}, u32[]{:S(2)}, u32[]{:S(2)}) async-start(bf16[2,32,896]{2,1,0:T(8,128)(2,1)} %pad_maximum_fusion.2), calls=%async_computation.1 | async-start | bytes 229376 | tf_op jit(solution)/shard_map/all_to_all | solution.py:60
  37.8 2.4 collective-permute-start.1
  40.2 3.8 %collective-permute-start.2 = (bf16[3,2560]{1,0:T(4,128)(2,1)S(1)}, bf16[3,2560]{1,0:T(4,128)(2,1)S(1)}, u32[]{:S(2)}, u32[]{:S(2)}) collective-permute-start(bf16[3,2560]{1,0:T(4,128)(2,1)S(1)} %slice.172), channel_id=1, source_target_pairs={{0,8},{4,12},{8,16},{12,20},{16,24},{20,28},{24,32},{28,36},{32,40... | collective-permute-start | bytes 46088 | tf_op jit(solution)/shard_map/ppermute | solution.py:16
  44.1 13.9 %all_gather.6 = bf16[256,896]{1,0:T(8,128)(2,1)} all-gather(bf16[64,896]{1,0:T(8,128)(2,1)S(1)} %bitcast.151), channel_id=1, replica_groups=mesh['x'=4,'z'=16,'c'=2,'head'=4] {'x'}, dimensions={0}, use_global_device_ids=true | all-gather | bytes 573440 | tf_op jit(solution)/shard_map/all_gather | solution.py:61
  58.0 2.6 %broadcast_select_fusion = (bf16[256,2560]{1,0:T(8,128)(2,1)S(1)}, bf16[256,2560]{1,0:T(8,128)(2,1)}) fusion(bf16[256,2560]{1,0:T(8,128)(2,1)} %collective-permute-done, pred[]{:T(512)S(6)} %eq.84, bf16[4,64,2560]{2,1,0:T(8,128)(2,1)S(1)} %all-to-all-done), kind=kLoop, calls=%fused_computation.11 | loop fusion | flops 1310720 | bytes 5242881 | tf_op jit(solution)/shard_map/jit(_where)/select_n | solution.py:87
  60.6 11.2 %concatenate.21 = bf16[528,2560]{1,0:T(8,128)(2,1)} concatenate(bf16[256,2560]{1,0:T(8,128)(2,1)} %get-tuple-element.23, bf16[3,2560]{1,0:T(4,128)(2,1)S(1)} %get-tuple-element.31, bf16[5,2560]{1,0:T(8,128)(2,1)S(1)} %broadcast_in_dim.44, bf16[256,2560]{1,0:T(8,128)(2,1)S(1)} %get-tuple-element.22, bf16[3,2560]{1,0:T(4,128)(2,1)S(1)} %get-tuple-element.30, ...), dimensions={0} | concatenate | bytes 5406720 | tf_op jit(solution)/shard_map/concatenate | solution.py:82
  71.8 3.4 %copy.145 = bf16[528,2560]{0,1:T(8,128)(2,1)S(1)} copy(bf16[528,2560]{1,0:T(8,128)(2,1)} %concatenate.21) | data formatting | bytes 5406720 | tf_op jit(solution)/shard_map/concatenate | solution.py:82
  75.2 2.7 %reshape.496 = bf16[528,4,16,2,20]{0,4,3,2,1:T(8,128)(2,1)} reshape(bf16[528,2560]{0,1:T(8,128)(2,1)S(1)} %copy.145) | data formatting | bytes 5406720 | tf_op jit(solution)/shard_map/reshape | solution.py:71
  77.8 3.0 %pad_bitcast_fusion = bf16[528,16,4,2,32]{0,4,3,1,2:T(8,128)(2,1)S(1)} fusion(bf16[528,4,16,2,20]{0,4,3,2,1:T(8,128)(2,1)} %reshape.496), kind=kLoop, calls=%fused_computation | loop fusion | bytes 7028736 | tf_op jit(solution)/shard_map/transpose | solution.py:73
  80.9 2.9 %copy.146 = bf16[528,16,4,2,32]{0,4,3,2,1:T(8,128)(2,1)} copy(bf16[528,16,4,2,32]{0,4,3,1,2:T(8,128)(2,1)S(1)} %pad_bitcast_fusion) | data formatting | bytes 8650752 | tf_op jit(solution)/shard_map/transpose | solution.py:73
  84.9 0.6 slice.192
  85.5 0.6 fusion.67
  87.4 0.7 slice.129
  88.1 0.8 dynamic_slice.12
  88.9 0.6 convert_reduce_fusion.4
  91.4 0.6 select_reduce_fusion
  92.1 1.1 broadcast_compare_fusion
  93.3 0.7 fusion.16
  94.0 86.3 %all-gather.2.cloned.1.call-done = bf16[4096,896]{1,0:T(8,128)(2,1)} async-done(((bf16[256,896]{1,0:T(8,128)(2,1)}), bf16[4096,896]{1,0:T(8,128)(2,1)}) %all-gather.2.cloned.1.call-update) | async-done | bytes 7340048 | tf_op jit(solution)/shard_map/all_gather | solution.py:93
  180.3 9.0 %fusion.68 = f32[528,896]{0,1:T(8,128)S(1)} fusion(bf16[528,4096]{0,1:T(8,128)(2,1)} %bitcast.144, bf16[4096,896]{1,0:T(8,128)(2,1)} %all-gather.2.cloned.1.call-done), kind=kOutput, calls=%fused_computation.145 | convolution fusion | flops 3875536896 | bytes 13557760 | tf_op jit(solution)/shard_map/dot_general | solution.py:95
  189.3 0.8 dynamic-slice
  190.1 1.9 collective-permute-start.4
  193.3 2.4 collective-permute-start.3
  195.7 0.7 slice.188
  196.6 0.6 reduce-window.19
  199.2 0.6 add_negate_fusion
  199.8 0.7 fusion.50
  200.5 1.4 copy.151
  202.4 1.5 multiply_convert_fusion.4
  204.4 1.9 collective-permute-start.6
  206.3 2.0 collective-permute-start.5
  208.2 4.9 %collective-permute-start.7 = (bf16[10,72,128]{2,1,0:T(8,128)(2,1)S(1)}, bf16[10,72,128]{2,1,0:T(8,128)(2,1)S(1)}, u32[]{:S(2)}, u32[]{:S(2)}) collective-permute-start(bf16[10,72,128]{2,1,0:T(8,128)(2,1)S(1)} %pad_maximum_fusion.1), channel_id=1, source_target_pairs={{0,12},{4,16},{8,20},{12,24},{16,28},{20,32},{24,36},{28,40},{32,4... | collective-permute-start | bytes 552968 | tf_op jit(solution)/shard_map/ppermute | solution.py:16
  213.6 0.7 slice-done
  214.3 0.9 copy.163
  215.1 4.3 %all-to-all-start.3 = ((bf16[4,64,640]{2,1,0:T(8,128)(2,1)}), bf16[4,64,640]{2,1,0:T(8,128)(2,1)S(1)}, u32[]{:S(2)}, u32[]{:S(2)}) async-start(bf16[4,64,640]{2,1,0:T(8,128)(2,1)} %bitcast.36), calls=%async_computation.3 | async-start | bytes 655360 | tf_op jit(solution)/shard_map/all_to_all | solution.py:116
  219.4 0.9 fusion.7
  220.7 1.5 collective-permute-done.7
  222.8 1.4 copy.160
  224.2 1.0 add_bitcast_fusion
  225.2 1.6 all-to-all-done.3
  226.8 3.5 %all-to-all-start.2 = ((bf16[4,64,640]{2,1,0:T(8,128)(2,1)}), bf16[4,64,640]{2,1,0:T(8,128)(2,1)S(1)}, u32[]{:S(2)}, u32[]{:S(2)}) async-start(bf16[4,64,640]{2,1,0:T(8,128)(2,1)} %copy.160), calls=%async_computation.2 | async-start | bytes 655360 | tf_op jit(solution)/shard_map/all_to_all | solution.py:244
  230.8 6.6 %all-to-all-done.2 = bf16[4,64,640]{2,1,0:T(8,128)(2,1)S(1)} async-done(((bf16[4,64,640]{2,1,0:T(8,128)(2,1)}), bf16[4,64,640]{2,1,0:T(8,128)(2,1)S(1)}, u32[]{:S(2)}, u32[]{:S(2)}) %all-to-all-start.2) | async-done | bytes 327712 | tf_op jit(solution)/shard_map/all_to_all | solution.py:244
  238.3 1.0 multiply_convert_fusion.5
  (111 shorter events, 7.8 us)
Async XLA Ops:
  7.2 6.7 %copy-start.8 = (bf16[20,10]{0,1:T(8,128)(2,1)S(1)}, bf16[20,10]{0,1:T(8,128)(2,1)}, u32[]{:S(2)}) copy-start(bf16[20,10]{0,1:T(8,128)(2,1)} %param.15) | copy-start | bytes 1204
  7.2 26.5 %copy-start.3 = (bf16[20,640]{1,0:T(8,128)(2,1)S(1)}, bf16[20,640]{1,0:T(8,128)(2,1)}, u32[]{:S(2)}) copy-start(bf16[20,640]{1,0:T(8,128)(2,1)} %param.13) | copy-start | bytes 76804
  7.2 26.5 %copy-start.2 = (bf16[20,640]{1,0:T(8,128)(2,1)S(1)}, bf16[20,640]{1,0:T(8,128)(2,1)}, u32[]{:S(2)}) copy-start(bf16[20,640]{1,0:T(8,128)(2,1)} %param.14) | copy-start | bytes 76804
  7.2 26.5 %copy-start.7 = (bf16[20,256]{1,0:T(8,128)(2,1)S(1)}, bf16[20,256]{1,0:T(8,128)(2,1)}, u32[]{:S(2)}) copy-start(bf16[20,256]{1,0:T(8,128)(2,1)} %param.16) | copy-start | bytes 30724
  9.4 22.4 %all-to-all-start = ((bf16[4,64,2560]{2,1,0:T(8,128)(2,1)}), bf16[4,64,2560]{2,1,0:T(8,128)(2,1)S(1)}, u32[]{:S(2)}, u32[]{:S(2)}) async-start(bf16[4,64,2560]{2,1,0:T(8,128)(2,1)} %broadcast_in_dim.43), calls=%async_computation | async-start | bytes 2621440 | tf_op jit(solution)/shard_map/all_to_all | solution.py:48
  31.7 26.3 %collective-permute-start = (bf16[256,2560]{1,0:T(8,128)(2,1)S(1)}, bf16[256,2560]{1,0:T(8,128)(2,1)}, u32[]{:S(2)}, u32[]{:S(2)}) collective-permute-start(bf16[256,2560]{1,0:T(8,128)(2,1)S(1)} %bitcast.141), channel_id=1, source_target_pairs={{0,4},{4,0},{1,5},{5,1},{2,6},{6,2},{3,7},{7,3},{8,12},{12,8},{9,1... | collective-permute-start | bytes 3932168 | tf_op jit(solution)/shard_map/ppermute | solution.py:80
  34.4 9.7 %all-to-all-start.1 = ((bf16[2,32,896]{2,1,0:T(8,128)(2,1)}), bf16[2,32,896]{2,1,0:T(8,128)(2,1)S(1)}, u32[]{:S(2)}, u32[]{:S(2)}) async-start(bf16[2,32,896]{2,1,0:T(8,128)(2,1)} %pad_maximum_fusion.2), calls=%async_computation.1 | async-start | bytes 229376 | tf_op jit(solution)/shard_map/all_to_all | solution.py:60
  37.8 142.6 %all-gather.2.cloned.1.call-start = ((), (), s32[]{:S(2)}) async-start(), calls=%async_computation.4 | async-start | bytes 7798784 | tf_op jit(solution)/shard_map/all_gather | solution.py:93
  37.8 20.1 %collective-permute-start.1 = (bf16[3,2560]{1,0:T(4,128)(2,1)S(1)}, bf16[3,2560]{1,0:T(4,128)(2,1)S(1)}, u32[]{:S(2)}, u32[]{:S(2)}) collective-permute-start(bf16[3,2560]{1,0:T(4,128)(2,1)S(1)} %slice.172), channel_id=1, source_target_pairs={{0,4},{4,8},{8,12},{12,16},{16,20},{20,24},{24,28},{28,32},{32,36}... | collective-permute-start | bytes 46088 | tf_op jit(solution)/shard_map/ppermute | solution.py:16
  40.2 17.7 %collective-permute-start.2 = (bf16[3,2560]{1,0:T(4,128)(2,1)S(1)}, bf16[3,2560]{1,0:T(4,128)(2,1)S(1)}, u32[]{:S(2)}, u32[]{:S(2)}) collective-permute-start(bf16[3,2560]{1,0:T(4,128)(2,1)S(1)} %slice.172), channel_id=1, source_target_pairs={{0,8},{4,12},{8,16},{12,20},{16,24},{20,28},{24,32},{28,36},{32,40... | collective-permute-start | bytes 46088 | tf_op jit(solution)/shard_map/ppermute | solution.py:16
  80.9 3.0 %copy-start.9 = (s32[64]{0:T(128)S(1)}, s32[64]{0:T(128)}, u32[]{:S(2)}) copy-start(s32[64]{0:T(128)} %param.23) | copy-start | bytes 772
  80.9 11.1 %copy-start.5 = (f32[4,2816]{1,0:T(4,128)S(1)}, f32[4,2816]{1,0:T(4,128)}, u32[]{:S(2)}) copy-start(f32[4,2816]{1,0:T(4,128)} %param.17) | copy-start | bytes 135172
  94.0 98.7 %slice-start.1 = ((f32[4,2816]{1,0:T(4,128)}), f32[4,256]{1,0:T(4,128)S(1)}, s32[]{:S(2)}) async-start(f32[4,2816]{1,0:T(4,128)} %param.17), calls=%async_computation.6 | async-start | bytes 8192 | tf_op jit(solution)/shard_map/slice | solution.py:122
  189.3 7.1 %copy-start.10 = (f32[10]{0:T(128)S(1)}, f32[10]{0:T(128)}, u32[]{:S(2)}) copy-start(f32[10]{0:T(128)} %param.20) | copy-start | bytes 124
  189.3 7.1 %copy-start.11 = (f32[10]{0:T(128)S(1)}, f32[10]{0:T(128)}, u32[]{:S(2)}) copy-start(f32[10]{0:T(128)} %param.19) | copy-start | bytes 124
  190.1 5.6 %collective-permute-start.4 = (f32[264,128]{0,1:T(8,128)}, f32[264,128]{0,1:T(8,128)}, u32[]{:S(2)}, u32[]{:S(2)}) collective-permute-start(f32[264,128]{0,1:T(8,128)} %dynamic-slice), channel_id=1, source_target_pairs={{0,4},{4,0},{1,5},{5,1},{2,6},{6,2},{3,7},{7,3},{8,12},{12,8},{9,1... | collective-permute-start | bytes 405512 | tf_op jit(solution)/shard_map/ppermute | solution.py:98
  193.3 7.2 %collective-permute-start.3 = (bf16[264,896]{1,0:T(8,128)(2,1)S(1)}, bf16[264,896]{1,0:T(8,128)(2,1)}, u32[]{:S(2)}, u32[]{:S(2)}) collective-permute-start(bf16[264,896]{1,0:T(8,128)(2,1)S(1)} %copy.150), channel_id=1, source_target_pairs={{0,4},{4,0},{1,5},{5,1},{2,6},{6,2},{3,7},{7,3},{8,12},{12,8},{9,1... | collective-permute-start | bytes 1419272 | tf_op jit(solution)/shard_map/ppermute | solution.py:98
  201.9 11.3 %copy-start = (bf16[264,896]{0,1:T(8,128)(2,1)}, bf16[264,896]{0,1:T(8,128)(2,1)S(1)}, u32[]{:S(2)}) copy-start(bf16[264,896]{0,1:T(8,128)(2,1)S(1)} %copy.151) | copy-start | bytes 1419268
  202.3 2.0 copy-start.13
  204.4 16.0 %collective-permute-start.6 = (bf16[10,72,128]{2,1,0:T(8,128)(2,1)S(1)}, bf16[10,72,128]{2,1,0:T(8,128)(2,1)S(1)}, u32[]{:S(2)}, u32[]{:S(2)}) collective-permute-start(bf16[10,72,128]{2,1,0:T(8,128)(2,1)S(1)} %pad_maximum_fusion.1), channel_id=1, source_target_pairs={{0,8},{4,12},{8,16},{12,20},{16,24},{20,28},{24,32},{28,36},{32,40... | collective-permute-start | bytes 552968 | tf_op jit(solution)/shard_map/ppermute | solution.py:16
  206.3 14.3 %collective-permute-start.5 = (bf16[10,72,128]{2,1,0:T(8,128)(2,1)S(1)}, bf16[10,72,128]{2,1,0:T(8,128)(2,1)S(1)}, u32[]{:S(2)}, u32[]{:S(2)}) collective-permute-start(bf16[10,72,128]{2,1,0:T(8,128)(2,1)S(1)} %pad_maximum_fusion.1), channel_id=1, source_target_pairs={{0,4},{4,8},{8,12},{12,16},{16,20},{20,24},{24,28},{28,32},{32,36}... | collective-permute-start | bytes 552968 | tf_op jit(solution)/shard_map/ppermute | solution.py:16
  208.2 13.9 %collective-permute-start.7 = (bf16[10,72,128]{2,1,0:T(8,128)(2,1)S(1)}, bf16[10,72,128]{2,1,0:T(8,128)(2,1)S(1)}, u32[]{:S(2)}, u32[]{:S(2)}) collective-permute-start(bf16[10,72,128]{2,1,0:T(8,128)(2,1)S(1)} %pad_maximum_fusion.1), channel_id=1, source_target_pairs={{0,12},{4,16},{8,20},{12,24},{16,28},{20,32},{24,36},{28,40},{32,4... | collective-permute-start | bytes 552968 | tf_op jit(solution)/shard_map/ppermute | solution.py:16
  213.2 1.0 slice-start
  213.2 6.2 %copy-start.1 = (pred[256,256]{1,0:T(8,128)(4,1)S(1)}, pred[256,256]{1,0:T(8,128)(4,1)}, u32[]{:S(2)}) copy-start(pred[256,256]{1,0:T(8,128)(4,1)} %fusion.16) | copy-start | bytes 196612
  213.2 6.2 %copy-start.4 = (f32[10,256]{1,0:T(8,128)S(1)}, f32[10,256]{1,0:T(8,128)}, u32[]{:S(2)}) copy-start(f32[10,256]{1,0:T(8,128)} %add_negate_fusion) | copy-start | bytes 30724
  215.1 11.7 %all-to-all-start.3 = ((bf16[4,64,640]{2,1,0:T(8,128)(2,1)}), bf16[4,64,640]{2,1,0:T(8,128)(2,1)S(1)}, u32[]{:S(2)}, u32[]{:S(2)}) async-start(bf16[4,64,640]{2,1,0:T(8,128)(2,1)} %bitcast.36), calls=%async_computation.3 | async-start | bytes 655360 | tf_op jit(solution)/shard_map/all_to_all | solution.py:116
  219.4 2.8 %copy-start.12 = (f32[10]{0:T(128)S(1)}, f32[10]{0:T(128)}, u32[]{:S(2)}) copy-start(f32[10]{0:T(128)} %param.21) | copy-start | bytes 124
  220.4 3.8 %copy-start.14 = (f32[10]{0:T(128)S(1)}, f32[10]{0:T(128)}, u32[]{:S(2)}) copy-start(f32[10]{0:T(128)} %exponential_multiply_fusion) | copy-start | bytes 124
  226.8 10.6 %all-to-all-start.2 = ((bf16[4,64,640]{2,1,0:T(8,128)(2,1)}), bf16[4,64,640]{2,1,0:T(8,128)(2,1)S(1)}, u32[]{:S(2)}, u32[]{:S(2)}) async-start(bf16[4,64,640]{2,1,0:T(8,128)(2,1)} %copy.160), calls=%async_computation.2 | async-start | bytes 655360 | tf_op jit(solution)/shard_map/all_to_all | solution.py:244
  230.7 7.5 %copy-start.6 = (f32[2560]{0:T(1024)S(1)}, f32[2560]{0:T(1024)}, u32[]{:S(2)}) copy-start(f32[2560]{0:T(1024)} %param.22) | copy-start | bytes 30724
Sparse Core Ops, SparseCore 0:
  84.0 96.2 all-gather.1

commit v7 on v6

--- a/solution.py
+++ b/solution.py
@@ -75,26 +75,16 @@
 
     last_rows = block_hidden[block_rows - (conv_taps - 1) :]
     rim_count = last_rows.shape[0]
-    rim_near = from_behind(last_rows, SEQ, 1)
-    rim_far = from_behind(last_rows, SEQ, 2)
-    partner_block = lax.ppermute(block_hidden, "c", swap)
+    rim_hidden = from_behind(last_rows, SEQ, 1)
     filler = jnp.zeros((8 - rim_count, block_hidden.shape[1]), jnp.bfloat16)
-    chip_rows = jnp.concatenate(
-        [
-            jnp.where(is_first, block_hidden, partner_block),
-            jnp.where(is_first, rim_near, rim_far),
-            filler,
-            jnp.where(is_first, partner_block, block_hidden),
-            jnp.where(is_first, last_rows, rim_near),
-            filler,
-        ]
-    )
-    spread, own_half = lax.optimization_barrier((spread_rows(chip_rows), own_half))
+    own_spread = spread_rows(jnp.concatenate([block_hidden, rim_hidden, filler]))
+    partner_spread = lax.ppermute(own_spread, "c", swap)
+    own_spread, partner_spread, own_half = lax.optimization_barrier(
+        (own_spread, partner_spread, own_half)
+    )
     own_half = lax.all_gather(own_half, "z", axis=0, tiled=True)
-    core_rows = block_rows + 8
-    results = jnp.dot(spread, own_half, preferred_element_type=jnp.float32)
-    own_rows = lax.dynamic_slice_in_dim(results, core_index * core_rows, core_rows, 0)
-    partner_rows = lax.dynamic_slice_in_dim(results, (1 - core_index) * core_rows, core_rows, 0)
+    own_rows = jnp.dot(own_spread, own_half, preferred_element_type=jnp.float32)
+    partner_rows = jnp.dot(partner_spread, own_half, preferred_element_type=jnp.float32)
     sent_narrow, sent_wide = lax.ppermute(
         (partner_rows.astype(jnp.bfloat16), partner_rows[:, local_width : local_width + 128]),
         "c",

time: 247 us -> 243 us (0.984)
  blocking collectives: 13.9 us -> 40.2 us
  waiting for transfers between devices: 114 us -> 96.8 us
  local copies, waits for them, and re-layouts: 37.3 us -> 26.1 us
  starting transfers between devices: 36.8 us -> 26.1 us
  matrix products: 11.6 us -> 20 us
    all_to_all x0 -> x2, blocking collectives: none -> 26.3 us  [the longest x1 22.2 us: on_device(): lax.all_to_all(jnp.broadcast_to(hidden[None], (groups,) + hidden.shape),...]
    all_to_all x2 -> x0, waiting for transfers between devices: 17.8 us -> none  [the longest x1 17.8 us: on_device(): lax.all_to_all(jnp.broadcast_to(hidden[None], (groups,) + hidden.shape),...]
    concatenate x2 -> x4, local copies, waits for them, and re-layouts: 14.6 us -> 4.16 us  [on_device(): jnp.concatenate([block_hidden, rim_hidden, filler])]
    all_to_all x2 -> x0, starting transfers between devices: 7.82 us -> none  [the longest x1 4.46 us: on_device(): lax.all_to_all(jnp.broadcast_to(hidden[None], (groups,) + hidden.shape),...]
    transpose x2, local copies, waits for them, and re-layouts: 5.96 us -> 1.02 us  [spread_rows(): split = jnp.transpose(split, (0, 2, 1, 3, 4))]
    dot_general x1 -> x2, matrix products: 8.98 us -> 13.5 us  [the longest x1 7.24 us: on_device(): jnp.dot(partner_spread, own_half, preferred_element_type=jnp.float32)]
    ppermute x5 -> x4, starting transfers between devices: 15 us -> 10.7 us  [from_behind(): return lax.ppermute(block, axis, route)]
    all_to_all x0 -> x1, local copies, waits for them, and re-layouts: none -> 3.81 us  [on_device(): lax.all_to_all(jnp.broadcast_to(hidden[None], (groups,) + hidden.shape),...]
  transfers between devices with their start and end apart: 13 -> 10, of which waited for: 5 -> 3; matrix products, arithmetic and copies ran while one was open for 8% -> 12% of each run, Pallas kernels for 0% -> 0%
where the time goes in v7:
time: 243 us; the launch traced here: 242 us
  waiting for transfers between devices  96.8 us (40%)
  blocking collectives  40.2 us (17%)
  starting transfers between devices  26.1 us (11%)
  local copies, waits for them, and re-layouts  26.1 us (11%)
  matrix products  20 us (8%)
  between operations  18.5 us (8%)
  other arithmetic  14.2 us (6%)
    all_gather x1, waiting for transfers between devices, on_device(): own_half = lax.all_gather(own_half, 'z', axis=0, tiled=True)  87.7 us
    all_to_all x1, blocking collectives, on_device(): lax.all_to_all(jnp.broadcast_to(hidden[None], (groups,) + hidden.shape),...  22.2 us
    all_gather x1, blocking collectives, on_device(): own_half = lax.all_gather(own_half, 'x', axis=0, tiled=True)  14 us
    ppermute x4, starting transfers between devices, from_behind(): return lax.ppermute(block, axis, route)  10.7 us
    dot_general x1, matrix products, on_device(): jnp.dot(partner_spread, own_half, preferred_element_type=jnp.float32)  7.24 us
    all_to_all x1, waiting for transfers between devices, on_device(): lax.all_to_all(ssm_rows.reshape(groups, sub_rows, local_width), 'head', 0...  6.48 us
    dot_general x1, matrix products, on_device(): own_rows = jnp.dot(own_spread, own_half, preferred_element_type=jnp.float32)  6.31 us
  transfers between devices with their start and end apart: 10, of which 3 were waited for; matrix products, arithmetic and copies ran while one was open for 12% of the time, Pallas kernels for 0%

profile of v7, /device:TPU:6, one launch (start us, length us, event | category | flops | bytes accessed | tf_op | source)
XLA Modules:
  0.0 241.9 jit_solution(8269915789899804241)
XLA Ops:
  7.2 1.1 broadcast_in_dim.43
  8.3 22.2 %all_to_all.28 = bf16[4,64,2560]{2,1,0:T(8,128)(2,1)S(1)} all-to-all(bf16[4,64,2560]{2,1,0:T(8,128)(2,1)S(1)} %broadcast_in_dim.43), channel_id=1, replica_groups=mesh['x'=4,'z'=16,'c'=2,'head'=4] {'head'}, dimensions={0} | all-to-all | bytes 2621440 | tf_op jit(solution)/shard_map/all_to_all | solution.py:48
  30.5 1.9 collective-permute-start
  32.5 3.8 %copy.136 = bf16[4,64,2560]{1,0,2:T(4,128)(2,1)S(1)} copy(bf16[4,64,2560]{2,1,0:T(8,128)(2,1)} %copy-done) | data formatting | bytes 2621440 | tf_op jit(solution)/shard_map/all_to_all | solution.py:48
  36.3 3.0 %concatenate.26 = bf16[256,4,16,2,20]{0,4,3,2,1:T(8,128)(2,1)} reshape(bf16[4,64,2560]{1,0,2:T(4,128)(2,1)S(1)} %copy.136) | data formatting | bytes 2621440 | tf_op jit(solution)/shard_map/concatenate | solution.py:80
  39.3 2.6 %collective-permute-done = bf16[3,2560]{1,0:T(4,128)(2,1)S(1)} collective-permute-done((bf16[3,2560]{1,0:T(4,128)(2,1)S(1)}, bf16[3,2560]{1,0:T(4,128)(2,1)S(1)}, u32[]{:S(2)}, u32[]{:S(2)}) %collective-permute-start) | collective-permute-done | bytes 15392 | tf_op jit(solution)/shard_map/ppermute | solution.py:16
  42.1 0.9 copy.137
  43.0 2.0 maximum_maximum_fusion
  46.1 2.6 %copy.139 = bf16[264,4096]{1,0:T(8,128)(2,1)} copy(bf16[264,4096]{0,1:T(8,128)(2,1)S(1)} %bitcast.134) | data formatting | bytes 4325376 | tf_op jit(solution)/shard_map/reshape | solution.py:74
  48.7 1.9 collective-permute-start.1
  50.8 4.1 %all_to_all.29 = bf16[2,32,896]{2,1,0:T(8,128)(2,1)S(1)} all-to-all(bf16[2,32,896]{2,1,0:T(8,128)(2,1)S(1)} %pad_maximum_fusion.2), channel_id=1, replica_groups=mesh['x'=4,'z'=16,'c'=2,'head'=4] {'c'}, dimensions={0} | all-to-all | bytes 229376 | tf_op jit(solution)/shard_map/all_to_all | solution.py:60
  54.9 14.0 %all_gather.6 = bf16[256,896]{1,0:T(8,128)(2,1)} all-gather(bf16[64,896]{1,0:T(8,128)(2,1)S(1)} %bitcast.145), channel_id=1, replica_groups=mesh['x'=4,'z'=16,'c'=2,'head'=4] {'x'}, dimensions={0}, use_global_device_ids=true | all-gather | bytes 573440 | tf_op jit(solution)/shard_map/all_gather | solution.py:61
  73.5 0.6 convert_reduce_fusion.4
  74.8 0.6 select_reduce_fusion
  75.5 0.6 compare_convert_fusion
  76.1 0.6 compare_convert_fusion.4
  76.8 87.7 %all-gather.2.cloned.1.call-done = bf16[4096,896]{1,0:T(8,128)(2,1)} async-done(((bf16[256,896]{1,0:T(8,128)(2,1)}), bf16[4096,896]{1,0:T(8,128)(2,1)}) %all-gather.2.cloned.1.call-update) | async-done | bytes 7340048 | tf_op jit(solution)/shard_map/all_gather | solution.py:85
  164.5 7.2 %fusion.66 = (bf16[264,896]{1,0:T(8,128)(2,1)}, f32[264,896]{1,0:T(8,128)}) fusion(bf16[264,4096]{1,0:T(8,128)(2,1)} %collective-permute-done.1, bf16[4096,896]{1,0:T(8,128)(2,1)} %all-gather.2.cloned.1.call-done), kind=kOutput, calls=%fused_computation.136 | convolution fusion | flops 1938004992 | bytes 10921984 | tf_op jit(solution)/shard_map/dot_general | solution.py:87
  171.7 1.9 collective-permute-start.2
  173.6 1.1 broadcast_compare_fusion
  174.9 0.9 slice.188
  175.9 2.4 collective-permute-start.3
  178.3 0.7 constant_dynamic-slice_fusion
  179.0 0.7 slice.129
  179.7 0.8 dynamic_slice.6
  181.2 0.7 slice.189
  181.9 6.3 %broadcast_select_fusion = (bf16[264,896]{1,0:T(8,128)(2,1)S(1)}, bf16[264,896]{1,0:T(8,128)(2,1)}, f32[264,896]{1,0:T(8,128)S(1)}) fusion(bf16[264,896]{1,0:T(8,128)(2,1)} %collective-permute-done.2, pred[]{:T(512)S(6)} %eq.84, bf16[264,4096]{0,1:T(8,128)(2,1)S(1)} %bitcast.135, bf16[4096,896]{1,0:T(8,128)(2,1)} %all-gather.2.cloned.1.call-done), kind=kOutput, calls=%fused_computation.26 | convolution fusion | flops 1938241536 | bytes 11868161 | tf_op jit(solution)/shard_map/dot_general | solution.py:86
  189.3 0.8 multiply_convert_fusion.4
  190.2 0.9 fusion.41
  193.1 0.9 multiply_convert_fusion.5
  194.0 1.1 copy.151
  195.5 0.7 pad_maximum_fusion.1
  196.2 1.9 collective-permute-start.5
  198.1 1.9 collective-permute-start.4
  200.1 4.9 %collective-permute-start.6 = (bf16[10,72,128]{2,1,0:T(8,128)(2,1)}, bf16[10,72,128]{2,1,0:T(8,128)(2,1)}, u32[]{:S(2)}, u32[]{:S(2)}) collective-permute-start(bf16[10,72,128]{2,1,0:T(8,128)(2,1)} %pad_maximum_fusion.1), channel_id=1, source_target_pairs={{0,12},{4,16},{8,20},{12,24},{16,28},{20,32},{24,36},{28,40},{32,4... | collective-permute-start | bytes 552968 | tf_op jit(solution)/shard_map/ppermute | solution.py:16
  205.0 0.9 copy.142
  206.0 1.0 slice.204
  207.0 0.8 slice_select_fusion
  207.8 4.3 %all-to-all-start.3 = ((bf16[4,64,640]{2,1,0:T(8,128)(2,1)}), bf16[4,64,640]{2,1,0:T(8,128)(2,1)S(1)}, u32[]{:S(2)}, u32[]{:S(2)}) async-start(bf16[4,64,640]{2,1,0:T(8,128)(2,1)} %bitcast.36), calls=%async_computation.3 | async-start | bytes 655360 | tf_op jit(solution)/shard_map/all_to_all | solution.py:106
  212.1 1.9 fusion.7
  214.5 0.9 fusion.50
  215.4 0.9 fusion.51
  216.3 1.4 fusion.11
  218.0 1.4 copy.153
  219.3 2.0 add_bitcast_fusion
  221.4 4.8 %all-to-all-start.2 = ((bf16[4,64,640]{2,1,0:T(8,128)(2,1)}), bf16[4,64,640]{2,1,0:T(8,128)(2,1)S(1)}, u32[]{:S(2)}, u32[]{:S(2)}) async-start(bf16[4,64,640]{2,1,0:T(8,128)(2,1)} %copy.153), calls=%async_computation.2 | async-start | bytes 655360 | tf_op jit(solution)/shard_map/all_to_all | solution.py:234
  226.7 6.5 %all-to-all-done.2 = bf16[4,64,640]{2,1,0:T(8,128)(2,1)S(1)} async-done(((bf16[4,64,640]{2,1,0:T(8,128)(2,1)}), bf16[4,64,640]{2,1,0:T(8,128)(2,1)S(1)}, u32[]{:S(2)}, u32[]{:S(2)}) %all-to-all-start.2) | async-done | bytes 327712 | tf_op jit(solution)/shard_map/all_to_all | solution.py:234
  234.1 1.0 multiply_convert_fusion.6
  (131 shorter events, 9.5 us)
Async XLA Ops:
  7.2 157.3 %all-gather.2.cloned.1.call-start = ((), (), s32[]{:S(2)}) async-start(), calls=%async_computation.4 | async-start | bytes 7798784 | tf_op jit(solution)/shard_map/all_gather | solution.py:85
  30.4 2.0 copy-start
  30.5 11.4 %collective-permute-start = (bf16[3,2560]{1,0:T(4,128)(2,1)S(1)}, bf16[3,2560]{1,0:T(4,128)(2,1)S(1)}, u32[]{:S(2)}, u32[]{:S(2)}) collective-permute-start(bf16[3,2560]{1,0:T(4,128)(2,1)S(1)} %slice.172), channel_id=1, source_target_pairs={{0,4},{4,8},{8,12},{12,16},{16,20},{20,24},{24,28},{28,32},{32,36}... | collective-permute-start | bytes 46088 | tf_op jit(solution)/shard_map/ppermute | solution.py:16
  46.0 4.6 %copy-start.10 = (bf16[20,10]{0,1:T(8,128)(2,1)S(1)}, bf16[20,10]{0,1:T(8,128)(2,1)}, u32[]{:S(2)}) copy-start(bf16[20,10]{0,1:T(8,128)(2,1)} %param.15) | copy-start | bytes 1204
  46.0 4.7 %copy-start.4 = (bf16[20,640]{1,0:T(8,128)(2,1)S(1)}, bf16[20,640]{1,0:T(8,128)(2,1)}, u32[]{:S(2)}) copy-start(bf16[20,640]{1,0:T(8,128)(2,1)} %param.14) | copy-start | bytes 76804
  46.0 4.7 %copy-start.5 = (bf16[20,640]{1,0:T(8,128)(2,1)S(1)}, bf16[20,640]{1,0:T(8,128)(2,1)}, u32[]{:S(2)}) copy-start(bf16[20,640]{1,0:T(8,128)(2,1)} %param.13) | copy-start | bytes 76804
  46.0 4.7 %copy-start.7 = (bf16[20,256]{1,0:T(8,128)(2,1)S(1)}, bf16[20,256]{1,0:T(8,128)(2,1)}, u32[]{:S(2)}) copy-start(bf16[20,256]{1,0:T(8,128)(2,1)} %param.16) | copy-start | bytes 30724
  46.0 22.9 %copy-start.18 = (s32[64]{0:T(128)S(1)}, s32[64]{0:T(128)}, u32[]{:S(2)}) copy-start(s32[64]{0:T(128)} %param.23) | copy-start | bytes 772
  48.7 20.2 %collective-permute-start.1 = (bf16[264,4096]{1,0:T(8,128)(2,1)}, bf16[264,4096]{1,0:T(8,128)(2,1)}, u32[]{:S(2)}, u32[]{:S(2)}) collective-permute-start(bf16[264,4096]{1,0:T(8,128)(2,1)} %copy.139), channel_id=1, source_target_pairs={{0,4},{4,0},{1,5},{5,1},{2,6},{6,2},{3,7},{7,3},{8,12},{12,8},{9,1... | collective-permute-start | bytes 6488072 | tf_op jit(solution)/shard_map/ppermute | solution.py:81
  76.8 104.3 %slice-start = ((f32[4,2816]{1,0:T(4,128)}), f32[4,256]{1,0:T(4,128)S(1)}, s32[]{:S(2)}) async-start(f32[4,2816]{1,0:T(4,128)} %param.17), calls=%async_computation.5 | async-start | bytes 8192 | tf_op jit(solution)/shard_map/slice | solution.py:112
  171.7 10.2 %collective-permute-start.2 = (bf16[264,896]{1,0:T(8,128)(2,1)}, bf16[264,896]{1,0:T(8,128)(2,1)}, u32[]{:S(2)}, u32[]{:S(2)}) collective-permute-start(bf16[264,896]{1,0:T(8,128)(2,1)} %get-tuple-element.38), channel_id=1, source_target_pairs={{0,4},{4,0},{1,5},{5,1},{2,6},{6,2},{3,7},{7,3},{8,12},{12,8},{9,1... | collective-permute-start | bytes 1419272 | tf_op jit(solution)/shard_map/ppermute | solution.py:88
  175.9 5.2 %collective-permute-start.3 = (f32[264,128]{0,1:T(8,128)S(1)}, f32[264,128]{0,1:T(8,128)}, u32[]{:S(2)}, u32[]{:S(2)}) collective-permute-start(f32[264,128]{0,1:T(8,128)S(1)} %copy.158), channel_id=1, source_target_pairs={{0,4},{4,0},{1,5},{5,1},{2,6},{6,2},{3,7},{7,3},{8,12},{12,8},{9,1... | collective-permute-start | bytes 405512 | tf_op jit(solution)/shard_map/ppermute | solution.py:88
  181.9 6.5 %copy-start.19 = (f32[10]{0:T(128)S(1)}, f32[10]{0:T(128)}, u32[]{:S(2)}) copy-start(f32[10]{0:T(128)} %param.20) | copy-start | bytes 124
  181.9 6.5 %copy-start.20 = (f32[10]{0:T(128)S(1)}, f32[10]{0:T(128)}, u32[]{:S(2)}) copy-start(f32[10]{0:T(128)} %param.19) | copy-start | bytes 124
  181.9 7.4 %copy-start.11 = (f32[256]{0:T(256)S(1)}, f32[256]{0:T(256)}, u32[]{:S(2)}) copy-start(f32[256]{0:T(256)} %get-tuple-element.30) | copy-start | bytes 3076
  181.9 7.4 %copy-start.12 = (f32[256]{0:T(256)S(1)}, f32[256]{0:T(256)}, u32[]{:S(2)}) copy-start(f32[256]{0:T(256)} %get-tuple-element.31) | copy-start | bytes 3076
  181.9 7.4 %copy-start.13 = (f32[256]{0:T(256)S(1)}, f32[256]{0:T(256)}, u32[]{:S(2)}) copy-start(f32[256]{0:T(256)} %get-tuple-element.32) | copy-start | bytes 3076
  188.2 3.1 %copy-start.9 = (f32[2,128]{1,0:T(2,128)S(1)}, f32[2,128]{1,0:T(2,128)}, u32[]{:S(2)}) copy-start(f32[2,128]{1,0:T(2,128)} %compare_convert_fusion) | copy-start | bytes 3076
  188.2 3.3 %copy-start.15 = (pred[256]{0:T(512)(128)(4,1)S(1)}, pred[256]{0:T(512)(128)(4,1)}, u32[]{:S(2)}) copy-start(pred[256]{0:T(512)(128)(4,1)} %get-tuple-element.35) | copy-start | bytes 772
  188.3 4.4 %copy-start.14 = (pred[256]{0:T(512)(128)(4,1)S(1)}, pred[256]{0:T(512)(128)(4,1)}, u32[]{:S(2)}) copy-start(pred[256]{0:T(512)(128)(4,1)} %get-tuple-element.33) | copy-start | bytes 772
  191.5 1.1 copy-start.16
  192.8 2.6 %copy-start.22 = (bf16[10]{0:T(256)(128)(2,1)S(1)}, bf16[10]{0:T(256)(128)(2,1)}, u32[]{:S(2)}) copy-start(bf16[10]{0:T(256)(128)(2,1)} %multiply_convert_fusion.8) | copy-start | bytes 64
  193.1 12.9 %copy-start.8 = (f32[256]{0:T(256)S(1)}, f32[256]{0:T(256)}, u32[]{:S(2)}) copy-start(f32[256]{0:T(256)} %get-tuple-element.34) | copy-start | bytes 3076
  193.1 12.9 %copy-start.1 = (bf16[264,896]{1,0:T(8,128)(2,1)S(1)}, bf16[264,896]{1,0:T(8,128)(2,1)}, u32[]{:S(2)}) copy-start(bf16[264,896]{1,0:T(8,128)(2,1)} %get-tuple-element.23) | copy-start | bytes 1419268
  196.2 18.3 %collective-permute-start.5 = (bf16[10,72,128]{2,1,0:T(8,128)(2,1)}, bf16[10,72,128]{2,1,0:T(8,128)(2,1)}, u32[]{:S(2)}, u32[]{:S(2)}) collective-permute-start(bf16[10,72,128]{2,1,0:T(8,128)(2,1)} %pad_maximum_fusion.1), channel_id=1, source_target_pairs={{0,8},{4,12},{8,16},{12,20},{16,24},{20,28},{24,32},{28,36},{32,40... | collective-permute-start | bytes 552968 | tf_op jit(solution)/shard_map/ppermute | solution.py:16
  198.1 17.3 %collective-permute-start.4 = (bf16[10,72,128]{2,1,0:T(8,128)(2,1)}, bf16[10,72,128]{2,1,0:T(8,128)(2,1)}, u32[]{:S(2)}, u32[]{:S(2)}) collective-permute-start(bf16[10,72,128]{2,1,0:T(8,128)(2,1)} %pad_maximum_fusion.1), channel_id=1, source_target_pairs={{0,4},{4,8},{8,12},{12,16},{16,20},{20,24},{24,28},{28,32},{32,36}... | collective-permute-start | bytes 552968 | tf_op jit(solution)/shard_map/ppermute | solution.py:16
  200.1 16.2 %collective-permute-start.6 = (bf16[10,72,128]{2,1,0:T(8,128)(2,1)}, bf16[10,72,128]{2,1,0:T(8,128)(2,1)}, u32[]{:S(2)}, u32[]{:S(2)}) collective-permute-start(bf16[10,72,128]{2,1,0:T(8,128)(2,1)} %pad_maximum_fusion.1), channel_id=1, source_target_pairs={{0,12},{4,16},{8,20},{12,24},{16,28},{20,32},{24,36},{28,40},{32,4... | collective-permute-start | bytes 552968 | tf_op jit(solution)/shard_map/ppermute | solution.py:16
  205.9 6.2 %copy-start.3 = (bf16[256,640]{0,1:T(8,128)(2,1)S(1)}, bf16[256,640]{0,1:T(8,128)(2,1)}, u32[]{:S(2)}) copy-start(bf16[256,640]{0,1:T(8,128)(2,1)} %copy.142) | copy-start | bytes 983044
  207.8 13.6 %all-to-all-start.3 = ((bf16[4,64,640]{2,1,0:T(8,128)(2,1)}), bf16[4,64,640]{2,1,0:T(8,128)(2,1)S(1)}, u32[]{:S(2)}, u32[]{:S(2)}) async-start(bf16[4,64,640]{2,1,0:T(8,128)(2,1)} %bitcast.36), calls=%async_computation.3 | async-start | bytes 655360 | tf_op jit(solution)/shard_map/all_to_all | solution.py:106
  212.1 2.0 copy-start.17
  212.1 2.2 copy-start.2
  212.1 4.2 %copy-start.21 = (f32[10]{0:T(128)S(1)}, f32[10]{0:T(128)}, u32[]{:S(2)}) copy-start(f32[10]{0:T(128)} %param.21) | copy-start | bytes 124
  221.4 11.8 %all-to-all-start.2 = ((bf16[4,64,640]{2,1,0:T(8,128)(2,1)}), bf16[4,64,640]{2,1,0:T(8,128)(2,1)S(1)}, u32[]{:S(2)}, u32[]{:S(2)}) async-start(bf16[4,64,640]{2,1,0:T(8,128)(2,1)} %copy.153), calls=%async_computation.2 | async-start | bytes 655360 | tf_op jit(solution)/shard_map/all_to_all | solution.py:234
  226.7 7.4 %copy-start.6 = (f32[2560]{0:T(1024)S(1)}, f32[2560]{0:T(1024)}, u32[]{:S(2)}) copy-start(f32[2560]{0:T(1024)} %param.22) | copy-start | bytes 30724
Sparse Core Ops, SparseCore 0:
  69.0 95.3 all-gather.1

commit v8 on v4

--- a/solution.py
+++ b/solution.py
@@ -59,6 +59,19 @@
     halves = jnp.stack([merged[:, :half], merged[:, half:]])
     own_half = lax.all_to_all(halves, "c", 0, 0, tiled=True).reshape(2 * padded_rows, half)
     own_half = lax.all_gather(own_half, "x", axis=0, tiled=True)
+    early_start = block_index * block_rows
+    ext_positions = (
+        early_start - (conv_taps - 1) + jnp.arange(block_rows + conv_taps - 1, dtype=jnp.int32)
+    )
+    positions = early_start + jnp.arange(block_rows, dtype=jnp.int32)
+    early_ids = (
+        segments_at(ext_positions, prompt_ends),
+        segments_at(positions, prompt_ends),
+        segments_at(positions + 1, prompt_ends),
+        segments_at(positions - 1, prompt_ends),
+    )
+    block_hidden, own_half, early_ids = lax.optimization_barrier((block_hidden, own_half, early_ids))
+    ext_ids, segment_ids, next_ids, before_ids = early_ids
     own_half = lax.all_gather(own_half, "z", axis=0, tiled=True)
     other_half = lax.ppermute(own_half, "c", [(0, 1), (1, 0)])
     x_size = lax.psum(1, "x")
@@ -110,10 +123,6 @@
     )
     block_start = block_index * block_rows
     extended = jnp.concatenate([prior_rim, pre_rows], axis=0)
-    ext_positions = (
-        block_start - (conv_taps - 1) + jnp.arange(block_rows + conv_taps - 1, dtype=jnp.int32)
-    )
-    ext_ids = segments_at(ext_positions, prompt_ends)
     own_ids = ext_ids[conv_taps - 1 :]
     filtered = jnp.zeros(pre_rows.shape, jnp.float32) + local_bias[None, :]
     for offset in range(conv_taps):
@@ -129,10 +138,6 @@
     both_states = conv_out[:, local_width:]
     stretch_rows = STRETCH
     stretches = block_rows // stretch_rows
-    positions = block_start + jnp.arange(block_rows, dtype=jnp.int32)
-    segment_ids = segments_at(positions, prompt_ends)
-    next_ids = segments_at(positions + 1, prompt_ends)
-    before_ids = segments_at(positions - 1, prompt_ends)
     stretch_ids = segment_ids.reshape(stretches, stretch_rows)
     prior_ids = before_ids.reshape(stretches, stretch_rows)[:, 0]
     ends_mask = (segment_ids != next_ids).reshape(stretches, stretch_rows)

time: 233 us -> 221 us (0.948)
  waiting for transfers between devices: 115 us -> 108 us
  starting transfers between devices: 24.6 us -> 30 us
  blocking collectives: 20.1 us -> 15.2 us
  local copies, waits for them, and re-layouts: 21.4 us -> 17.1 us
    all_to_all x1, waiting for transfers between devices: 8.98 us -> 2.85 us  [on_device(): lax.all_to_all(jnp.broadcast_to(hidden[None], (groups,) + hidden.shape),...]
    all_to_all x1 -> x0, local copies, waits for them, and re-layouts: 3.82 us -> none  [on_device(): lax.all_to_all(jnp.broadcast_to(hidden[None], (groups,) + hidden.shape),...]
    all_to_all x1 -> x0, blocking collectives: 3.82 us -> none  [on_device(): lax.all_to_all(halves, 'c', 0, 0, tiled=True).reshape(2 * padded_rows, half)]
    all_to_all x0 -> x1, starting transfers between devices: none -> 3.36 us  [on_device(): lax.all_to_all(halves, 'c', 0, 0, tiled=True).reshape(2 * padded_rows, half)]
    reshape x0 -> x1, local copies, waits for them, and re-layouts: none -> 2.51 us  [spread_rows(): split = rows.reshape(count, x_size, z_size, c_size, shard_rows)]
  transfers between devices with their start and end apart: 9 -> 10, of which waited for: 4 -> 4; matrix products, arithmetic and copies ran while one was open for 13% -> 12% of each run, Pallas kernels for 0% -> 0%
where the time goes in v8:
time: 221 us; the launch traced here: 220 us
  waiting for transfers between devices  108 us (49%)
  starting transfers between devices  30 us (14%)
  between operations  17.8 us (8%)
  local copies, waits for them, and re-layouts  17.1 us (8%)
  matrix products  17 us (8%)
  blocking collectives  15.2 us (7%)
  other arithmetic  14.2 us (6%)
    all_gather x1, waiting for transfers between devices, on_device(): own_half = lax.all_gather(own_half, 'z', axis=0, tiled=True)  97.9 us
    all_gather x1, blocking collectives, on_device(): own_half = lax.all_gather(own_half, 'x', axis=0, tiled=True)  15.2 us
    ppermute x4, starting transfers between devices, from_behind(): return lax.ppermute(block, axis, route)  11.2 us
    all_to_all x1, waiting for transfers between devices, on_device(): lax.all_to_all(ssm_rows.reshape(groups, sub_rows, local_width), 'head', 0...  7.16 us
    dot_general x1, matrix products, on_device(): with_other = jnp.dot(spread, other_half, preferred_element_type=jnp.float32)  6.52 us
    all_to_all x1, starting transfers between devices, on_device(): lax.all_to_all(ssm_rows.reshape(groups, sub_rows, local_width), 'head', 0...  4.79 us
    all_to_all x1, starting transfers between devices, on_device(): lax.all_to_all(jnp.broadcast_to(hidden[None], (groups,) + hidden.shape),...  4.46 us
  transfers between devices with their start and end apart: 10, of which 4 were waited for; matrix products, arithmetic and copies ran while one was open for 12% of the time, Pallas kernels for 0%

profile of v8, /device:TPU:6, one launch (start us, length us, event | category | flops | bytes accessed | tf_op | source)
XLA Modules:
  0.0 219.7 jit_solution(13898539905793476150)
XLA Ops:
  7.2 0.8 copy.129
  8.0 0.8 fusion.32
  8.8 0.7 pad_maximum_fusion.2
  9.4 3.4 %all-to-all-start.1 = ((bf16[2,32,896]{2,1,0:T(8,128)(2,1)}), bf16[2,32,896]{2,1,0:T(8,128)(2,1)S(1)}, u32[]{:S(2)}, u32[]{:S(2)}) async-start(bf16[2,32,896]{2,1,0:T(8,128)(2,1)} %pad_maximum_fusion.2), calls=%async_computation.1 | async-start | bytes 229376 | tf_op jit(solution)/shard_map/all_to_all | solution.py:60
  12.8 0.7 copy.130
  14.2 2.1 broadcast_in_dim.39
  16.4 4.5 %all-to-all-start = ((bf16[4,64,2560]{2,1,0:T(8,128)(2,1)}), bf16[4,64,2560]{2,1,0:T(8,128)(2,1)S(1)}, u32[]{:S(2)}, u32[]{:S(2)}) async-start(bf16[4,64,2560]{2,1,0:T(8,128)(2,1)} %broadcast_in_dim.39), calls=%async_computation | async-start | bytes 2621440 | tf_op jit(solution)/shard_map/all_to_all | solution.py:48
  21.0 15.2 %all_gather.6 = bf16[256,896]{1,0:T(8,128)(2,1)} all-gather(bf16[64,896]{1,0:T(8,128)(2,1)S(1)} %bitcast.148), channel_id=1, replica_groups=mesh['x'=4,'z'=16,'c'=2,'head'=4] {'x'}, dimensions={0}, use_global_device_ids=true | all-gather | bytes 573440 | tf_op jit(solution)/shard_map/all_gather | solution.py:61
  36.2 2.8 %all-to-all-done = bf16[4,64,2560]{2,1,0:T(8,128)(2,1)S(1)} async-done(((bf16[4,64,2560]{2,1,0:T(8,128)(2,1)}), bf16[4,64,2560]{2,1,0:T(8,128)(2,1)S(1)}, u32[]{:S(2)}, u32[]{:S(2)}) %all-to-all-start) | async-done | bytes 1310752 | tf_op jit(solution)/shard_map/all_to_all | solution.py:48
  39.1 97.9 %all-gather.2.cloned.1.call-done = bf16[4096,896]{1,0:T(8,128)(2,1)} async-done(((bf16[256,896]{1,0:T(8,128)(2,1)}), bf16[4096,896]{1,0:T(8,128)(2,1)}) %all-gather.2.cloned.1.call-update) | async-done | bytes 7340048 | tf_op jit(solution)/shard_map/all_gather | solution.py:75
  137.0 1.9 collective-permute-start.1
  139.0 0.7 slice.123
  139.7 0.8 dynamic_slice.6
  140.6 2.4 %collective-permute-start = (bf16[3,2560]{1,0:T(4,128)(2,1)S(1)}, bf16[3,2560]{1,0:T(4,128)(2,1)S(1)}, u32[]{:S(2)}, u32[]{:S(2)}) collective-permute-start(bf16[3,2560]{1,0:T(4,128)(2,1)S(1)} %slice.128), channel_id=1, source_target_pairs={{0,4},{4,8},{8,12},{12,16},{16,20},{20,24},{24,28},{28,32},{32,36}... | collective-permute-start | bytes 46088 | tf_op jit(solution)/shard_map/ppermute | solution.py:16
  143.0 0.6 slice.180
  143.6 0.6 slice.178
  144.2 0.6 convert_reduce_fusion.4
  145.4 0.6 select_reduce_fusion
  146.1 2.5 %broadcast_compare_fusion = (pred[256]{0:T(512)(128)(4,1)S(1)}, f32[256]{0:T(256)}, pred[256]{0:T(512)(128)(4,1)S(1)}) fusion(s32[256]{0:T(256)S(1)} %compare_select_fusion.3, s32[]{:T(128)} %bitcast.18, s32[]{:T(128)} %bitcast.29, pred[]{:T(512)} %gt.8, s32[]{:T(128)} %select_reduce_fusion), kind=kLoop, calls=%fused_computation.132 | loop fusion | flops 1280 | bytes 2573 | tf_op jit(solution)/shard_map/eq | solution.py:169
  151.6 2.4 %copy.131 = bf16[264,2560]{0,1:T(8,128)(2,1)} copy(bf16[264,2560]{1,0:T(8,128)(2,1)S(1)} %maximum_maximum_fusion) | data formatting | bytes 2703360 | tf_op jit(solution)/shard_map/concatenate | solution.py:91
  154.1 2.5 %reshape.411 = bf16[264,4,16,2,20]{0,4,3,2,1:T(8,128)(2,1)S(1)} reshape(bf16[264,2560]{0,1:T(8,128)(2,1)} %copy.131) | data formatting | bytes 2703360 | tf_op jit(solution)/shard_map/reshape | solution.py:84
  156.6 0.6 pad_bitcast_fusion
  157.2 0.4 copy.132
  157.7 6.5 %fusion.65 = f32[264,896]{0,1:T(8,128)S(1)} fusion(bf16[264,4096]{0,1:T(8,128)(2,1)S(1)} %bitcast.140, bf16[4096,896]{1,0:T(8,128)(2,1)} %collective-permute-done.1), kind=kOutput, calls=%fused_computation.137 | convolution fusion | flops 1937768448 | bytes 10448896 | tf_op jit(solution)/shard_map/dot_general | solution.py:96
  164.2 4.0 %select_convert_fusion = (bf16[264,896]{0,1:T(8,128)(2,1)S(1)}, f32[264,896]{0,1:T(8,128)S(1)}) fusion(f32[264,896]{0,1:T(8,128)S(1)} %fusion.65, pred[]{:T(512)S(6)} %eq.70, bf16[264,4096]{0,1:T(8,128)(2,1)S(1)} %bitcast.141, bf16[4096,896]{1,0:T(8,128)(2,1)S(1)} %bitcast.162), kind=kOutput, calls=%fused_computation.2 | convolution fusion | flops 1938004992 | bytes 11868161 | tf_op jit(solution)/shard_map/dot_general | solution.py:95
  168.4 0.5 copy-done.2
  168.9 0.7 multiply_bitcast_fusion.1
  169.6 0.6 reduce-window.19
  171.2 1.5 multiply_convert_fusion.4
  173.2 0.7 pad_maximum_fusion.1
  173.9 1.9 collective-permute-start.3
  175.8 2.6 %collective-permute-start.2 = (bf16[10,72,128]{2,1,0:T(8,128)(2,1)}, bf16[10,72,128]{2,1,0:T(8,128)(2,1)}, u32[]{:S(2)}, u32[]{:S(2)}) collective-permute-start(bf16[10,72,128]{2,1,0:T(8,128)(2,1)} %pad_maximum_fusion.1), channel_id=1, source_target_pairs={{0,4},{4,8},{8,12},{12,16},{16,20},{20,24},{24,28},{28,32},{32,36}... | collective-permute-start | bytes 552968 | tf_op jit(solution)/shard_map/ppermute | solution.py:16
  178.4 4.3 %collective-permute-start.4 = (bf16[10,72,128]{2,1,0:T(8,128)(2,1)}, bf16[10,72,128]{2,1,0:T(8,128)(2,1)}, u32[]{:S(2)}, u32[]{:S(2)}) collective-permute-start(bf16[10,72,128]{2,1,0:T(8,128)(2,1)} %pad_maximum_fusion.1), channel_id=1, source_target_pairs={{0,12},{4,16},{8,20},{12,24},{16,28},{20,32},{24,36},{28,40},{32,4... | collective-permute-start | bytes 552968 | tf_op jit(solution)/shard_map/ppermute | solution.py:16
  182.8 0.9 fusion.43
  183.8 0.7 exponential_multiply_fusion
  184.5 0.9 copy.146
  185.4 4.3 %all-to-all-start.3 = ((bf16[4,64,640]{2,1,0:T(8,128)(2,1)}), bf16[4,64,640]{2,1,0:T(8,128)(2,1)S(1)}, u32[]{:S(2)}, u32[]{:S(2)}) async-start(bf16[4,64,640]{2,1,0:T(8,128)(2,1)} %bitcast.36), calls=%async_computation.3 | async-start | bytes 655360 | tf_op jit(solution)/shard_map/all_to_all | solution.py:107
  189.7 1.9 fusion.7
  191.6 0.9 fusion.51
  192.5 0.9 fusion.52
  193.4 1.4 fusion.11
  195.1 1.4 copy.144
  196.5 2.0 add_bitcast_fusion
  198.5 4.8 %all-to-all-start.2 = ((bf16[4,64,640]{2,1,0:T(8,128)(2,1)}), bf16[4,64,640]{2,1,0:T(8,128)(2,1)S(1)}, u32[]{:S(2)}, u32[]{:S(2)}) async-start(bf16[4,64,640]{2,1,0:T(8,128)(2,1)} %copy.144), calls=%async_computation.2 | async-start | bytes 655360 | tf_op jit(solution)/shard_map/all_to_all | solution.py:227
  203.4 0.4 copy.147
  203.8 7.2 %all-to-all-done.2 = bf16[4,64,640]{2,1,0:T(8,128)(2,1)S(1)} async-done(((bf16[4,64,640]{2,1,0:T(8,128)(2,1)}), bf16[4,64,640]{2,1,0:T(8,128)(2,1)S(1)}, u32[]{:S(2)}, u32[]{:S(2)}) %all-to-all-start.2) | async-done | bytes 327712 | tf_op jit(solution)/shard_map/all_to_all | solution.py:227
  211.4 0.4 copy.145
  211.9 1.0 multiply_convert_fusion.5
  (87 shorter events, 4.0 us)
Async XLA Ops:
  9.4 4.8 %all-to-all-start.1 = ((bf16[2,32,896]{2,1,0:T(8,128)(2,1)}), bf16[2,32,896]{2,1,0:T(8,128)(2,1)S(1)}, u32[]{:S(2)}, u32[]{:S(2)}) async-start(bf16[2,32,896]{2,1,0:T(8,128)(2,1)} %pad_maximum_fusion.2), calls=%async_computation.1 | async-start | bytes 229376 | tf_op jit(solution)/shard_map/all_to_all | solution.py:60
  13.9 126.6 %copy-start = (f32[4,2816]{1,0:T(4,128)S(1)}, f32[4,2816]{1,0:T(4,128)}, u32[]{:S(2)}) copy-start(f32[4,2816]{1,0:T(4,128)} %param.17) | copy-start | bytes 135172
  13.9 126.6 %slice-start = ((f32[4,2816]{1,0:T(4,128)}), f32[4,256]{1,0:T(4,128)S(1)}, s32[]{:S(2)}) async-start(f32[4,2816]{1,0:T(4,128)} %param.17), calls=%async_computation.5 | async-start | bytes 8192 | tf_op jit(solution)/shard_map/slice | solution.py:113
  16.4 22.7 %all-to-all-start = ((bf16[4,64,2560]{2,1,0:T(8,128)(2,1)}), bf16[4,64,2560]{2,1,0:T(8,128)(2,1)S(1)}, u32[]{:S(2)}, u32[]{:S(2)}) async-start(bf16[4,64,2560]{2,1,0:T(8,128)(2,1)} %broadcast_in_dim.39), calls=%async_computation | async-start | bytes 2621440 | tf_op jit(solution)/shard_map/all_to_all | solution.py:48
  20.8 116.2 %all-gather.2.cloned.1.call-start = ((), (), s32[]{:S(2)}) async-start(), calls=%async_computation.4 | async-start | bytes 7798784 | tf_op jit(solution)/shard_map/all_gather | solution.py:75
  137.0 20.6 %collective-permute-start.1 = (bf16[4096,896]{1,0:T(8,128)(2,1)}, bf16[4096,896]{1,0:T(8,128)(2,1)}, u32[]{:S(2)}, u32[]{:S(2)}) collective-permute-start(bf16[4096,896]{1,0:T(8,128)(2,1)} %all-gather.2.cloned.1.call-done), channel_id=1, source_target_pairs={{0,4},{4,0},{1,5},{5,1},{2,6},{6,2},{3,7},{7,3},{8,12},{12,8},{9,1... | collective-permute-start | bytes 22020104 | tf_op jit(solution)/shard_map/ppermute | solution.py:76
  140.6 10.7 %collective-permute-start = (bf16[3,2560]{1,0:T(4,128)(2,1)S(1)}, bf16[3,2560]{1,0:T(4,128)(2,1)S(1)}, u32[]{:S(2)}, u32[]{:S(2)}) collective-permute-start(bf16[3,2560]{1,0:T(4,128)(2,1)S(1)} %slice.128), channel_id=1, source_target_pairs={{0,4},{4,8},{8,12},{12,16},{16,20},{20,24},{24,28},{28,32},{32,36}... | collective-permute-start | bytes 46088 | tf_op jit(solution)/shard_map/ppermute | solution.py:16
  157.2 7.0 %slice-start.1 = ((s8[7340032]{0:T(1024)(128)(4,1)}), s8[4194304]{0:T(1024)(128)(4,1)S(1)}, s32[]{:S(2)}) async-start(s8[7340032]{0:T(1024)(128)(4,1)} %bitcast.161), calls=%async_computation.6 | async-start | bytes 8388608
  157.7 6.5 %slice-start.2 = ((s8[7340032]{0:T(1024)(128)(4,1)}), s8[3145728]{0:T(1024)(128)(4,1)S(1)}, s32[]{:S(2)}) async-start(s8[7340032]{0:T(1024)(128)(4,1)} %bitcast.161), calls=%async_computation.7 | async-start | bytes 6291456
  168.2 0.7 copy-start.2
  168.2 0.7 copy-start.5
  170.7 12.1 %copy-start.4 = (f32[10]{0:T(128)}, f32[10]{0:T(128)S(1)}, u32[]{:S(2)}) copy-start(f32[10]{0:T(128)S(1)} %multiply_reduce_fusion.1) | copy-start | bytes 124
  173.9 17.7 %collective-permute-start.3 = (bf16[10,72,128]{2,1,0:T(8,128)(2,1)}, bf16[10,72,128]{2,1,0:T(8,128)(2,1)}, u32[]{:S(2)}, u32[]{:S(2)}) collective-permute-start(bf16[10,72,128]{2,1,0:T(8,128)(2,1)} %pad_maximum_fusion.1), channel_id=1, source_target_pairs={{0,8},{4,12},{8,16},{12,20},{16,24},{20,28},{24,32},{28,36},{32,40... | collective-permute-start | bytes 552968 | tf_op jit(solution)/shard_map/ppermute | solution.py:16
  175.8 16.7 %collective-permute-start.2 = (bf16[10,72,128]{2,1,0:T(8,128)(2,1)}, bf16[10,72,128]{2,1,0:T(8,128)(2,1)}, u32[]{:S(2)}, u32[]{:S(2)}) collective-permute-start(bf16[10,72,128]{2,1,0:T(8,128)(2,1)} %pad_maximum_fusion.1), channel_id=1, source_target_pairs={{0,4},{4,8},{8,12},{12,16},{16,20},{20,24},{24,28},{28,32},{32,36}... | collective-permute-start | bytes 552968 | tf_op jit(solution)/shard_map/ppermute | solution.py:16
  178.4 15.0 %collective-permute-start.4 = (bf16[10,72,128]{2,1,0:T(8,128)(2,1)}, bf16[10,72,128]{2,1,0:T(8,128)(2,1)}, u32[]{:S(2)}, u32[]{:S(2)}) collective-permute-start(bf16[10,72,128]{2,1,0:T(8,128)(2,1)} %pad_maximum_fusion.1), channel_id=1, source_target_pairs={{0,12},{4,16},{8,20},{12,24},{16,28},{20,32},{24,36},{28,40},{32,4... | collective-permute-start | bytes 552968 | tf_op jit(solution)/shard_map/ppermute | solution.py:16
  185.4 13.1 %all-to-all-start.3 = ((bf16[4,64,640]{2,1,0:T(8,128)(2,1)}), bf16[4,64,640]{2,1,0:T(8,128)(2,1)S(1)}, u32[]{:S(2)}, u32[]{:S(2)}) async-start(bf16[4,64,640]{2,1,0:T(8,128)(2,1)} %bitcast.36), calls=%async_computation.3 | async-start | bytes 655360 | tf_op jit(solution)/shard_map/all_to_all | solution.py:107
  189.6 1.9 copy-start.3
  189.6 3.7 %copy-start.6 = (f32[10]{0:T(128)S(1)}, f32[10]{0:T(128)}, u32[]{:S(2)}) copy-start(f32[10]{0:T(128)} %param.21) | copy-start | bytes 124
  198.5 12.5 %all-to-all-start.2 = ((bf16[4,64,640]{2,1,0:T(8,128)(2,1)}), bf16[4,64,640]{2,1,0:T(8,128)(2,1)S(1)}, u32[]{:S(2)}, u32[]{:S(2)}) async-start(bf16[4,64,640]{2,1,0:T(8,128)(2,1)} %copy.144), calls=%async_computation.2 | async-start | bytes 655360 | tf_op jit(solution)/shard_map/all_to_all | solution.py:227
  203.8 8.1 %copy-start.1 = (f32[2560]{0:T(1024)S(1)}, f32[2560]{0:T(1024)}, u32[]{:S(2)}) copy-start(f32[2560]{0:T(1024)} %param.22) | copy-start | bytes 30724
Sparse Core Ops, SparseCore 0:
  39.2 97.7 all-gather.1

commit v9 on v8

--- a/solution.py
+++ b/solution.py
@@ -94,9 +94,9 @@
     spread = spread_rows(both_rows)
     with_own = jnp.dot(spread, own_half, preferred_element_type=jnp.float32)
     with_other = jnp.dot(spread, other_half, preferred_element_type=jnp.float32)
-    first_cols = jnp.where(core_index == 0, with_own, with_other)
-    second_cols = jnp.where(core_index == 0, with_other, with_own)
-    projected = jnp.concatenate([first_cols, second_cols], axis=1)
+    projected = jnp.zeros((with_own.shape[0], 2 * half), jnp.float32)
+    projected = lax.dynamic_update_slice_in_dim(projected, with_own, core_index * half, 1)
+    projected = lax.dynamic_update_slice_in_dim(projected, with_other, (1 - core_index) * half, 1)
     conv_end = local_width + 2 * state_width
     prior_rim = projected[block_rows : block_rows + rim_count, :conv_end].astype(jnp.bfloat16)
     projected = projected[:block_rows]

time: 221 us -> 224 us (1.014)
  matrix products: 17 us -> 13 us
  waiting for transfers between devices: 108 us -> 112 us
  local copies, waits for them, and re-layouts: 17.1 us -> 21 us
    unnamed x25 -> x29, local copies, waits for them, and re-layouts: 1.44 us -> 4.16 us
    all_to_all x1, waiting for transfers between devices: 0.01 us -> 2.42 us  [on_device(): lax.all_to_all(head_gates.reshape(groups, sub_rows, local_width), 'head',...]
  transfers between devices with their start and end apart: 10 -> 10, of which waited for: 4 -> 6; matrix products, arithmetic and copies ran while one was open for 12% -> 12% of each run, Pallas kernels for 0% -> 0%
where the time goes in v9:
time: 224 us; the launch traced here: 223 us
  waiting for transfers between devices  112 us (50%)
  starting transfers between devices  28.7 us (13%)
  local copies, waits for them, and re-layouts  21 us (9%)
  between operations  18 us (8%)
  blocking collectives  15.2 us (7%)
  other arithmetic  14.8 us (7%)
  matrix products  13 us (6%)
    all_gather x1, waiting for transfers between devices, on_device(): own_half = lax.all_gather(own_half, 'z', axis=0, tiled=True)  97.9 us
    all_gather x1, blocking collectives, on_device(): own_half = lax.all_gather(own_half, 'x', axis=0, tiled=True)  15.2 us
    ppermute x4, starting transfers between devices, from_behind(): return lax.ppermute(block, axis, route)  11.2 us
    all_to_all x1, waiting for transfers between devices, on_device(): lax.all_to_all(ssm_rows.reshape(groups, sub_rows, local_width), 'head', 0...  6.9 us
    dot_general x1, matrix products, on_device(): with_other = jnp.dot(spread, other_half, preferred_element_type=jnp.float32)  6.39 us
  transfers between devices with their start and end apart: 10, of which 6 were waited for; matrix products, arithmetic and copies ran while one was open for 12% of the time, Pallas kernels for 0%

profile of v9, /device:TPU:6, one launch (start us, length us, event | category | flops | bytes accessed | tf_op | source)
XLA Modules:
  0.0 222.7 jit_solution(16070621753257227842)
XLA Ops:
  7.2 0.8 copy.127
  8.0 0.8 fusion.32
  8.8 0.7 pad_maximum_fusion.2
  9.4 3.4 %all-to-all-start.1 = ((bf16[2,32,896]{2,1,0:T(8,128)(2,1)}), bf16[2,32,896]{2,1,0:T(8,128)(2,1)S(1)}, u32[]{:S(2)}, u32[]{:S(2)}) async-start(bf16[2,32,896]{2,1,0:T(8,128)(2,1)} %pad_maximum_fusion.2), calls=%async_computation.1 | async-start | bytes 229376 | tf_op jit(solution)/shard_map/all_to_all | solution.py:60
  12.8 0.7 copy.128
  14.2 2.1 broadcast_in_dim.42
  16.4 4.5 %all-to-all-start = ((bf16[4,64,2560]{2,1,0:T(8,128)(2,1)}), bf16[4,64,2560]{2,1,0:T(8,128)(2,1)S(1)}, u32[]{:S(2)}, u32[]{:S(2)}) async-start(bf16[4,64,2560]{2,1,0:T(8,128)(2,1)} %broadcast_in_dim.42), calls=%async_computation | async-start | bytes 2621440 | tf_op jit(solution)/shard_map/all_to_all | solution.py:48
  21.0 15.2 %all_gather.6 = bf16[256,896]{1,0:T(8,128)(2,1)} all-gather(bf16[64,896]{1,0:T(8,128)(2,1)S(1)} %bitcast.148), channel_id=1, replica_groups=mesh['x'=4,'z'=16,'c'=2,'head'=4] {'x'}, dimensions={0}, use_global_device_ids=true | all-gather | bytes 573440 | tf_op jit(solution)/shard_map/all_gather | solution.py:61
  36.2 2.8 %all-to-all-done = bf16[4,64,2560]{2,1,0:T(8,128)(2,1)S(1)} async-done(((bf16[4,64,2560]{2,1,0:T(8,128)(2,1)}), bf16[4,64,2560]{2,1,0:T(8,128)(2,1)S(1)}, u32[]{:S(2)}, u32[]{:S(2)}) %all-to-all-start) | async-done | bytes 1310752 | tf_op jit(solution)/shard_map/all_to_all | solution.py:48
  39.1 97.9 %all-gather.2.cloned.1.call-done = bf16[4096,896]{1,0:T(8,128)(2,1)} async-done(((bf16[256,896]{1,0:T(8,128)(2,1)}), bf16[4096,896]{1,0:T(8,128)(2,1)}) %all-gather.2.cloned.1.call-update) | async-done | bytes 7340048 | tf_op jit(solution)/shard_map/all_gather | solution.py:75
  137.0 1.9 collective-permute-start.1
  139.0 0.7 slice.120
  139.7 0.8 dynamic_slice.6
  140.6 2.4 %collective-permute-start = (bf16[3,2560]{1,0:T(4,128)(2,1)S(1)}, bf16[3,2560]{1,0:T(4,128)(2,1)S(1)}, u32[]{:S(2)}, u32[]{:S(2)}) collective-permute-start(bf16[3,2560]{1,0:T(4,128)(2,1)S(1)} %slice.125), channel_id=1, source_target_pairs={{0,4},{4,8},{8,12},{12,16},{16,20},{20,24},{24,28},{28,32},{32,36}... | collective-permute-start | bytes 46088 | tf_op jit(solution)/shard_map/ppermute | solution.py:16
  143.0 0.6 slice.177
  143.6 0.6 slice.175
  144.3 0.6 convert_reduce_fusion.4
  145.5 0.7 select_reduce_fusion
  146.2 2.6 %broadcast_compare_fusion = (pred[256]{0:T(512)(128)(4,1)}, f32[256]{0:T(256)}, pred[256]{0:T(512)(128)(4,1)}) fusion(s32[256]{0:T(256)S(1)} %compare_select_fusion.3, s32[]{:T(128)} %bitcast.18, s32[]{:T(128)} %bitcast.29, pred[]{:T(512)} %gt.8, s32[]{:T(128)} %select_reduce_fusion), kind=kLoop, calls=%fused_computation.132 | loop fusion | flops 1280 | bytes 2573 | tf_op jit(solution)/shard_map/eq | solution.py:169
  148.8 0.7 compare_convert_fusion.3
  149.5 0.7 fusion.16
  153.3 2.4 %copy.129 = bf16[264,2560]{0,1:T(8,128)(2,1)} copy(bf16[264,2560]{1,0:T(8,128)(2,1)S(1)} %maximum_maximum_fusion) | data formatting | bytes 2703360 | tf_op jit(solution)/shard_map/concatenate | solution.py:91
  155.7 2.5 %reshape.411 = bf16[264,4,16,2,20]{0,4,3,2,1:T(8,128)(2,1)S(1)} reshape(bf16[264,2560]{0,1:T(8,128)(2,1)} %copy.129) | data formatting | bytes 2703360 | tf_op jit(solution)/shard_map/reshape | solution.py:84
  158.2 0.6 pad_bitcast_fusion
  159.4 1.0 slice-done.1
  160.4 1.1 slice-done.2
  161.5 4.0 %convolution_dynamic-update-slice_fusion.1 = f32[264,1792]{0,1:T(8,128)S(1)} fusion(f32[264,1792]{0,1:T(8,128)S(1)} %broadcast_in_dim.41, s32[]{:T(128)S(6)} %select_n.54, bf16[264,4096]{0,1:T(8,128)(2,1)S(1)} %bitcast.140, bf16[4096,896]{1,0:T(8,128)(2,1)S(1)} %bitcast.162), kind=kOutput, calls=%fused_computation.3 | convolution fusion | flops 1937768448 | bytes 11862020 | tf_op jit(solution)/shard_map/dot_general | solution.py:95
  165.6 6.4 %convolution_dynamic-update-slice_fusion = f32[264,1792]{0,1:T(8,128)S(1)} fusion(f32[264,1792]{0,1:T(8,128)S(1)} %convolution_dynamic-update-slice_fusion.1, s32[]{:T(128)S(6)} %select_n.55, bf16[264,4096]{0,1:T(8,128)(2,1)S(1)} %bitcast.141, bf16[4096,896]{1,0:T(8,128)(2,1)} %collective-permute-done.1), kind=kOutput, calls=%fused_computation.2 | convolution fusion | flops 1937768448 | bytes 11862020 | tf_op jit(solution)/shard_map/dot_general | solution.py:96
  172.1 0.6 reduce-window.19
  173.1 1.0 copy-done
  174.3 0.7 multiply_reduce_fusion.1
  175.1 0.8 fusion.48
  176.0 0.7 fusion.49
  176.8 2.2 multiply_convert_fusion.4
  179.4 1.9 collective-permute-start.3
  181.4 2.6 %collective-permute-start.2 = (bf16[10,72,128]{2,1,0:T(8,128)(2,1)S(1)}, bf16[10,72,128]{2,1,0:T(8,128)(2,1)S(1)}, u32[]{:S(2)}, u32[]{:S(2)}) collective-permute-start(bf16[10,72,128]{2,1,0:T(8,128)(2,1)S(1)} %pad_maximum_fusion.1), channel_id=1, source_target_pairs={{0,4},{4,8},{8,12},{12,16},{16,20},{20,24},{24,28},{28,32},{32,36}... | collective-permute-start | bytes 552968 | tf_op jit(solution)/shard_map/ppermute | solution.py:16
  184.0 4.3 %collective-permute-start.4 = (bf16[10,72,128]{2,1,0:T(8,128)(2,1)S(1)}, bf16[10,72,128]{2,1,0:T(8,128)(2,1)S(1)}, u32[]{:S(2)}, u32[]{:S(2)}) collective-permute-start(bf16[10,72,128]{2,1,0:T(8,128)(2,1)S(1)} %pad_maximum_fusion.1), channel_id=1, source_target_pairs={{0,12},{4,16},{8,20},{12,24},{16,28},{20,32},{24,36},{28,40},{32,4... | collective-permute-start | bytes 552968 | tf_op jit(solution)/shard_map/ppermute | solution.py:16
  188.6 1.0 slice.183
  189.7 0.9 copy.142
  190.5 4.3 %all-to-all-start.3 = ((bf16[4,64,640]{2,1,0:T(8,128)(2,1)}), bf16[4,64,640]{2,1,0:T(8,128)(2,1)S(1)}, u32[]{:S(2)}, u32[]{:S(2)}) async-start(bf16[4,64,640]{2,1,0:T(8,128)(2,1)} %bitcast.36), calls=%async_computation.3 | async-start | bytes 655360 | tf_op jit(solution)/shard_map/all_to_all | solution.py:107
  194.8 0.9 fusion.7
  196.1 1.6 collective-permute-done.4
  198.3 1.4 copy.140
  199.7 1.0 add_bitcast_fusion
  200.7 2.4 %all-to-all-done.3 = bf16[4,64,640]{2,1,0:T(8,128)(2,1)S(1)} async-done(((bf16[4,64,640]{2,1,0:T(8,128)(2,1)}), bf16[4,64,640]{2,1,0:T(8,128)(2,1)S(1)}, u32[]{:S(2)}, u32[]{:S(2)}) %all-to-all-start.3) | async-done | bytes 327712 | tf_op jit(solution)/shard_map/all_to_all | solution.py:107
  203.1 3.5 %all-to-all-start.2 = ((bf16[4,64,640]{2,1,0:T(8,128)(2,1)}), bf16[4,64,640]{2,1,0:T(8,128)(2,1)S(1)}, u32[]{:S(2)}, u32[]{:S(2)}) async-start(bf16[4,64,640]{2,1,0:T(8,128)(2,1)} %copy.140), calls=%async_computation.2 | async-start | bytes 655360 | tf_op jit(solution)/shard_map/all_to_all | solution.py:227
  207.1 6.9 %all-to-all-done.2 = bf16[4,64,640]{2,1,0:T(8,128)(2,1)S(1)} async-done(((bf16[4,64,640]{2,1,0:T(8,128)(2,1)}), bf16[4,64,640]{2,1,0:T(8,128)(2,1)S(1)}, u32[]{:S(2)}, u32[]{:S(2)}) %all-to-all-start.2) | async-done | bytes 327712 | tf_op jit(solution)/shard_map/all_to_all | solution.py:227
  214.9 1.0 multiply_convert_fusion.5
  (92 shorter events, 5.7 us)
Async XLA Ops:
  9.4 4.8 %all-to-all-start.1 = ((bf16[2,32,896]{2,1,0:T(8,128)(2,1)}), bf16[2,32,896]{2,1,0:T(8,128)(2,1)S(1)}, u32[]{:S(2)}, u32[]{:S(2)}) async-start(bf16[2,32,896]{2,1,0:T(8,128)(2,1)} %pad_maximum_fusion.2), calls=%async_computation.1 | async-start | bytes 229376 | tf_op jit(solution)/shard_map/all_to_all | solution.py:60
  13.8 126.7 %copy-start.2 = (f32[4,2816]{1,0:T(4,128)S(1)}, f32[4,2816]{1,0:T(4,128)}, u32[]{:S(2)}) copy-start(f32[4,2816]{1,0:T(4,128)} %param.17) | copy-start | bytes 135172
  13.8 126.7 %slice-start = ((f32[4,2816]{1,0:T(4,128)}), f32[4,256]{1,0:T(4,128)S(1)}, s32[]{:S(2)}) async-start(f32[4,2816]{1,0:T(4,128)} %param.17), calls=%async_computation.5 | async-start | bytes 8192 | tf_op jit(solution)/shard_map/slice | solution.py:113
  16.4 22.7 %all-to-all-start = ((bf16[4,64,2560]{2,1,0:T(8,128)(2,1)}), bf16[4,64,2560]{2,1,0:T(8,128)(2,1)S(1)}, u32[]{:S(2)}, u32[]{:S(2)}) async-start(bf16[4,64,2560]{2,1,0:T(8,128)(2,1)} %broadcast_in_dim.42), calls=%async_computation | async-start | bytes 2621440 | tf_op jit(solution)/shard_map/all_to_all | solution.py:48
  20.8 116.2 %all-gather.2.cloned.1.call-start = ((), (), s32[]{:S(2)}) async-start(), calls=%async_computation.4 | async-start | bytes 7798784 | tf_op jit(solution)/shard_map/all_gather | solution.py:75
  137.0 28.5 %collective-permute-start.1 = (bf16[4096,896]{1,0:T(8,128)(2,1)}, bf16[4096,896]{1,0:T(8,128)(2,1)}, u32[]{:S(2)}, u32[]{:S(2)}) collective-permute-start(bf16[4096,896]{1,0:T(8,128)(2,1)} %all-gather.2.cloned.1.call-done), channel_id=1, source_target_pairs={{0,4},{4,0},{1,5},{5,1},{2,6},{6,2},{3,7},{7,3},{8,12},{12,8},{9,1... | collective-permute-start | bytes 22020104 | tf_op jit(solution)/shard_map/ppermute | solution.py:76
  140.6 12.4 %collective-permute-start = (bf16[3,2560]{1,0:T(4,128)(2,1)S(1)}, bf16[3,2560]{1,0:T(4,128)(2,1)S(1)}, u32[]{:S(2)}, u32[]{:S(2)}) collective-permute-start(bf16[3,2560]{1,0:T(4,128)(2,1)S(1)} %slice.125), channel_id=1, source_target_pairs={{0,4},{4,8},{8,12},{12,16},{16,20},{20,24},{24,28},{28,32},{32,36}... | collective-permute-start | bytes 46088 | tf_op jit(solution)/shard_map/ppermute | solution.py:16
  158.2 2.2 slice-start.1
  158.8 2.7 %slice-start.2 = ((s8[7340032]{0:T(1024)(128)(4,1)}), s8[3145728]{0:T(1024)(128)(4,1)S(1)}, s32[]{:S(2)}) async-start(s8[7340032]{0:T(1024)(128)(4,1)} %bitcast.161), calls=%async_computation.7 | async-start | bytes 6291456
  165.5 6.4 %copy-start.4 = (f32[10]{0:T(128)S(1)}, f32[10]{0:T(128)}, u32[]{:S(2)}) copy-start(f32[10]{0:T(128)} %param.19) | copy-start | bytes 124
  165.5 6.4 %copy-start.7 = (f32[10]{0:T(128)S(1)}, f32[10]{0:T(128)}, u32[]{:S(2)}) copy-start(f32[10]{0:T(128)} %param.20) | copy-start | bytes 124
  173.0 1.1 copy-start
  176.8 12.8 %copy-start.6 = (f32[10]{0:T(128)S(1)}, f32[10]{0:T(128)}, u32[]{:S(2)}) copy-start(f32[10]{0:T(128)} %multiply_reduce_fusion.1) | copy-start | bytes 124
  178.9 15.9 %copy-start.1 = (pred[256,256]{1,0:T(8,128)(4,1)S(1)}, pred[256,256]{1,0:T(8,128)(4,1)}, u32[]{:S(2)}) copy-start(pred[256,256]{1,0:T(8,128)(4,1)} %fusion.16) | copy-start | bytes 196612
  179.4 16.3 %collective-permute-start.3 = (bf16[10,72,128]{2,1,0:T(8,128)(2,1)S(1)}, bf16[10,72,128]{2,1,0:T(8,128)(2,1)S(1)}, u32[]{:S(2)}, u32[]{:S(2)}) collective-permute-start(bf16[10,72,128]{2,1,0:T(8,128)(2,1)S(1)} %pad_maximum_fusion.1), channel_id=1, source_target_pairs={{0,8},{4,12},{8,16},{12,20},{16,24},{20,28},{24,32},{28,36},{32,40... | collective-permute-start | bytes 552968 | tf_op jit(solution)/shard_map/ppermute | solution.py:16
  181.4 14.6 %collective-permute-start.2 = (bf16[10,72,128]{2,1,0:T(8,128)(2,1)S(1)}, bf16[10,72,128]{2,1,0:T(8,128)(2,1)S(1)}, u32[]{:S(2)}, u32[]{:S(2)}) collective-permute-start(bf16[10,72,128]{2,1,0:T(8,128)(2,1)S(1)} %pad_maximum_fusion.1), channel_id=1, source_target_pairs={{0,4},{4,8},{8,12},{12,16},{16,20},{20,24},{24,28},{28,32},{32,36}... | collective-permute-start | bytes 552968 | tf_op jit(solution)/shard_map/ppermute | solution.py:16
  184.0 13.7 %collective-permute-start.4 = (bf16[10,72,128]{2,1,0:T(8,128)(2,1)S(1)}, bf16[10,72,128]{2,1,0:T(8,128)(2,1)S(1)}, u32[]{:S(2)}, u32[]{:S(2)}) collective-permute-start(bf16[10,72,128]{2,1,0:T(8,128)(2,1)S(1)} %pad_maximum_fusion.1), channel_id=1, source_target_pairs={{0,12},{4,16},{8,20},{12,24},{16,28},{20,32},{24,36},{28,40},{32,4... | collective-permute-start | bytes 552968 | tf_op jit(solution)/shard_map/ppermute | solution.py:16
  190.5 12.5 %all-to-all-start.3 = ((bf16[4,64,640]{2,1,0:T(8,128)(2,1)}), bf16[4,64,640]{2,1,0:T(8,128)(2,1)S(1)}, u32[]{:S(2)}, u32[]{:S(2)}) async-start(bf16[4,64,640]{2,1,0:T(8,128)(2,1)} %bitcast.36), calls=%async_computation.3 | async-start | bytes 655360 | tf_op jit(solution)/shard_map/all_to_all | solution.py:107
  194.8 1.0 copy-start.5
  194.8 2.9 %copy-start.8 = (f32[10]{0:T(128)S(1)}, f32[10]{0:T(128)}, u32[]{:S(2)}) copy-start(f32[10]{0:T(128)} %param.21) | copy-start | bytes 124
  203.1 10.9 %all-to-all-start.2 = ((bf16[4,64,640]{2,1,0:T(8,128)(2,1)}), bf16[4,64,640]{2,1,0:T(8,128)(2,1)S(1)}, u32[]{:S(2)}, u32[]{:S(2)}) async-start(bf16[4,64,640]{2,1,0:T(8,128)(2,1)} %copy.140), calls=%async_computation.2 | async-start | bytes 655360 | tf_op jit(solution)/shard_map/all_to_all | solution.py:227
  207.0 7.8 %copy-start.3 = (f32[2560]{0:T(1024)S(1)}, f32[2560]{0:T(1024)}, u32[]{:S(2)}) copy-start(f32[2560]{0:T(1024)} %param.22) | copy-start | bytes 30724
Sparse Core Ops, SparseCore 0:
  39.2 97.7 all-gather.1

commit v10 on v8

--- a/solution.py
+++ b/solution.py
@@ -58,7 +58,10 @@
     merged = jnp.pad(merged, ((0, padded_rows - shard_rows), (0, 2 * half - merged.shape[1])))
     halves = jnp.stack([merged[:, :half], merged[:, half:]])
     own_half = lax.all_to_all(halves, "c", 0, 0, tiled=True).reshape(2 * padded_rows, half)
-    own_half = lax.all_gather(own_half, "x", axis=0, tiled=True)
+    x_count = lax.psum(1, "x")
+    own_half = lax.all_to_all(
+        jnp.broadcast_to(own_half[None], (x_count,) + own_half.shape), "x", 0, 0, tiled=True
+    ).reshape(x_count * own_half.shape[0], own_half.shape[1])
     early_start = block_index * block_rows
     ext_positions = (
         early_start - (conv_taps - 1) + jnp.arange(block_rows + conv_taps - 1, dtype=jnp.int32)

time: 221 us -> 230 us (1.041)
  waiting for transfers between devices: 108 us -> 124 us
  blocking collectives: 15.2 us -> 3.82 us
  starting transfers between devices: 30 us -> 35.1 us
    all_gather x1 -> x0, blocking collectives: 15.2 us -> none  [on_device(): own_half = lax.all_gather(own_half, 'x', axis=0, tiled=True)]
    all_to_all x1, waiting for transfers between devices: 2.85 us -> 17.3 us  [on_device(): lax.all_to_all(jnp.broadcast_to(hidden[None], (groups,) + hidden.shape),...]
    all_to_all x1, waiting for transfers between devices: 0.31 us -> 6.3 us  [on_device(): lax.all_to_all(jnp.broadcast_to(own_half[None], (x_count,) + own_half.sha...]
    all_to_all x1, starting transfers between devices: 3.36 us -> 9.29 us  [on_device(): lax.all_to_all(jnp.broadcast_to(own_half[None], (x_count,) + own_half.sha...]
    all_gather x1, waiting for transfers between devices: 97.9 us -> 93.2 us  [on_device(): own_half = lax.all_gather(own_half, 'z', axis=0, tiled=True)]
    all_to_all x0 -> x1, blocking collectives: none -> 3.82 us  [on_device(): lax.all_to_all(halves, 'c', 0, 0, tiled=True).reshape(2 * padded_rows, half)]
  transfers between devices with their start and end apart: 10 -> 10, of which waited for: 4 -> 4; matrix products, arithmetic and copies ran while one was open for 12% -> 11% of each run, Pallas kernels for 0% -> 0%
where the time goes in v10:
time: 230 us; the launch traced here: 228 us
  waiting for transfers between devices  124 us (54%)
  starting transfers between devices  35.1 us (15%)
  between operations  17.8 us (8%)
  local copies, waits for them, and re-layouts  17.1 us (7%)
  matrix products  17 us (7%)
  other arithmetic  13.6 us (6%)
  blocking collectives  3.82 us (2%)
    all_gather x1, waiting for transfers between devices, on_device(): own_half = lax.all_gather(own_half, 'z', axis=0, tiled=True)  93.2 us
    all_to_all x1, waiting for transfers between devices, on_device(): lax.all_to_all(jnp.broadcast_to(hidden[None], (groups,) + hidden.shape),...  17.3 us
    ppermute x4, starting transfers between devices, from_behind(): return lax.ppermute(block, axis, route)  11.2 us
    all_to_all x1, starting transfers between devices, on_device(): lax.all_to_all(jnp.broadcast_to(own_half[None], (x_count,) + own_half.sha...  9.29 us
    all_to_all x1, waiting for transfers between devices, on_device(): lax.all_to_all(ssm_rows.reshape(groups, sub_rows, local_width), 'head', 0...  7.15 us
    dot_general x1, matrix products, on_device(): with_other = jnp.dot(spread, other_half, preferred_element_type=jnp.float32)  6.52 us
    all_to_all x1, waiting for transfers between devices, on_device(): lax.all_to_all(jnp.broadcast_to(own_half[None], (x_count,) + own_half.sha...  6.3 us
    all_to_all x1, starting transfers between devices, on_device(): lax.all_to_all(ssm_rows.reshape(groups, sub_rows, local_width), 'head', 0...  4.8 us
  transfers between devices with their start and end apart: 10, of which 4 were waited for; matrix products, arithmetic and copies ran while one was open for 11% of the time, Pallas kernels for 0%

profile of v10, /device:TPU:6, one launch (start us, length us, event | category | flops | bytes accessed | tf_op | source)
XLA Modules:
  0.0 228.4 jit_solution(3545425516700313203)
XLA Ops:
  7.2 0.8 copy.129
  8.0 0.8 fusion.32
  8.9 3.8 %all_to_all.33 = bf16[2,32,896]{2,1,0:T(8,128)(2,1)S(1)} all-to-all(bf16[2,32,896]{2,1,0:T(8,128)(2,1)S(1)} %pad_maximum_fusion.2), channel_id=1, replica_groups=mesh['x'=4,'z'=16,'c'=2,'head'=4] {'c'}, dimensions={0} | all-to-all | bytes 229376 | tf_op jit(solution)/shard_map/all_to_all | solution.py:60
  12.7 0.8 broadcast_in_dim.45
  13.5 9.3 %all-to-all-start.2 = ((bf16[4,64,896]{2,1,0:T(8,128)(2,1)}), bf16[4,64,896]{2,1,0:T(8,128)(2,1)S(1)}, u32[]{:S(2)}, u32[]{:S(2)}) async-start(bf16[4,64,896]{2,1,0:T(8,128)(2,1)} %broadcast_in_dim.45), calls=%async_computation.2 | async-start | bytes 917504 | tf_op jit(solution)/shard_map/all_to_all | solution.py:62
  22.8 0.7 copy.130
  23.8 6.3 %all-to-all-done.2 = bf16[4,64,896]{2,1,0:T(8,128)(2,1)S(1)} async-done(((bf16[4,64,896]{2,1,0:T(8,128)(2,1)}), bf16[4,64,896]{2,1,0:T(8,128)(2,1)S(1)}, u32[]{:S(2)}, u32[]{:S(2)}) %all-to-all-start.2) | async-done | bytes 458784 | tf_op jit(solution)/shard_map/all_to_all | solution.py:62
  30.1 1.2 broadcast_in_dim.43
  31.3 3.5 %all-to-all-start = ((bf16[4,64,2560]{2,1,0:T(8,128)(2,1)}), bf16[4,64,2560]{2,1,0:T(8,128)(2,1)S(1)}, u32[]{:S(2)}, u32[]{:S(2)}) async-start(bf16[4,64,2560]{2,1,0:T(8,128)(2,1)} %broadcast_in_dim.43), calls=%async_computation | async-start | bytes 2621440 | tf_op jit(solution)/shard_map/all_to_all | solution.py:48
  35.2 17.3 %all-to-all-done = bf16[4,64,2560]{2,1,0:T(8,128)(2,1)S(1)} async-done(((bf16[4,64,2560]{2,1,0:T(8,128)(2,1)}), bf16[4,64,2560]{2,1,0:T(8,128)(2,1)S(1)}, u32[]{:S(2)}, u32[]{:S(2)}) %all-to-all-start) | async-done | bytes 1310752 | tf_op jit(solution)/shard_map/all_to_all | solution.py:48
  52.5 93.2 %all-gather.2.cloned.1.call-done = bf16[4096,896]{1,0:T(8,128)(2,1)} async-done(((bf16[256,896]{1,0:T(8,128)(2,1)}), bf16[4096,896]{1,0:T(8,128)(2,1)}) %all-gather.2.cloned.1.call-update) | async-done | bytes 7340048 | tf_op jit(solution)/shard_map/all_gather | solution.py:78
  145.8 1.9 collective-permute-start.1
  147.7 0.7 slice.123
  148.4 0.8 dynamic_slice.6
  149.3 2.4 %collective-permute-start = (bf16[3,2560]{1,0:T(4,128)(2,1)S(1)}, bf16[3,2560]{1,0:T(4,128)(2,1)S(1)}, u32[]{:S(2)}, u32[]{:S(2)}) collective-permute-start(bf16[3,2560]{1,0:T(4,128)(2,1)S(1)} %slice.128), channel_id=1, source_target_pairs={{0,4},{4,8},{8,12},{12,16},{16,20},{20,24},{24,28},{28,32},{32,36}... | collective-permute-start | bytes 46088 | tf_op jit(solution)/shard_map/ppermute | solution.py:16
  151.7 0.6 slice.180
  152.3 0.6 slice.178
  152.9 0.6 convert_reduce_fusion.4
  154.2 0.6 select_reduce_fusion
  154.8 2.5 %broadcast_compare_fusion = (pred[256]{0:T(512)(128)(4,1)S(1)}, f32[256]{0:T(256)}, pred[256]{0:T(512)(128)(4,1)S(1)}) fusion(s32[256]{0:T(256)S(1)} %compare_select_fusion.3, s32[]{:T(128)} %bitcast.19, s32[]{:T(128)} %bitcast.30, pred[]{:T(512)} %gt.8, s32[]{:T(128)} %select_reduce_fusion), kind=kLoop, calls=%fused_computation.132 | loop fusion | flops 1280 | bytes 2573 | tf_op jit(solution)/shard_map/eq | solution.py:172
  160.4 2.4 %copy.131 = bf16[264,2560]{0,1:T(8,128)(2,1)} copy(bf16[264,2560]{1,0:T(8,128)(2,1)S(1)} %maximum_maximum_fusion) | data formatting | bytes 2703360 | tf_op jit(solution)/shard_map/concatenate | solution.py:94
  162.8 2.5 %reshape.412 = bf16[264,4,16,2,20]{0,4,3,2,1:T(8,128)(2,1)S(1)} reshape(bf16[264,2560]{0,1:T(8,128)(2,1)} %copy.131) | data formatting | bytes 2703360 | tf_op jit(solution)/shard_map/reshape | solution.py:87
  165.3 0.6 pad_bitcast_fusion
  165.9 0.4 copy.132
  166.4 6.5 %fusion.65 = f32[264,896]{0,1:T(8,128)S(1)} fusion(bf16[264,4096]{0,1:T(8,128)(2,1)S(1)} %bitcast.141, bf16[4096,896]{1,0:T(8,128)(2,1)} %collective-permute-done.1), kind=kOutput, calls=%fused_computation.137 | convolution fusion | flops 1937768448 | bytes 10448896 | tf_op jit(solution)/shard_map/dot_general | solution.py:99
  172.9 4.0 %select_convert_fusion = (bf16[264,896]{0,1:T(8,128)(2,1)S(1)}, f32[264,896]{0,1:T(8,128)S(1)}) fusion(f32[264,896]{0,1:T(8,128)S(1)} %fusion.65, pred[]{:T(512)S(6)} %eq.70, bf16[264,4096]{0,1:T(8,128)(2,1)S(1)} %bitcast.142, bf16[4096,896]{1,0:T(8,128)(2,1)S(1)} %bitcast.164), kind=kOutput, calls=%fused_computation.2 | convolution fusion | flops 1938004992 | bytes 11868161 | tf_op jit(solution)/shard_map/dot_general | solution.py:98
  177.1 0.5 copy-done.4
  177.6 0.7 multiply_bitcast_fusion.1
  178.3 0.6 reduce-window.19
  179.9 1.5 multiply_convert_fusion.4
  181.9 0.7 pad_maximum_fusion.1
  182.6 1.9 collective-permute-start.3
  184.5 2.6 %collective-permute-start.2 = (bf16[10,72,128]{2,1,0:T(8,128)(2,1)}, bf16[10,72,128]{2,1,0:T(8,128)(2,1)}, u32[]{:S(2)}, u32[]{:S(2)}) collective-permute-start(bf16[10,72,128]{2,1,0:T(8,128)(2,1)} %pad_maximum_fusion.1), channel_id=1, source_target_pairs={{0,4},{4,8},{8,12},{12,16},{16,20},{20,24},{24,28},{28,32},{32,36}... | collective-permute-start | bytes 552968 | tf_op jit(solution)/shard_map/ppermute | solution.py:16
  187.1 4.3 %collective-permute-start.4 = (bf16[10,72,128]{2,1,0:T(8,128)(2,1)}, bf16[10,72,128]{2,1,0:T(8,128)(2,1)}, u32[]{:S(2)}, u32[]{:S(2)}) collective-permute-start(bf16[10,72,128]{2,1,0:T(8,128)(2,1)} %pad_maximum_fusion.1), channel_id=1, source_target_pairs={{0,12},{4,16},{8,20},{12,24},{16,28},{20,32},{24,36},{28,40},{32,4... | collective-permute-start | bytes 552968 | tf_op jit(solution)/shard_map/ppermute | solution.py:16
  191.5 0.9 fusion.43
  192.5 0.7 exponential_multiply_fusion
  193.2 0.9 copy.146
  194.1 4.3 %all-to-all-start.4 = ((bf16[4,64,640]{2,1,0:T(8,128)(2,1)}), bf16[4,64,640]{2,1,0:T(8,128)(2,1)S(1)}, u32[]{:S(2)}, u32[]{:S(2)}) async-start(bf16[4,64,640]{2,1,0:T(8,128)(2,1)} %bitcast.37), calls=%async_computation.4 | async-start | bytes 655360 | tf_op jit(solution)/shard_map/all_to_all | solution.py:110
  198.4 1.9 fusion.7
  200.3 0.9 fusion.51
  201.2 0.9 fusion.52
  202.1 1.4 fusion.11
  203.8 1.4 copy.144
  205.2 2.0 add_bitcast_fusion
  207.2 4.8 %all-to-all-start.3 = ((bf16[4,64,640]{2,1,0:T(8,128)(2,1)}), bf16[4,64,640]{2,1,0:T(8,128)(2,1)S(1)}, u32[]{:S(2)}, u32[]{:S(2)}) async-start(bf16[4,64,640]{2,1,0:T(8,128)(2,1)} %copy.144), calls=%async_computation.3 | async-start | bytes 655360 | tf_op jit(solution)/shard_map/all_to_all | solution.py:230
  212.1 0.4 copy.147
  212.6 7.2 %all-to-all-done.3 = bf16[4,64,640]{2,1,0:T(8,128)(2,1)S(1)} async-done(((bf16[4,64,640]{2,1,0:T(8,128)(2,1)}), bf16[4,64,640]{2,1,0:T(8,128)(2,1)S(1)}, u32[]{:S(2)}, u32[]{:S(2)}) %all-to-all-start.3) | async-done | bytes 327712 | tf_op jit(solution)/shard_map/all_to_all | solution.py:230
  220.6 1.0 multiply_convert_fusion.5
  (92 shorter events, 4.2 us)
Async XLA Ops:
  7.2 22.9 %copy-start.1 = (bf16[64,2560]{1,0:T(8,128)(2,1)S(1)}, bf16[64,2560]{1,0:T(8,128)(2,1)}, u32[]{:S(2)}) copy-start(bf16[64,2560]{1,0:T(8,128)(2,1)} %param.12) | copy-start | bytes 983044
  13.5 16.6 %all-to-all-start.2 = ((bf16[4,64,896]{2,1,0:T(8,128)(2,1)}), bf16[4,64,896]{2,1,0:T(8,128)(2,1)S(1)}, u32[]{:S(2)}, u32[]{:S(2)}) async-start(bf16[4,64,896]{2,1,0:T(8,128)(2,1)} %broadcast_in_dim.45), calls=%async_computation.2 | async-start | bytes 917504 | tf_op jit(solution)/shard_map/all_to_all | solution.py:62
  22.8 126.5 %copy-start.2 = (f32[4,2816]{1,0:T(4,128)S(1)}, f32[4,2816]{1,0:T(4,128)}, u32[]{:S(2)}) copy-start(f32[4,2816]{1,0:T(4,128)} %param.17) | copy-start | bytes 135172
  22.8 126.5 %slice-start = ((f32[4,2816]{1,0:T(4,128)}), f32[4,256]{1,0:T(4,128)S(1)}, s32[]{:S(2)}) async-start(f32[4,2816]{1,0:T(4,128)} %param.17), calls=%async_computation.6 | async-start | bytes 8192 | tf_op jit(solution)/shard_map/slice | solution.py:116
  30.1 22.4 %copy-start = (bf16[4,64,896]{2,1,0:T(8,128)(2,1)}, bf16[4,64,896]{2,1,0:T(8,128)(2,1)S(1)}, u32[]{:S(2)}) copy-start(bf16[4,64,896]{2,1,0:T(8,128)(2,1)S(1)} %all-to-all-done.2) | copy-start | bytes 1376260
  31.3 21.2 %all-to-all-start = ((bf16[4,64,2560]{2,1,0:T(8,128)(2,1)}), bf16[4,64,2560]{2,1,0:T(8,128)(2,1)S(1)}, u32[]{:S(2)}, u32[]{:S(2)}) async-start(bf16[4,64,2560]{2,1,0:T(8,128)(2,1)} %broadcast_in_dim.43), calls=%async_computation | async-start | bytes 2621440 | tf_op jit(solution)/shard_map/all_to_all | solution.py:48
  34.9 110.9 %all-gather.2.cloned.1.call-start = ((), (), s32[]{:S(2)}) async-start(), calls=%async_computation.5 | async-start | bytes 7798784 | tf_op jit(solution)/shard_map/all_gather | solution.py:78
  145.8 20.6 %collective-permute-start.1 = (bf16[4096,896]{1,0:T(8,128)(2,1)}, bf16[4096,896]{1,0:T(8,128)(2,1)}, u32[]{:S(2)}, u32[]{:S(2)}) collective-permute-start(bf16[4096,896]{1,0:T(8,128)(2,1)} %all-gather.2.cloned.1.call-done), channel_id=1, source_target_pairs={{0,4},{4,0},{1,5},{5,1},{2,6},{6,2},{3,7},{7,3},{8,12},{12,8},{9,1... | collective-permute-start | bytes 22020104 | tf_op jit(solution)/shard_map/ppermute | solution.py:79
  149.3 10.7 %collective-permute-start = (bf16[3,2560]{1,0:T(4,128)(2,1)S(1)}, bf16[3,2560]{1,0:T(4,128)(2,1)S(1)}, u32[]{:S(2)}, u32[]{:S(2)}) collective-permute-start(bf16[3,2560]{1,0:T(4,128)(2,1)S(1)} %slice.128), channel_id=1, source_target_pairs={{0,4},{4,8},{8,12},{12,16},{16,20},{20,24},{24,28},{28,32},{32,36}... | collective-permute-start | bytes 46088 | tf_op jit(solution)/shard_map/ppermute | solution.py:16
  165.9 7.0 %slice-start.1 = ((s8[7340032]{0:T(1024)(128)(4,1)}), s8[4194304]{0:T(1024)(128)(4,1)S(1)}, s32[]{:S(2)}) async-start(s8[7340032]{0:T(1024)(128)(4,1)} %bitcast.163), calls=%async_computation.7 | async-start | bytes 8388608
  166.4 6.6 %slice-start.2 = ((s8[7340032]{0:T(1024)(128)(4,1)}), s8[3145728]{0:T(1024)(128)(4,1)S(1)}, s32[]{:S(2)}) async-start(s8[7340032]{0:T(1024)(128)(4,1)} %bitcast.163), calls=%async_computation.8 | async-start | bytes 6291456
  176.9 0.7 copy-start.4
  177.0 0.7 copy-start.7
  179.5 12.1 %copy-start.6 = (f32[10]{0:T(128)}, f32[10]{0:T(128)S(1)}, u32[]{:S(2)}) copy-start(f32[10]{0:T(128)S(1)} %multiply_reduce_fusion.1) | copy-start | bytes 124
  182.6 17.7 %collective-permute-start.3 = (bf16[10,72,128]{2,1,0:T(8,128)(2,1)}, bf16[10,72,128]{2,1,0:T(8,128)(2,1)}, u32[]{:S(2)}, u32[]{:S(2)}) collective-permute-start(bf16[10,72,128]{2,1,0:T(8,128)(2,1)} %pad_maximum_fusion.1), channel_id=1, source_target_pairs={{0,8},{4,12},{8,16},{12,20},{16,24},{20,28},{24,32},{28,36},{32,40... | collective-permute-start | bytes 552968 | tf_op jit(solution)/shard_map/ppermute | solution.py:16
  184.5 16.7 %collective-permute-start.2 = (bf16[10,72,128]{2,1,0:T(8,128)(2,1)}, bf16[10,72,128]{2,1,0:T(8,128)(2,1)}, u32[]{:S(2)}, u32[]{:S(2)}) collective-permute-start(bf16[10,72,128]{2,1,0:T(8,128)(2,1)} %pad_maximum_fusion.1), channel_id=1, source_target_pairs={{0,4},{4,8},{8,12},{12,16},{16,20},{20,24},{24,28},{28,32},{32,36}... | collective-permute-start | bytes 552968 | tf_op jit(solution)/shard_map/ppermute | solution.py:16
  187.1 15.0 %collective-permute-start.4 = (bf16[10,72,128]{2,1,0:T(8,128)(2,1)}, bf16[10,72,128]{2,1,0:T(8,128)(2,1)}, u32[]{:S(2)}, u32[]{:S(2)}) collective-permute-start(bf16[10,72,128]{2,1,0:T(8,128)(2,1)} %pad_maximum_fusion.1), channel_id=1, source_target_pairs={{0,12},{4,16},{8,20},{12,24},{16,28},{20,32},{24,36},{28,40},{32,4... | collective-permute-start | bytes 552968 | tf_op jit(solution)/shard_map/ppermute | solution.py:16
  194.1 13.1 %all-to-all-start.4 = ((bf16[4,64,640]{2,1,0:T(8,128)(2,1)}), bf16[4,64,640]{2,1,0:T(8,128)(2,1)S(1)}, u32[]{:S(2)}, u32[]{:S(2)}) async-start(bf16[4,64,640]{2,1,0:T(8,128)(2,1)} %bitcast.37), calls=%async_computation.4 | async-start | bytes 655360 | tf_op jit(solution)/shard_map/all_to_all | solution.py:110
  198.4 1.9 copy-start.5
  198.4 3.7 %copy-start.8 = (f32[10]{0:T(128)S(1)}, f32[10]{0:T(128)}, u32[]{:S(2)}) copy-start(f32[10]{0:T(128)} %param.21) | copy-start | bytes 124
  207.2 12.5 %all-to-all-start.3 = ((bf16[4,64,640]{2,1,0:T(8,128)(2,1)}), bf16[4,64,640]{2,1,0:T(8,128)(2,1)S(1)}, u32[]{:S(2)}, u32[]{:S(2)}) async-start(bf16[4,64,640]{2,1,0:T(8,128)(2,1)} %copy.144), calls=%async_computation.3 | async-start | bytes 655360 | tf_op jit(solution)/shard_map/all_to_all | solution.py:230
  212.5 8.1 %copy-start.3 = (f32[2560]{0:T(1024)S(1)}, f32[2560]{0:T(1024)}, u32[]{:S(2)}) copy-start(f32[2560]{0:T(1024)} %param.22) | copy-start | bytes 30724
Sparse Core Ops, SparseCore 0:
  52.6 93.0 all-gather.1

commit v11 on v8

--- a/solution.py
+++ b/solution.py
@@ -104,9 +104,6 @@
     gates_sum = projected[:, conv_end : conv_end + local_width]
     steps_sum = projected[:, conv_end + local_width : conv_end + local_width + step_width]
     head_gates = gates_sum.astype(jnp.bfloat16)
-    gates_tokens = lax.all_to_all(
-        head_gates.reshape(groups, sub_rows, local_width), "head", 0, 2, tiled=True
-    ).reshape(sub_rows, inner_width)
     local_taps = jnp.concatenate(
         [
             lax.dynamic_slice_in_dim(conv_weight, group_index * local_width, local_width, 1),
@@ -224,10 +221,9 @@
     )
     end_states = end_states + end_carry[:, :, None, None] * arriving
     final_block = jnp.sum(end_states, axis=0)[None]
-    y_tokens = lax.all_to_all(
-        ssm_rows.reshape(groups, sub_rows, local_width), "head", 0, 2, tiled=True
-    ).reshape(sub_rows, inner_width)
-    token_rows = (y_tokens.astype(jnp.float32), gates_tokens.astype(jnp.float32))
+    both = jnp.stack([ssm_rows, head_gates]).reshape(2, groups, sub_rows, local_width)
+    returned = lax.all_to_all(both, "head", split_axis=1, concat_axis=3, tiled=True)
+    token_rows = returned.reshape(2, sub_rows, inner_width).astype(jnp.float32)
     gated = token_rows[0] * jax.nn.silu(token_rows[1])
     mean_square = jnp.mean(gated * gated, axis=1)
     scaled = gated * lax.rsqrt(mean_square + epsilon)[:, None] * norm_gain[None, :]

time: 221 us -> 229 us (1.036)
  other arithmetic: 14.2 us -> 19.6 us
  waiting for transfers between devices: 108 us -> 113 us
  starting transfers between devices: 30 us -> 25.4 us
    all_to_all x2 -> x1, starting transfers between devices: 9.07 us -> 4.29 us  [on_device(): lax.all_to_all(both, 'head', split_axis=1, concat_axis=3, tiled=True)]
    ppermute x4, waiting for transfers between devices: 0.01 us -> 4.19 us  [from_behind(): return lax.ppermute(block, axis, route)]
    another operation x9 -> x11, local copies, waits for them, and re-layouts: 0.97 us -> 4.21 us  [the longest x2 3.24 us: on_device(): jnp.stack([ssm_rows, head_gates]).reshape(2, groups, sub_rows, local_width)]
    dot_general x1, matrix products: 3.99 us -> 6.29 us  [on_device(): with_own = jnp.dot(spread, own_half, preferred_element_type=jnp.float32)]
    all_to_all x2 -> x1, waiting for transfers between devices: 7.16 us -> 7.89 us  [on_device(): lax.all_to_all(both, 'head', split_axis=1, concat_axis=3, tiled=True)]
  transfers between devices with their start and end apart: 10 -> 9, of which waited for: 4 -> 5; matrix products, arithmetic and copies ran while one was open for 12% -> 13% of each run, Pallas kernels for 0% -> 0%
where the time goes in v11:
time: 229 us; the launch traced here: 228 us
  waiting for transfers between devices  113 us (49%)
  starting transfers between devices  25.4 us (11%)
  other arithmetic  19.6 us (9%)
  local copies, waits for them, and re-layouts  19 us (8%)
  between operations  17.6 us (8%)
  matrix products  17.5 us (8%)
  blocking collectives  15.2 us (7%)
    all_gather x1, waiting for transfers between devices, on_device(): own_half = lax.all_gather(own_half, 'z', axis=0, tiled=True)  97.9 us
    all_gather x1, blocking collectives, on_device(): own_half = lax.all_gather(own_half, 'x', axis=0, tiled=True)  15.2 us
    ppermute x4, starting transfers between devices, from_behind(): return lax.ppermute(block, axis, route)  11.4 us
    all_to_all x1, waiting for transfers between devices, on_device(): lax.all_to_all(both, 'head', split_axis=1, concat_axis=3, tiled=True)  7.89 us
    dot_general x1, matrix products, on_device(): with_other = jnp.dot(spread, other_half, preferred_element_type=jnp.float32)  6.43 us
    dot_general x1, matrix products, on_device(): with_own = jnp.dot(spread, own_half, preferred_element_type=jnp.float32)  6.29 us
  transfers between devices with their start and end apart: 9, of which 5 were waited for; matrix products, arithmetic and copies ran while one was open for 13% of the time, Pallas kernels for 0%

profile of v11, /device:TPU:6, one launch (start us, length us, event | category | flops | bytes accessed | tf_op | source)
XLA Modules:
  0.0 227.6 jit_solution(16945405754403509333)
XLA Ops:
  7.2 0.8 copy.130
  8.0 0.8 fusion.32
  8.8 0.7 pad_maximum_fusion.3
  9.4 3.4 %all-to-all-start.1 = ((bf16[2,32,896]{2,1,0:T(8,128)(2,1)}), bf16[2,32,896]{2,1,0:T(8,128)(2,1)S(1)}, u32[]{:S(2)}, u32[]{:S(2)}) async-start(bf16[2,32,896]{2,1,0:T(8,128)(2,1)} %pad_maximum_fusion.3), calls=%async_computation.1 | async-start | bytes 229376 | tf_op jit(solution)/shard_map/all_to_all | solution.py:60
  12.8 0.7 copy.131
  14.2 2.1 broadcast_in_dim.39
  16.4 4.5 %all-to-all-start = ((bf16[4,64,2560]{2,1,0:T(8,128)(2,1)}), bf16[4,64,2560]{2,1,0:T(8,128)(2,1)S(1)}, u32[]{:S(2)}, u32[]{:S(2)}) async-start(bf16[4,64,2560]{2,1,0:T(8,128)(2,1)} %broadcast_in_dim.39), calls=%async_computation | async-start | bytes 2621440 | tf_op jit(solution)/shard_map/all_to_all | solution.py:48
  21.0 15.2 %all_gather.6 = bf16[256,896]{1,0:T(8,128)(2,1)} all-gather(bf16[64,896]{1,0:T(8,128)(2,1)S(1)} %bitcast.136), channel_id=1, replica_groups=mesh['x'=4,'z'=16,'c'=2,'head'=4] {'x'}, dimensions={0}, use_global_device_ids=true | all-gather | bytes 573440 | tf_op jit(solution)/shard_map/all_gather | solution.py:61
  36.2 2.8 %all-to-all-done = bf16[4,64,2560]{2,1,0:T(8,128)(2,1)S(1)} async-done(((bf16[4,64,2560]{2,1,0:T(8,128)(2,1)}), bf16[4,64,2560]{2,1,0:T(8,128)(2,1)S(1)}, u32[]{:S(2)}, u32[]{:S(2)}) %all-to-all-start) | async-done | bytes 1310752 | tf_op jit(solution)/shard_map/all_to_all | solution.py:48
  39.1 97.9 %all-gather.2.cloned.1.call-done = bf16[4096,896]{1,0:T(8,128)(2,1)} async-done(((bf16[256,896]{1,0:T(8,128)(2,1)}), bf16[4096,896]{1,0:T(8,128)(2,1)}) %all-gather.2.cloned.1.call-update) | async-done | bytes 7340048 | tf_op jit(solution)/shard_map/all_gather | solution.py:75
  137.0 1.9 collective-permute-start.1
  139.0 0.7 slice.131
  139.7 0.8 dynamic_slice.6
  140.5 0.6 fusion.58
  141.2 0.6 pad_maximum_fusion.4
  141.8 2.4 %collective-permute-start = (bf16[3,2560]{1,0:T(4,128)(2,1)S(1)}, bf16[3,2560]{1,0:T(4,128)(2,1)S(1)}, u32[]{:S(2)}, u32[]{:S(2)}) collective-permute-start(bf16[3,2560]{1,0:T(4,128)(2,1)S(1)} %slice.136), channel_id=1, source_target_pairs={{0,4},{4,8},{8,12},{12,16},{16,20},{20,24},{24,28},{28,32},{32,36}... | collective-permute-start | bytes 46088 | tf_op jit(solution)/shard_map/ppermute | solution.py:16
  144.7 0.6 slice.188
  145.3 0.6 convert_reduce_fusion.4
  146.6 0.7 select_reduce_fusion
  147.3 2.4 %broadcast_compare_fusion = (pred[256]{0:T(512)(128)(4,1)}, f32[256]{0:T(256)}, pred[256]{0:T(512)(128)(4,1)}) fusion(s32[256]{0:T(256)S(1)} %compare_select_fusion.3, s32[]{:T(128)} %bitcast.18, s32[]{:T(128)} %bitcast.29, pred[]{:T(512)} %gt.8, s32[]{:T(128)} %select_reduce_fusion), kind=kLoop, calls=%fused_computation.133 | loop fusion | flops 1280 | bytes 2573 | tf_op jit(solution)/shard_map/eq | solution.py:166
  149.6 0.7 compare_convert_fusion.3
  152.5 2.4 %copy.132 = bf16[264,2560]{0,1:T(8,128)(2,1)} copy(bf16[264,2560]{1,0:T(8,128)(2,1)S(1)} %maximum_maximum_fusion) | data formatting | bytes 2703360 | tf_op jit(solution)/shard_map/concatenate | solution.py:91
  154.9 2.5 %reshape.414 = bf16[264,4,16,2,20]{0,4,3,2,1:T(8,128)(2,1)S(1)} reshape(bf16[264,2560]{0,1:T(8,128)(2,1)} %copy.132) | data formatting | bytes 2703360 | tf_op jit(solution)/shard_map/reshape | solution.py:84
  157.4 0.6 pad_bitcast_fusion
  158.5 6.3 %fusion.66 = f32[264,896]{0,1:T(8,128)S(1)} fusion(bf16[264,4096]{0,1:T(8,128)(2,1)S(1)} %bitcast.127, bf16[4096,896]{1,0:T(8,128)(2,1)} %all-gather.2.cloned.1.call-done), kind=kOutput, calls=%fused_computation.139 | convolution fusion | flops 1937768448 | bytes 10448896 | tf_op jit(solution)/shard_map/dot_general | solution.py:95
  164.8 6.4 %broadcast_select_fusion = (f32[264,896]{0,1:T(8,128)S(1)}, bf16[264,896]{0,1:T(8,128)(2,1)S(1)}) fusion(f32[264,896]{0,1:T(8,128)S(1)} %fusion.66, pred[]{:T(512)S(6)} %eq.70, bf16[264,4096]{0,1:T(8,128)(2,1)S(1)} %bitcast.128, bf16[4096,896]{1,0:T(8,128)(2,1)} %collective-permute-done.1), kind=kOutput, calls=%fused_computation.25 | convolution fusion | flops 1938241536 | bytes 11868161 | tf_op jit(solution)/shard_map/dot_general | solution.py:96
  171.3 0.8 multiply_bitcast_fusion.1
  173.2 0.8 multiply_reduce_fusion.1
  174.1 0.8 fusion.48
  175.0 0.8 fusion.49
  175.8 2.3 multiply_convert_fusion.4
  178.5 0.7 pad_maximum_fusion.2
  179.2 1.9 collective-permute-start.3
  181.1 2.6 %collective-permute-start.2 = (bf16[10,72,128]{2,1,0:T(8,128)(2,1)}, bf16[10,72,128]{2,1,0:T(8,128)(2,1)}, u32[]{:S(2)}, u32[]{:S(2)}) collective-permute-start(bf16[10,72,128]{2,1,0:T(8,128)(2,1)} %pad_maximum_fusion.2), channel_id=1, source_target_pairs={{0,4},{4,8},{8,12},{12,16},{16,20},{20,24},{24,28},{28,32},{32,36}... | collective-permute-start | bytes 552968 | tf_op jit(solution)/shard_map/ppermute | solution.py:16
  183.8 4.4 %collective-permute-start.4 = (bf16[10,72,128]{2,1,0:T(8,128)(2,1)}, bf16[10,72,128]{2,1,0:T(8,128)(2,1)}, u32[]{:S(2)}, u32[]{:S(2)}) collective-permute-start(bf16[10,72,128]{2,1,0:T(8,128)(2,1)} %pad_maximum_fusion.2), channel_id=1, source_target_pairs={{0,12},{4,16},{8,20},{12,24},{16,28},{20,32},{24,36},{28,40},{32,4... | collective-permute-start | bytes 552968 | tf_op jit(solution)/shard_map/ppermute | solution.py:16
  188.6 0.9 fusion.7
  189.6 1.1 slice.326
  190.9 0.8 copy.146
  191.8 0.9 fusion.51
  192.7 0.9 fusion.52
  193.6 4.2 %collective-permute-done.4 = bf16[10,72,128]{2,1,0:T(8,128)(2,1)} collective-permute-done((bf16[10,72,128]{2,1,0:T(8,128)(2,1)}, bf16[10,72,128]{2,1,0:T(8,128)(2,1)}, u32[]{:S(2)}, u32[]{:S(2)}) %collective-permute-start.4) | collective-permute-done | bytes 184352 | tf_op jit(solution)/shard_map/ppermute | solution.py:16
  197.7 1.4 fusion.11
  199.4 1.1 pad_maximum_fusion
  200.5 2.4 %copy.147 = bf16[2,4,64,640]{3,2,0,1:T(8,128)(2,1)} copy(bf16[2,4,64,640]{2,1,3,0:T(4,128)(2,1)S(1)} %pad_maximum_fusion) | data formatting | bytes 1310720 | tf_op jit(solution)/shard_map/stack | solution.py:224
  202.9 4.3 %all-to-all-start.2 = ((bf16[2,4,64,640]{3,2,0,1:T(8,128)(2,1)}), bf16[2,4,64,640]{3,2,0,1:T(8,128)(2,1)S(1)}, u32[]{:S(2)}, u32[]{:S(2)}) async-start(bf16[2,4,64,640]{3,2,0,1:T(8,128)(2,1)} %copy.147), calls=%async_computation.2 | async-start | bytes 1310720 | tf_op jit(solution)/shard_map/all_to_all | solution.py:225
  208.4 2.1 add_bitcast_fusion
  210.5 7.9 %all-to-all-done.2 = bf16[2,4,64,640]{3,2,0,1:T(8,128)(2,1)S(1)} async-done(((bf16[2,4,64,640]{3,2,0,1:T(8,128)(2,1)}), bf16[2,4,64,640]{3,2,0,1:T(8,128)(2,1)S(1)}, u32[]{:S(2)}, u32[]{:S(2)}) %all-to-all-start.2) | async-done | bytes 655392 | tf_op jit(solution)/shard_map/all_to_all | solution.py:225
  219.9 0.9 multiply_convert_fusion.5
  (88 shorter events, 6.9 us)
Async XLA Ops:
  9.4 4.8 %all-to-all-start.1 = ((bf16[2,32,896]{2,1,0:T(8,128)(2,1)}), bf16[2,32,896]{2,1,0:T(8,128)(2,1)S(1)}, u32[]{:S(2)}, u32[]{:S(2)}) async-start(bf16[2,32,896]{2,1,0:T(8,128)(2,1)} %pad_maximum_fusion.3), calls=%async_computation.1 | async-start | bytes 229376 | tf_op jit(solution)/shard_map/all_to_all | solution.py:60
  13.9 126.6 %copy-start.2 = (f32[4,2816]{1,0:T(4,128)S(1)}, f32[4,2816]{1,0:T(4,128)}, u32[]{:S(2)}) copy-start(f32[4,2816]{1,0:T(4,128)} %param.17) | copy-start | bytes 135172
  13.9 126.6 %slice-start = ((f32[4,2816]{1,0:T(4,128)}), f32[4,256]{1,0:T(4,128)S(1)}, s32[]{:S(2)}) async-start(f32[4,2816]{1,0:T(4,128)} %param.17), calls=%async_computation.4 | async-start | bytes 8192 | tf_op jit(solution)/shard_map/slice | solution.py:110
  16.4 22.7 %all-to-all-start = ((bf16[4,64,2560]{2,1,0:T(8,128)(2,1)}), bf16[4,64,2560]{2,1,0:T(8,128)(2,1)S(1)}, u32[]{:S(2)}, u32[]{:S(2)}) async-start(bf16[4,64,2560]{2,1,0:T(8,128)(2,1)} %broadcast_in_dim.39), calls=%async_computation | async-start | bytes 2621440 | tf_op jit(solution)/shard_map/all_to_all | solution.py:48
  20.8 116.2 %all-gather.2.cloned.1.call-start = ((), (), s32[]{:S(2)}) async-start(), calls=%async_computation.3 | async-start | bytes 7798784 | tf_op jit(solution)/shard_map/all_gather | solution.py:75
  137.0 27.7 %collective-permute-start.1 = (bf16[4096,896]{1,0:T(8,128)(2,1)}, bf16[4096,896]{1,0:T(8,128)(2,1)}, u32[]{:S(2)}, u32[]{:S(2)}) collective-permute-start(bf16[4096,896]{1,0:T(8,128)(2,1)} %all-gather.2.cloned.1.call-done), channel_id=1, source_target_pairs={{0,4},{4,0},{1,5},{5,1},{2,6},{6,2},{3,7},{7,3},{8,12},{12,8},{9,1... | collective-permute-start | bytes 22020104 | tf_op jit(solution)/shard_map/ppermute | solution.py:76
  141.8 10.4 %collective-permute-start = (bf16[3,2560]{1,0:T(4,128)(2,1)S(1)}, bf16[3,2560]{1,0:T(4,128)(2,1)S(1)}, u32[]{:S(2)}, u32[]{:S(2)}) collective-permute-start(bf16[3,2560]{1,0:T(4,128)(2,1)S(1)} %slice.136), channel_id=1, source_target_pairs={{0,4},{4,8},{8,12},{12,16},{16,20},{20,24},{24,28},{28,32},{32,36}... | collective-permute-start | bytes 46088 | tf_op jit(solution)/shard_map/ppermute | solution.py:16
  164.7 6.5 %copy-start.4 = (f32[10]{0:T(128)S(1)}, f32[10]{0:T(128)}, u32[]{:S(2)}) copy-start(f32[10]{0:T(128)} %param.19) | copy-start | bytes 124
  164.8 6.5 %copy-start.8 = (f32[10]{0:T(128)S(1)}, f32[10]{0:T(128)}, u32[]{:S(2)}) copy-start(f32[10]{0:T(128)} %param.20) | copy-start | bytes 124
  171.2 6.8 %copy-start = (f32[264,896]{0,1:T(8,128)}, f32[264,896]{0,1:T(8,128)S(1)}, u32[]{:S(2)}) copy-start(f32[264,896]{0,1:T(8,128)S(1)} %get-tuple-element.43) | copy-start | bytes 2838532
  174.0 14.2 %copy-start.6 = (f32[10]{0:T(128)}, f32[10]{0:T(128)S(1)}, u32[]{:S(2)}) copy-start(f32[10]{0:T(128)S(1)} %multiply_reduce_fusion.1) | copy-start | bytes 124
  174.1 14.5 %copy-start.1 = (f32[10,256]{1,0:T(8,128)S(1)}, f32[10,256]{1,0:T(8,128)}, u32[]{:S(2)}) copy-start(f32[10,256]{1,0:T(8,128)} %get-tuple-element.28) | copy-start | bytes 30724
  179.2 12.5 %collective-permute-start.3 = (bf16[10,72,128]{2,1,0:T(8,128)(2,1)}, bf16[10,72,128]{2,1,0:T(8,128)(2,1)}, u32[]{:S(2)}, u32[]{:S(2)}) collective-permute-start(bf16[10,72,128]{2,1,0:T(8,128)(2,1)} %pad_maximum_fusion.2), channel_id=1, source_target_pairs={{0,8},{4,12},{8,16},{12,20},{16,24},{20,28},{24,32},{28,36},{32,40... | collective-permute-start | bytes 552968 | tf_op jit(solution)/shard_map/ppermute | solution.py:16
  181.1 11.5 %collective-permute-start.2 = (bf16[10,72,128]{2,1,0:T(8,128)(2,1)}, bf16[10,72,128]{2,1,0:T(8,128)(2,1)}, u32[]{:S(2)}, u32[]{:S(2)}) collective-permute-start(bf16[10,72,128]{2,1,0:T(8,128)(2,1)} %pad_maximum_fusion.2), channel_id=1, source_target_pairs={{0,4},{4,8},{8,12},{12,16},{16,20},{20,24},{24,28},{28,32},{32,36}... | collective-permute-start | bytes 552968 | tf_op jit(solution)/shard_map/ppermute | solution.py:16
  183.8 14.0 %collective-permute-start.4 = (bf16[10,72,128]{2,1,0:T(8,128)(2,1)}, bf16[10,72,128]{2,1,0:T(8,128)(2,1)}, u32[]{:S(2)}, u32[]{:S(2)}) collective-permute-start(bf16[10,72,128]{2,1,0:T(8,128)(2,1)} %pad_maximum_fusion.2), channel_id=1, source_target_pairs={{0,12},{4,16},{8,20},{12,24},{16,28},{20,32},{24,36},{28,40},{32,4... | collective-permute-start | bytes 552968 | tf_op jit(solution)/shard_map/ppermute | solution.py:16
  188.5 1.0 copy-start.5
  188.6 9.1 %copy-start.9 = (f32[10]{0:T(128)S(1)}, f32[10]{0:T(128)}, u32[]{:S(2)}) copy-start(f32[10]{0:T(128)} %param.21) | copy-start | bytes 124
  199.4 9.0 %copy-start.7 = (f32[10]{0:T(128)S(1)}, f32[10]{0:T(128)}, u32[]{:S(2)}) copy-start(f32[10]{0:T(128)} %copy-done.6) | copy-start | bytes 124
  202.9 15.5 %all-to-all-start.2 = ((bf16[2,4,64,640]{3,2,0,1:T(8,128)(2,1)}), bf16[2,4,64,640]{3,2,0,1:T(8,128)(2,1)S(1)}, u32[]{:S(2)}, u32[]{:S(2)}) async-start(bf16[2,4,64,640]{3,2,0,1:T(8,128)(2,1)} %copy.147), calls=%async_computation.2 | async-start | bytes 1310720 | tf_op jit(solution)/shard_map/all_to_all | solution.py:225
  219.1 0.8 copy-start.3
Sparse Core Ops, SparseCore 0:
  39.2 97.7 all-gather.1
